TPU v7x, 128 devices: a whole 4x4x4 slice. The times are simulated.
128 devices in a mesh: req: 8 (over y, x_hi), row: 4 (over x_lo, core), col: 4 (over z).
Axes of the slice: x: 4 (x_hi: 2, x_lo: 2; x = x_hi * 2 + x_lo), y: 4, z: 4, core: 2. Of those that a mesh axis runs over, the one named last changes fastest.
Arguments:
- text_embed: bfloat16 [6144, 4096], P(('req', 'col'), 'row')
- vis_embed: bfloat16 [4096, 4096], P(('req', 'col'), 'row')
- vis_segment: int32 [4096], P(('req', 'col')), may hold values from 0 to 20, never falling along the last dimension, each value on 1 to 256 neighbouring positions
- vis_valid: int32 [4096], P(('req', 'col')), may hold values 0 or 1
- vis_gain: bfloat16 [4096], P('row'), may hold values from 0.25 to 1.75
- vis_wq: bfloat16 [4096, 4096], P('row', 'col')
- vis_wk: bfloat16 [4096, 4096], P('row', 'col')
- vis_wv: bfloat16 [4096, 4096], P('row', 'col'), may hold values from -0.09375 to 0.09375
- vis_wo: bfloat16 [4096, 4096], P('col', 'row'), may hold values from -0.09375 to 0.09375
- dec_gain: bfloat16 [4096], P('row'), may hold values from 0.25 to 1.75
- dec_wq: bfloat16 [4096, 4096], P('row', 'col')
- dec_wk: bfloat16 [4096, 4096], P('row', 'col')
- dec_wv: bfloat16 [4096, 4096], P('row', 'col'), may hold values from -0.09375 to 0.09375
- dec_wo: bfloat16 [4096, 4096], P('col', 'row'), may hold values from -0.09375 to 0.09375
Outputs:
- hidden_out: bfloat16 [6144, 4096], P(('req', 'col'), 'row')
Inputs may be any that keep to these rules, and one draw needn't show every extreme that they name: `vis_segment`: images take consecutive slots in order, each 1 to 256 slots, one exactly 256.
All inputs are finite; a program needn't handle non-finite values. No bound on the sum of `vis_valid` on one device may be relied on, other than what follows from the above.
Results may differ from a plain program's by a relative error of at most 0.008.
Values may be sent and summed in bfloat16 or wider, within the bound.
No kernel may reach another device: no remote copies, remote signals or barrier semaphores. Data moves between devices by JAX's collectives and lax.ppermute only.
A program may use at most 192 MiB of HBM per device.

v0:
```python
import jax
import jax.numpy as jnp
from jax import lax
from jax.sharding import PartitionSpec as P

D = 4096
HD = 128
MAXIMG = 256


def with_halo(cells, sides, width):
    for axis, dim in sides:
        count = lax.axis_size(axis)
        ends = count - 1
        head = lax.slice_in_dim(cells, 0, width, axis=dim)
        tail = lax.slice_in_dim(cells, cells.shape[dim] - width, cells.shape[dim], axis=dim)
        cells = jnp.concatenate(
            [
                lax.ppermute(tail, axis, [(i, (i + 1) % count) for i in range(ends)]),
                cells,
                lax.ppermute(head, axis, [((i + 1) % count, i) for i in range(ends)]),
            ],
            axis=dim,
        )
    return cells


def passed_along(shard, axis, by):
    size = lax.axis_size(axis)
    pairs = [(i, i + by) for i in range(size) if 0 <= i + by < size]
    return lax.ppermute(shard, axis, pairs)


def norm_local(values, gain):
    floats = values.astype(jnp.float32)
    squares = jnp.sum(floats * floats, axis=-1)
    totals = lax.psum(squares, "row")
    factor = lax.rsqrt(totals / D + 1e-05)
    return (floats * factor[:, None] * gain.astype(jnp.float32)[None, :]).astype(jnp.bfloat16)


def gather_cols(values):
    return lax.all_gather(values, "col", axis=0, tiled=True)


def out_project(attended, weight):
    whole = lax.all_gather(attended, "row", axis=0, tiled=True)
    return lax.psum_scatter(
        jnp.dot(whole, weight, preferred_element_type=jnp.float32).astype(jnp.bfloat16),
        "col",
        scatter_dimension=0,
        tiled=True,
    ).astype(jnp.float32)


def split_heads(values):
    return values.reshape(values.shape[0], values.shape[1] // HD, HD)


def attend_block(queries, keys, values, allowed):
    query_heads = split_heads(queries)
    scores = jnp.einsum(
        "qhd,khd->hqk", query_heads, split_heads(keys), preferred_element_type=jnp.float32
    ) * HD ** (-0.5)
    scores = jnp.where(allowed[None], scores, -1e30)
    peak = jnp.max(scores, axis=-1, keepdims=True)
    weights = jnp.where(allowed[None], jnp.exp(scores - peak), 0.0)
    mass = jnp.sum(weights, axis=-1)
    summed = jnp.einsum(
        "hqk,khd->qhd",
        weights.astype(jnp.bfloat16),
        split_heads(values),
        preferred_element_type=jnp.float32,
    )
    result = summed / jnp.transpose(mass)[:, :, None]
    return result.reshape(queries.shape[0], queries.shape[1]).astype(jnp.bfloat16)


def fold_step(carry, query_heads, query_slots, key_heads, value_heads):
    peak, mass, accum = carry
    piece_slots = jnp.arange(key_heads.shape[0], dtype=jnp.int32)
    allowed = query_slots[:, None] >= piece_slots[None, :]
    scores = jnp.einsum(
        "qhd,khd->hqk", query_heads, key_heads, preferred_element_type=jnp.float32
    ) * HD ** (-0.5)
    scores = jnp.where(allowed[None], scores, -1e30)
    new_peak = jnp.maximum(peak, jnp.max(scores, axis=-1))
    weights = jnp.where(allowed[None], jnp.exp(scores - new_peak[:, :, None]), 0.0)
    summed = jnp.einsum(
        "hqk,khd->hqd",
        weights.astype(jnp.bfloat16),
        value_heads,
        preferred_element_type=jnp.float32,
    )
    return (new_peak, jnp.sum(weights, axis=-1), summed)


def start_state(head_count, query_count):
    return (
        jnp.full((head_count, query_count), -1e30, jnp.float32),
        jnp.zeros((head_count, query_count), jnp.float32),
        jnp.zeros((head_count, query_count, HD), jnp.float32),
    )


def per_device(
    text_embed,
    vis_embed,
    vis_segment,
    vis_valid,
    vis_gain,
    vis_wq,
    vis_wk,
    vis_wv,
    vis_wo,
    dec_gain,
    dec_wq,
    dec_wk,
    dec_wv,
    dec_wo,
):
    row_count = lax.axis_size("row")
    col_count = lax.axis_size("col")
    width = vis_wq.shape[1]
    margin = MAXIMG - 1
    piece_ids = lax.all_gather(jnp.stack([vis_segment, vis_valid]), "col", axis=1, tiled=True)
    piece_len = piece_ids.shape[1]
    framed_ids = with_halo(piece_ids, (("req", 1),), margin)
    total_slots = piece_len * lax.axis_size("req")
    prompt_rows = text_embed.shape[0]
    prompt_total = prompt_rows * lax.axis_size("req") * col_count
    window_len = piece_len + 2 * margin
    window_start = lax.axis_index("req") * piece_len - margin
    window_index = jnp.arange(window_len, dtype=jnp.int32)
    key_slots = window_start + window_index
    inside = (key_slots >= 0) & (key_slots < total_slots)
    key_segment = framed_ids[0]
    key_valid = framed_ids[1]
    begins = jnp.concatenate([jnp.ones((1,), jnp.bool_), key_segment[1:] != key_segment[:-1]])
    begins = begins | (key_slots == 0)
    image_first = lax.cummax(jnp.where(begins, key_slots, window_start), axis=0)
    target_window = image_first * prompt_total // total_slots + key_slots - image_first
    vis_cols = gather_cols(norm_local(vis_embed, vis_gain))
    vis_stack = jnp.concatenate([vis_wq, vis_wk, vis_wv], axis=1)
    vis_rows = vis_cols.shape[0] // row_count
    vis_proj = lax.psum_scatter(
        jnp.dot(vis_cols, vis_stack, preferred_element_type=jnp.float32).astype(jnp.bfloat16),
        "row",
        scatter_dimension=0,
        tiled=True,
    )
    vis_pairs = jnp.stack([vis_proj[:, width : 2 * width], vis_proj[:, 2 * width :]])
    piece_keys = lax.all_gather(vis_pairs, "row", axis=1, tiled=True)
    framed = with_halo(piece_keys, (("req", 1),), margin)
    query_local = margin + lax.axis_index("row") * vis_rows + jnp.arange(vis_rows, dtype=jnp.int32)
    query_slots = window_start + query_local
    query_segment = key_segment[query_local]
    seen = (
        inside[None, :]
        & (query_segment[:, None] == key_segment[None, :])
        & ((key_valid[None, :] == 1) | (query_slots[:, None] == key_slots[None, :]))
    )
    vis_att = attend_block(vis_proj[:, :width], framed[0], framed[1], seen)
    vis_out = (vis_embed.astype(jnp.float32) + out_project(vis_att, vis_wo)).astype(jnp.bfloat16)
    device_place = lax.axis_index("req") * col_count + lax.axis_index("col")
    owned = device_place * prompt_rows + jnp.arange(prompt_rows, dtype=jnp.int32)
    slot_rows = vis_out.shape[0]
    following = passed_along(vis_out, ("req", "col"), -1)
    near_rows = jnp.concatenate([vis_out, following], axis=0)
    near_local = (
        margin + lax.axis_index("col") * slot_rows + jnp.arange(2 * slot_rows, dtype=jnp.int32)
    )
    near_slots = window_start + near_local
    present = near_slots < total_slots
    near_target = jnp.where(present, target_window[near_local], -1)
    near_valid = key_valid[near_local]
    onehot = ((owned[:, None] == near_target[None, :]) & (near_valid[None, :] == 1)).astype(
        jnp.bfloat16
    )
    carried = jnp.dot(onehot, near_rows, preferred_element_type=jnp.float32)
    mixed = (text_embed.astype(jnp.float32) + carried).astype(jnp.bfloat16)
    dec_cols = gather_cols(norm_local(mixed, dec_gain))
    dec_stack = jnp.concatenate([dec_wq, dec_wk, dec_wv], axis=1)
    dec_rows = dec_cols.shape[0] // row_count
    dec_proj = lax.psum_scatter(
        jnp.dot(dec_cols, dec_stack, preferred_element_type=jnp.float32),
        "row",
        scatter_dimension=0,
        tiled=True,
    ).astype(jnp.bfloat16)
    local_heads = width // HD
    dec_pairs = jnp.stack([dec_proj[:, width : 2 * width], dec_proj[:, 2 * width :]])
    query_heads = split_heads(dec_proj[:, :width])
    token_slots = (
        lax.axis_index("req") * row_count + lax.axis_index("row")
    ) * dec_rows + jnp.arange(dec_rows, dtype=jnp.int32)
    piece = lax.all_gather(dec_pairs, ("req", "row"), axis=1, tiled=True)
    final_peak, final_mass, final_accum = fold_step(
        start_state(local_heads, dec_rows),
        query_heads,
        token_slots,
        split_heads(piece[0]),
        split_heads(piece[1]),
    )
    dec_att = (
        jnp.transpose(final_accum / final_mass[:, :, None], (1, 0, 2))
        .reshape(dec_rows, width)
        .astype(jnp.bfloat16)
    )
    return (mixed.astype(jnp.float32) + out_project(dec_att, dec_wo)).astype(jnp.bfloat16)


def solution(mesh):
    return jax.shard_map(
        per_device,
        mesh=mesh,
        in_specs=(
            P(("req", "col"), "row"),
            P(("req", "col"), "row"),
            P(("req", "col")),
            P(("req", "col")),
            P("row"),
            P("row", "col"),
            P("row", "col"),
            P("row", "col"),
            P("col", "row"),
            P("row"),
            P("row", "col"),
            P("row", "col"),
            P("row", "col"),
            P("col", "row"),
        ),
        out_specs=P(("req", "col"), "row"),
        check_vma=False,
    )
```

profile of v0, /device:TPU:28, one launch (start us, length us, event | category | flops | bytes accessed | tf_op | source)
XLA Modules:
  0.0 640.8 jit_solution(467458760197187966)
XLA Ops:
  7.8 6.6 %psum.14 = f32[128]{0:T(128)S(1)} all-reduce(f32[128]{0:T(128)S(1)} %fusion.64), channel_id=1, replica_groups=mesh['req'=8,'row'=4,'col'=4] {'row'}, use_global_device_ids=true, to_apply=%region_3.4 | all-reduce | flops 128 | bytes 1024 | tf_op jit(solution)/shard_map/psum | solution.py:37
  16.9 26.4 %all-gather.7.cloned.1.call-done = bf16[512,1024]{1,0:T(8,128)(2,1)} async-done(((bf16[128,1024]{1,0:T(8,128)(2,1)}), bf16[512,1024]{1,0:T(8,128)(2,1)}) %all-gather.7.cloned.1.call-update) | async-done | bytes 1048592 | tf_op jit(solution)/shard_map/all_gather | solution.py:43
  43.3 8.2 %fusion.22 = bf16[512,3072]{1,0:T(8,128)(2,1)} fusion(bf16[512,1024]{1,0:T(8,128)(2,1)} %all-gather.7.cloned.1.call-done, bf16[1024,1024]{1,0:T(8,128)(2,1)} %param.21, bf16[1024,1024]{1,0:T(8,128)(2,1)} %param.20, bf16[1024,1024]{1,0:T(8,128)(2,1)} %param.19), kind=kOutput, calls=%fused_computation.29 | convolution fusion | flops 3241672704 | bytes 10485760 | tf_op jit(solution)/shard_map/dot_general | solution.py:147
  51.6 37.0 %reduce-scatter.5.cloned.1.call-done = bf16[128,3072]{1,0:T(8,128)(2,1)} async-done(((bf16[512,3072]{1,0:T(8,128)(2,1)}), bf16[128,3072]{1,0:T(8,128)(2,1)}) %reduce-scatter.5.cloned.1.call-update) | async-done | bytes 786448 | tf_op jit(solution)/shard_map/reduce_scatter | solution.py:146
  90.7 9.9 %all_gather.21 = s32[2,512]{1,0:T(2,128)S(1)} all-gather(s32[2,128]{1,0:T(2,128)S(1)} %pad_add_fusion.1), channel_id=1, replica_groups=mesh['req'=8,'row'=4,'col'=4] {'col'}, dimensions={1}, use_global_device_ids=true | all-gather | bytes 5120 | tf_op jit(solution)/shard_map/all_gather | solution.py:126
  102.0 6.1 collective-permute-start.1
  108.6 12.1 %all-gather.9.cloned.1.call-done = bf16[2,512,1024]{2,1,0:T(8,128)(2,1)} async-done(((bf16[2,128,1024]{2,1,0:T(8,128)(2,1)}), bf16[2,512,1024]{2,1,0:T(8,128)(2,1)}) %all-gather.9.cloned.1.call-update) | async-done | bytes 2097168 | tf_op jit(solution)/shard_map/all_gather | solution.py:153
  134.2 17.5 %collective-permute-done.3 = bf16[2,255,1024]{2,0,1:T(2,128)(2,1)} collective-permute-done((bf16[2,255,1024]{2,0,1:T(2,128)(2,1)}, bf16[2,255,1024]{2,0,1:T(2,128)(2,1)}, u32[]{:S(2)}, u32[]{:S(2)}) %collective-permute-start.3) | collective-permute-done | bytes 1044512 | tf_op jit(solution)/shard_map/ppermute | solution.py:21
  153.3 24.3 %collective-permute-done.2 = bf16[2,255,1024]{2,0,1:T(2,128)(2,1)} collective-permute-done((bf16[2,255,1024]{2,0,1:T(2,128)(2,1)S(1)}, bf16[2,255,1024]{2,0,1:T(2,128)(2,1)}, u32[]{:S(2)}, u32[]{:S(2)}) %collective-permute-start.2) | collective-permute-done | bytes 1044512 | tf_op jit(solution)/shard_map/ppermute | solution.py:19
  194.2 22.0 %all-gather.11.cloned.1.call-done = bf16[512,1024]{0,1:T(8,128)(2,1)} async-done(((bf16[128,1024]{0,1:T(8,128)(2,1)}), bf16[512,1024]{0,1:T(8,128)(2,1)}) %all-gather.11.cloned.1.call-update) | async-done | bytes 1048592 | tf_op jit(solution)/shard_map/all_gather | solution.py:47
  222.6 22.8 %reduce-scatter.7.cloned.1.call-done = bf16[128,1024]{1,0:T(8,128)(2,1)} async-done(((bf16[512,1024]{1,0:T(8,128)(2,1)}), bf16[128,1024]{1,0:T(8,128)(2,1)}) %reduce-scatter.7.cloned.1.call-update) | async-done | bytes 262160 | tf_op jit(solution)/shard_map/reduce_scatter | solution.py:48
  256.5 5.7 psum.15
  263.2 30.4 %all-gather.13.cloned.1.call-done = bf16[768,1024]{1,0:T(8,128)(2,1)} async-done(((bf16[192,1024]{1,0:T(8,128)(2,1)}), bf16[768,1024]{1,0:T(8,128)(2,1)}) %all-gather.13.cloned.1.call-update) | async-done | bytes 1572880 | tf_op jit(solution)/shard_map/all_gather | solution.py:43
  293.6 12.0 %fusion.16 = f32[768,3072]{1,0:T(8,128)} fusion(bf16[768,1024]{1,0:T(8,128)(2,1)} %all-gather.13.cloned.1.call-done, bf16[1024,1024]{1,0:T(8,128)(2,1)} %param.26, bf16[1024,1024]{1,0:T(8,128)(2,1)} %param.25, bf16[1024,1024]{1,0:T(8,128)(2,1)} %param.24), kind=kOutput, calls=%fused_computation.22 | convolution fusion | flops 4850712576 | bytes 17301504 | tf_op jit(solution)/shard_map/dot_general | solution.py:186
  305.6 87.2 %reduce-scatter.9.cloned.1.call-done = f32[192,3072]{1,0:T(8,128)} async-done(((f32[768,3072]{1,0:T(8,128)}), f32[192,3072]{1,0:T(8,128)}) %reduce-scatter.9.cloned.1.call-update) | async-done | bytes 2359312 | tf_op jit(solution)/shard_map/reduce_scatter | solution.py:185
  397.4 90.6 %all-gather.15.cloned.1.call-done = bf16[2,6144,1024]{2,1,0:T(8,128)(2,1)} async-done(((bf16[2,192,1024]{2,1,0:T(8,128)(2,1)}), bf16[2,6144,1024]{2,1,0:T(8,128)(2,1)}) %all-gather.15.cloned.1.call-update) | async-done | bytes 25165840 | tf_op jit(solution)/shard_map/all_gather | solution.py:197
  488.0 11.3 %slice_bitcast_fusion.1 = (bf16[768,8,8,128]{3,1,2,0:T(8,128)(2,1)S(1)}, bf16[768,8,8,128]{3,1,2,0:T(8,128)(2,1)S(1)}) fusion(bf16[2,6144,1024]{2,1,0:T(8,128)(2,1)} %all-gather.15.cloned.1.call-done), kind=kLoop, calls=%fused_computation.12 | loop fusion | bytes 50331648
  499.3 7.0 %copy.44 = bf16[768,8,8,128]{3,2,1,0:T(8,128)(2,1)} copy(bf16[768,8,8,128]{3,1,2,0:T(8,128)(2,1)S(1)} %get-tuple-element.5) | data formatting | bytes 25165824
  506.3 7.0 %copy.45 = bf16[768,8,8,128]{3,2,1,0:T(8,128)(2,1)} copy(bf16[768,8,8,128]{3,1,2,0:T(8,128)(2,1)S(1)} %get-tuple-element.6) | data formatting | bytes 25165824
  513.3 19.5 %fusion.1 = (f32[8,192]{1,0:T(8,128)S(1)}, f32[8,192,6144]{2,1,0:T(8,128)}) fusion(pred[192,6144]{1,0:T(8,128)(4,1)S(1)} %iota_compare_fusion, bf16[6144,8,128]{2,1,0:T(8,128)(2,1)} %bitcast.78, bf16[24,8,8,128]{3,2,1,0:T(8,128)(2,1)S(1)} %copy-done.6), kind=kOutput, calls=%fused_computation.6 | convolution fusion | flops 2444229120 | bytes 51910656 | tf_op jit(solution)/shard_map/qhd,khd->hqk/dot_general | solution.py:83
  532.8 18.6 %fusion.2 = f32[8,192]{1,0:T(8,128)S(1)} fusion(f32[8,192,6144]{2,1,0:T(8,128)} %get-tuple-element.26, f32[8,192]{1,0:T(8,128)S(1)} %broadcast_maximum_fusion, pred[192,6144]{1,0:T(8,128)(4,1)S(1)} %iota_compare_fusion), kind=kLoop, calls=%fused_computation.7 | loop fusion | flops 47184384 | bytes 38940672 | tf_op jit(solution)/shard_map/reduce_sum | solution.py:95
  551.4 21.2 %fusion.59 = bf16[8,24,8,128]{3,2,1,0:T(8,128)(2,1)} fusion(bf16[6144,8,128]{2,1,0:T(8,128)(2,1)} %bitcast.77, f32[8,192,6144]{2,1,0:T(8,128)} %get-tuple-element.26, f32[8,192]{1,0:T(8,128)S(1)} %broadcast_maximum_fusion, pred[192,6144]{1,0:T(8,128)(4,1)S(1)} %iota_compare_fusion, f32[192,8]{0,1:T(8,128)S(1)} %bitcast.84), kind=kOutput, calls=%fused_computation.52 | convolution fusion | flops 2463498240 | bytes 51916800 | tf_op jit(solution)/shard_map/hqk,khd->hqd/dot_general | solution.py:89
  574.6 25.9 %all-gather.17.cloned.1.call-done = bf16[768,1024]{1,0:T(8,128)(2,1)} async-done(((bf16[192,1024]{1,0:T(8,128)(2,1)}), bf16[768,1024]{1,0:T(8,128)(2,1)}) %all-gather.17.cloned.1.call-update) | async-done | bytes 1572880 | tf_op jit(solution)/shard_map/all_gather | solution.py:47
  604.9 27.3 %reduce-scatter.11.cloned.1.call-done = bf16[192,1024]{1,0:T(8,128)(2,1)} async-done(((bf16[768,1024]{1,0:T(8,128)(2,1)}), bf16[192,1024]{1,0:T(8,128)(2,1)}) %reduce-scatter.11.cloned.1.call-update) | async-done | bytes 393232 | tf_op jit(solution)/shard_map/reduce_scatter | solution.py:48
  (109 shorter events, 70.4 us)
Async XLA Ops:
  6.5 593.9 %copy-start = (bf16[1024,1024]{1,0:T(8,128)(2,1)S(1)}, bf16[1024,1024]{1,0:T(8,128)(2,1)}, u32[]{:S(2)}) copy-start(bf16[1024,1024]{1,0:T(8,128)(2,1)} %param.27) | copy-start | bytes 6291460
  6.5 36.7 %all-gather.7.cloned.1.call-start = ((), (), s32[]{:S(2)}) async-start(), calls=%async_computation.4 | async-start | bytes 1310720 | tf_op jit(solution)/shard_map/all_gather | solution.py:43
  16.9 71.7 %reduce-scatter.5.cloned.1.call-start = ((), (), s32[]{:S(2)}) async-start(), calls=%async_computation.5 | async-start | bytes 3932160 | tf_op jit(solution)/shard_map/reduce_scatter | solution.py:146
  51.5 39.1 %copy-start.8 = (s32[128]{0:T(128)S(1)}, s32[128]{0:T(128)}, u32[]{:S(2)}) copy-start(s32[128]{0:T(128)} %param.17) | copy-start | bytes 1540
  51.5 39.1 %copy-start.9 = (s32[128]{0:T(128)S(1)}, s32[128]{0:T(128)}, u32[]{:S(2)}) copy-start(s32[128]{0:T(128)} %param.16) | copy-start | bytes 1540
  51.6 69.1 %all-gather.9.cloned.1.call-start = ((), (), s32[]{:S(2)}) async-start(), calls=%async_computation.6 | async-start | bytes 2621440 | tf_op jit(solution)/shard_map/all_gather | solution.py:153
  90.6 125.6 %all-gather.11.cloned.1.call-start = ((), (), s32[]{:S(2)}) async-start(), calls=%async_computation.7 | async-start | bytes 1310720 | tf_op jit(solution)/shard_map/all_gather | solution.py:47
  100.7 30.9 %collective-permute-start = (s32[2,255]{1,0:T(2,128)S(1)}, s32[2,255]{1,0:T(2,128)S(1)}, u32[]{:S(2)}, u32[]{:S(2)}) collective-permute-start(s32[2,255]{1,0:T(2,128)S(1)} %get-tuple-element.19), channel_id=1, source_target_pairs={{0,16},{16,32},{32,48},{48,64},{64,80},{80,96},{96,112},{1,17},{17... | collective-permute-start | bytes 6128 | tf_op jit(solution)/shard_map/ppermute | solution.py:19
  102.0 29.6 %collective-permute-start.1 = (s32[2,255]{1,0:T(2,128)S(1)}, s32[2,255]{1,0:T(2,128)S(1)}, u32[]{:S(2)}, u32[]{:S(2)}) collective-permute-start(s32[2,255]{1,0:T(2,128)S(1)} %get-tuple-element.20), channel_id=1, source_target_pairs={{16,0},{32,16},{48,32},{64,48},{80,64},{96,80},{112,96},{17,1},{33... | collective-permute-start | bytes 6128 | tf_op jit(solution)/shard_map/ppermute | solution.py:21
  125.8 26.0 %collective-permute-start.3 = (bf16[2,255,1024]{2,0,1:T(2,128)(2,1)}, bf16[2,255,1024]{2,0,1:T(2,128)(2,1)}, u32[]{:S(2)}, u32[]{:S(2)}) collective-permute-start(bf16[2,255,1024]{2,0,1:T(2,128)(2,1)} %copy.29), channel_id=1, source_target_pairs={{16,0},{32,16},{48,32},{64,48},{80,64},{96,80},{112,96},{17,1},{33... | collective-permute-start | bytes 3133448 | tf_op jit(solution)/shard_map/ppermute | solution.py:21
  129.6 48.0 %collective-permute-start.2 = (bf16[2,255,1024]{2,0,1:T(2,128)(2,1)S(1)}, bf16[2,255,1024]{2,0,1:T(2,128)(2,1)}, u32[]{:S(2)}, u32[]{:S(2)}) collective-permute-start(bf16[2,255,1024]{2,0,1:T(2,128)(2,1)S(1)} %copy.28), channel_id=1, source_target_pairs={{0,16},{16,32},{32,48},{48,64},{64,80},{80,96},{96,112},{1,17},{17... | collective-permute-start | bytes 3133448 | tf_op jit(solution)/shard_map/ppermute | solution.py:19
  133.2 45.9 %copy-start.1 = (bf16[2,512,1024]{2,1,0:T(8,128)(2,1)S(1)}, bf16[2,512,1024]{2,1,0:T(8,128)(2,1)}, u32[]{:S(2)}) copy-start(bf16[2,512,1024]{2,1,0:T(8,128)(2,1)} %all-gather.9.cloned.1.call-done) | copy-start | bytes 6291460
  192.7 27.7 %copy-start.7 = (bf16[1024]{0:T(1024)(128)(2,1)S(1)}, bf16[1024]{0:T(1024)(128)(2,1)}, u32[]{:S(2)}) copy-start(bf16[1024]{0:T(1024)(128)(2,1)} %param.23) | copy-start | bytes 6148
  194.2 51.3 %copy-start.4 = (bf16[128,1024]{1,0:T(8,128)(2,1)S(1)}, bf16[128,1024]{1,0:T(8,128)(2,1)}, u32[]{:S(2)}) copy-start(bf16[128,1024]{1,0:T(8,128)(2,1)} %param.15) | copy-start | bytes 786436
  194.2 51.3 %reduce-scatter.7.cloned.1.call-start = ((), (), s32[]{:S(2)}) async-start(), calls=%async_computation.8 | async-start | bytes 1310720 | tf_op jit(solution)/shard_map/reduce_scatter | solution.py:48
  220.4 73.2 %all-gather.13.cloned.1.call-start = ((), (), s32[]{:S(2)}) async-start(), calls=%async_computation.9 | async-start | bytes 1966080 | tf_op jit(solution)/shard_map/all_gather | solution.py:43
  246.5 8.6 %collective-permute-start.4 = (bf16[128,1024]{1,0:T(8,128)(2,1)S(1)}, bf16[128,1024]{1,0:T(8,128)(2,1)S(1)}, u32[]{:S(2)}, u32[]{:S(2)}) collective-permute-start(bf16[128,1024]{1,0:T(8,128)(2,1)S(1)} %fusion.67), channel_id=1, source_target_pairs={{1,0},{2,1},{3,2},{16,3},{17,16},{18,17},{19,18},{32,19},{33,32},{... | collective-permute-start | bytes 786440 | tf_op jit(solution)/shard_map/ppermute | solution.py:31
  256.5 49.0 %copy-start.2 = (f32[192,1024]{1,0:T(8,128)}, f32[192,1024]{1,0:T(8,128)S(1)}, u32[]{:S(2)}) copy-start(f32[192,1024]{1,0:T(8,128)S(1)} %get-tuple-element.24) | copy-start | bytes 2359300
  263.1 129.8 %reduce-scatter.9.cloned.1.call-start = ((), (), s32[]{:S(2)}) async-start(), calls=%async_computation.10 | async-start | bytes 11796480 | tf_op jit(solution)/shard_map/reduce_scatter | solution.py:185
  305.6 182.4 %all-gather.15.cloned.1.call-start = ((), (), s32[]{:S(2)}) async-start(), calls=%async_computation.11 | async-start | bytes 25952256 | tf_op jit(solution)/shard_map/all_gather | solution.py:197
  396.6 203.9 %all-gather.17.cloned.1.call-start = ((), (), s32[]{:S(2)}) async-start(), calls=%async_computation.12 | async-start | bytes 1966080 | tf_op jit(solution)/shard_map/all_gather | solution.py:47
  506.3 7.0 %copy-start.6 = (bf16[24,8,8,128]{3,2,1,0:T(8,128)(2,1)S(1)}, bf16[24,8,8,128]{3,2,1,0:T(8,128)(2,1)}, u32[]{:S(2)}) copy-start(bf16[24,8,8,128]{3,2,1,0:T(8,128)(2,1)} %get-tuple-element.11) | copy-start | bytes 1179652
  574.5 57.6 %copy-start.3 = (f32[192,1024]{1,0:T(8,128)S(1)}, f32[192,1024]{1,0:T(8,128)}, u32[]{:S(2)}) copy-start(f32[192,1024]{1,0:T(8,128)} %copy-done.2) | copy-start | bytes 2359300
  574.5 57.6 %reduce-scatter.11.cloned.1.call-start = ((), (), s32[]{:S(2)}) async-start(), calls=%async_computation.13 | async-start | bytes 1966080 | tf_op jit(solution)/shard_map/reduce_scatter | solution.py:48
  (1 other events, 2.3 us)
Sparse Core Ops, SparseCore 0:
  17.0 26.2 all-gather.6
  51.7 36.8 reduce-scatter.4
  90.7 29.9 all-gather.8
  194.3 21.8 all-gather.10
  220.5 24.9 reduce-scatter.6
  263.2 30.2 all-gather.12
  305.7 87.1 reduce-scatter.8
  396.7 91.2 all-gather.14
  574.6 25.7 all-gather.16
  605.0 27.1 reduce-scatter.10
where the time goes:
time: 642 us; the launch traced here: 641 us
  waiting for transfers between devices  428 us (67%)
  matrix products  74.6 us (12%)
  local copies, waits for them, and re-layouts  49.5 us (8%)
  other arithmetic  36.9 us (6%)
  blocking collectives  22.2 us (3%)
  starting transfers between devices  15.4 us (2%)
  between operations  13.9 us (2%)
    all_gather x1, waiting for transfers between devices, per_device(): piece = lax.all_gather(dec_pairs, ('req', 'row'), axis=1, tiled=True)  90.6 us
    reduce_scatter x1, waiting for transfers between devices, per_device(): lax.psum_scatter(jnp.dot(dec_cols, dec_stack, preferred_element_type=jnp....  87.2 us
    all_gather x2, waiting for transfers between devices, gather_cols(): return lax.all_gather(values, 'col', axis=0, tiled=True)  56.8 us
    reduce_scatter x2, waiting for transfers between devices, out_project(): lax.psum_scatter(jnp.dot(whole, weight, preferred_element_type=jnp.float3...  50.1 us
    all_gather x2, waiting for transfers between devices, out_project(): whole = lax.all_gather(attended, 'row', axis=0, tiled=True)  47.9 us
    reduce_scatter x1, waiting for transfers between devices, per_device(): lax.psum_scatter(jnp.dot(vis_cols, vis_stack, preferred_element_type=jnp....  37 us
    unnamed x26, local copies, waits for them, and re-layouts  27.9 us
    ppermute x2, waiting for transfers between devices, with_halo(): lax.ppermute(tail, axis, [(i, (i + 1) % count) for i in range(ends)])  24.3 us
  transfers between devices with their start and end apart: 15, of which 13 were waited for; matrix products, arithmetic and copies ran while one was open for 2% of the time, Pallas kernels for 0%

commit v1 on v0

--- a/solution.py
+++ b/solution.py
@@ -101,6 +101,31 @@
         jnp.zeros((head_count, query_count), jnp.float32),
         jnp.zeros((head_count, query_count, HD), jnp.float32),
     )
+
+
+def head_project(values, weights):
+    count = values.shape[0]
+    row_count = lax.axis_size("row")
+    width = weights[0].shape[1]
+    parts = [
+        jnp.dot(values, w, preferred_element_type=jnp.float32)
+        .astype(jnp.bfloat16)
+        .reshape(count, row_count, width // row_count)
+        for w in weights
+    ]
+    stacked = jnp.stack(parts, axis=2).transpose(1, 0, 2, 3)
+    stacked = stacked.reshape(row_count * count, len(weights) * (width // row_count))
+    return lax.psum_scatter(stacked, "row", scatter_dimension=0, tiled=True)
+
+
+def out_project_heads(attended, weight):
+    row_count = lax.axis_size("row")
+    whole = lax.all_gather(attended, "row", axis=0, tiled=False)
+    shaped = weight.reshape(row_count, weight.shape[0] // row_count, weight.shape[1])
+    summed = jnp.einsum("rtf,rfo->to", whole, shaped, preferred_element_type=jnp.float32)
+    return lax.psum_scatter(
+        summed.astype(jnp.bfloat16), "col", scatter_dimension=0, tiled=True
+    ).astype(jnp.float32)
 
 
 def per_device(
@@ -122,6 +147,7 @@
     row_count = lax.axis_size("row")
     col_count = lax.axis_size("col")
     width = vis_wq.shape[1]
+    local = width // row_count
     margin = MAXIMG - 1
     piece_ids = lax.all_gather(jnp.stack([vis_segment, vis_valid]), "col", axis=1, tiled=True)
     piece_len = piece_ids.shape[1]
@@ -141,18 +167,10 @@
     image_first = lax.cummax(jnp.where(begins, key_slots, window_start), axis=0)
     target_window = image_first * prompt_total // total_slots + key_slots - image_first
     vis_cols = gather_cols(norm_local(vis_embed, vis_gain))
-    vis_stack = jnp.concatenate([vis_wq, vis_wk, vis_wv], axis=1)
-    vis_rows = vis_cols.shape[0] // row_count
-    vis_proj = lax.psum_scatter(
-        jnp.dot(vis_cols, vis_stack, preferred_element_type=jnp.float32).astype(jnp.bfloat16),
-        "row",
-        scatter_dimension=0,
-        tiled=True,
-    )
-    vis_pairs = jnp.stack([vis_proj[:, width : 2 * width], vis_proj[:, 2 * width :]])
-    piece_keys = lax.all_gather(vis_pairs, "row", axis=1, tiled=True)
-    framed = with_halo(piece_keys, (("req", 1),), margin)
-    query_local = margin + lax.axis_index("row") * vis_rows + jnp.arange(vis_rows, dtype=jnp.int32)
+    vis_proj = head_project(vis_cols, (vis_wq, vis_wk, vis_wv))
+    vis_pairs = jnp.stack([vis_proj[:, local : 2 * local], vis_proj[:, 2 * local :]])
+    framed = with_halo(vis_pairs, (("req", 1),), margin)
+    query_local = margin + jnp.arange(piece_len, dtype=jnp.int32)
     query_slots = window_start + query_local
     query_segment = key_segment[query_local]
     seen = (
@@ -160,8 +178,10 @@
         & (query_segment[:, None] == key_segment[None, :])
         & ((key_valid[None, :] == 1) | (query_slots[:, None] == key_slots[None, :]))
     )
-    vis_att = attend_block(vis_proj[:, :width], framed[0], framed[1], seen)
-    vis_out = (vis_embed.astype(jnp.float32) + out_project(vis_att, vis_wo)).astype(jnp.bfloat16)
+    vis_att = attend_block(vis_proj[:, :local], framed[0], framed[1], seen)
+    vis_out = (vis_embed.astype(jnp.float32) + out_project_heads(vis_att, vis_wo)).astype(
+        jnp.bfloat16
+    )
     device_place = lax.axis_index("req") * col_count + lax.axis_index("col")
     owned = device_place * prompt_rows + jnp.arange(prompt_rows, dtype=jnp.int32)
     slot_rows = vis_out.shape[0]
@@ -180,34 +200,15 @@
     carried = jnp.dot(onehot, near_rows, preferred_element_type=jnp.float32)
     mixed = (text_embed.astype(jnp.float32) + carried).astype(jnp.bfloat16)
     dec_cols = gather_cols(norm_local(mixed, dec_gain))
-    dec_stack = jnp.concatenate([dec_wq, dec_wk, dec_wv], axis=1)
-    dec_rows = dec_cols.shape[0] // row_count
-    dec_proj = lax.psum_scatter(
-        jnp.dot(dec_cols, dec_stack, preferred_element_type=jnp.float32),
-        "row",
-        scatter_dimension=0,
-        tiled=True,
-    ).astype(jnp.bfloat16)
-    local_heads = width // HD
-    dec_pairs = jnp.stack([dec_proj[:, width : 2 * width], dec_proj[:, 2 * width :]])
-    query_heads = split_heads(dec_proj[:, :width])
-    token_slots = (
-        lax.axis_index("req") * row_count + lax.axis_index("row")
-    ) * dec_rows + jnp.arange(dec_rows, dtype=jnp.int32)
-    piece = lax.all_gather(dec_pairs, ("req", "row"), axis=1, tiled=True)
-    final_peak, final_mass, final_accum = fold_step(
-        start_state(local_heads, dec_rows),
-        query_heads,
-        token_slots,
-        split_heads(piece[0]),
-        split_heads(piece[1]),
-    )
-    dec_att = (
-        jnp.transpose(final_accum / final_mass[:, :, None], (1, 0, 2))
-        .reshape(dec_rows, width)
-        .astype(jnp.bfloat16)
-    )
-    return (mixed.astype(jnp.float32) + out_project(dec_att, dec_wo)).astype(jnp.bfloat16)
+    dec_proj = head_project(dec_cols, (dec_wq, dec_wk, dec_wv))
+    dec_rows = dec_cols.shape[0]
+    dec_pairs = jnp.stack([dec_proj[:, local : 2 * local], dec_proj[:, 2 * local :]])
+    piece = lax.all_gather(dec_pairs, "req", axis=1, tiled=True)
+    token_slots = lax.axis_index("req") * dec_rows + jnp.arange(dec_rows, dtype=jnp.int32)
+    all_slots = jnp.arange(piece.shape[1], dtype=jnp.int32)
+    causal = token_slots[:, None] >= all_slots[None, :]
+    dec_att = attend_block(dec_proj[:, :local], piece[0], piece[1], causal)
+    return (mixed.astype(jnp.float32) + out_project_heads(dec_att, dec_wo)).astype(jnp.bfloat16)
 
 
 def solution(mesh):

time: 642 us -> 571 us (0.89)
  waiting for transfers between devices: 428 us -> 316 us
  other arithmetic: 36.9 us -> 64.9 us
  local copies, waits for them, and re-layouts: 49.5 us -> 59.1 us
    reduce_scatter x4, waiting for transfers between devices: 174 us -> 119 us  [the longest x2 68.4 us: head_project(): return lax.psum_scatter(stacked, 'row', scatter_dimension=0, tiled=True)]
    sub x1, other arithmetic: 2.26 us -> 36.8 us  [attend_block(): weights = jnp.where(allowed[None], jnp.exp(scores - peak), 0.0)]
    dot_general x6 -> x8, matrix products: 69.4 us -> 36.1 us  [the longest x6 27.6 us: head_project(): jnp.dot(values, w, preferred_element_type=jnp.float32).astype(jnp.bfloat16)]
    another operation x3 -> x13, local copies, waits for them, and re-layouts: 5.51 us -> 37 us  [the longest x12 36.9 us: head_project(): stacked = jnp.stack(parts, axis=2).transpose(1, 0, 2, 3)]
    ppermute x2, waiting for transfers between devices: 24.3 us -> 1.64 us  [with_halo(): lax.ppermute(tail, axis, [(i, (i + 1) % count) for i in range(ends)])]
    unnamed x26 -> x16, local copies, waits for them, and re-layouts: 27.9 us -> 6.46 us
    reduce_sum x1 -> x0, other arithmetic: 18.6 us -> none  [fold_step(): return (new_peak, jnp.sum(weights, axis=-1), summed)]
    all_gather x4 -> x3, waiting for transfers between devices: 151 us -> 133 us  [the longest x1 79.6 us: per_device(): piece = lax.all_gather(dec_pairs, 'req', axis=1, tiled=True)]
  transfers between devices with their start and end apart: 15 -> 14, of which waited for: 13 -> 13; matrix products, arithmetic and copies ran while one was open for 2% -> 2% of each run, Pallas kernels for 0% -> 0%
where the time goes in v1:
time: 571 us; the launch traced here: 563 us
  waiting for transfers between devices  316 us (55%)
  matrix products  69.7 us (12%)
  other arithmetic  64.9 us (11%)
  local copies, waits for them, and re-layouts  59.1 us (10%)
  blocking collectives  20.8 us (4%)
  starting transfers between devices  18.7 us (3%)
  between operations  14 us (2%)
    all_gather x1, waiting for transfers between devices, per_device(): piece = lax.all_gather(dec_pairs, 'req', axis=1, tiled=True)  79.6 us
    reduce_scatter x2, waiting for transfers between devices, head_project(): return lax.psum_scatter(stacked, 'row', scatter_dimension=0, tiled=True)  68.4 us
    all_gather x2, waiting for transfers between devices, gather_cols(): return lax.all_gather(values, 'col', axis=0, tiled=True)  56.8 us
    all_gather x2, waiting for transfers between devices, out_project_heads(): whole = lax.all_gather(attended, 'row', axis=0, tiled=False)  53.6 us
    reduce_scatter x2, waiting for transfers between devices, out_project_heads(): lax.psum_scatter(summed.astype(jnp.bfloat16), 'col', scatter_dimension=0,...  50.2 us
    another operation x12, local copies, waits for them, and re-layouts, head_project(): stacked = jnp.stack(parts, axis=2).transpose(1, 0, 2, 3)  36.9 us
    sub x1, other arithmetic, attend_block(): weights = jnp.where(allowed[None], jnp.exp(scores - peak), 0.0)  36.8 us
    dot_general x6, matrix products, head_project(): jnp.dot(values, w, preferred_element_type=jnp.float32).astype(jnp.bfloat16)  27.6 us
  transfers between devices with their start and end apart: 14, of which 13 were waited for; matrix products, arithmetic and copies ran while one was open for 2% of the time, Pallas kernels for 0%

profile of v1, /device:TPU:28, one launch (start us, length us, event | category | flops | bytes accessed | tf_op | source)
XLA Modules:
  0.0 563.4 jit_solution(1932380565323348486)
XLA Ops:
  7.8 6.6 %psum.14 = f32[128]{0:T(128)S(1)} all-reduce(f32[128]{0:T(128)S(1)} %fusion.34), channel_id=1, replica_groups=mesh['req'=8,'row'=4,'col'=4] {'row'}, use_global_device_ids=true, to_apply=%region_3.4 | all-reduce | flops 128 | bytes 1024 | tf_op jit(solution)/shard_map/psum | solution.py:37
  16.9 26.4 %all-gather.6.cloned.1.call-done = bf16[512,1024]{1,0:T(8,128)(2,1)} async-done(((bf16[128,1024]{1,0:T(8,128)(2,1)}), bf16[512,1024]{1,0:T(8,128)(2,1)}) %all-gather.6.cloned.1.call-update) | async-done | bytes 1048592 | tf_op jit(solution)/shard_map/all_gather | solution.py:43
  76.0 8.6 %all_gather.20 = s32[2,512]{1,0:T(2,128)S(1)} all-gather(s32[2,128]{1,0:T(2,128)S(1)} %pad_add_fusion.1), channel_id=1, replica_groups=mesh['req'=8,'row'=4,'col'=4] {'col'}, dimensions={1}, use_global_device_ids=true | all-gather | bytes 5120 | tf_op jit(solution)/shard_map/all_gather | solution.py:152
  85.9 6.1 %collective-permute-start.1 = (s32[2,255]{1,0:T(2,128)S(1)}, s32[2,255]{1,0:T(2,128)S(1)}, u32[]{:S(2)}, u32[]{:S(2)}) collective-permute-start(s32[2,255]{1,0:T(2,128)S(1)} %get-tuple-element.20), channel_id=1, source_target_pairs={{16,0},{32,16},{48,32},{64,48},{80,64},{96,80},{112,96},{17,1},{33... | collective-permute-start | bytes 6128 | tf_op jit(solution)/shard_map/ppermute | solution.py:21
  93.4 19.0 %reduce-scatter.5.cloned.1.call-done = bf16[512,768]{0,1:T(8,128)(2,1)} async-done(((bf16[2048,768]{0,1:T(8,128)(2,1)}), bf16[512,768]{0,1:T(8,128)(2,1)}) %reduce-scatter.5.cloned.1.call-update) | async-done | bytes 786448 | tf_op jit(solution)/shard_map/reduce_scatter | solution.py:118
  115.7 6.9 %collective-permute-start.3 = (bf16[2,255,256]{1,2,0:T(8,128)(2,1)}, bf16[2,255,256]{1,2,0:T(8,128)(2,1)}, u32[]{:S(2)}, u32[]{:S(2)}) collective-permute-start(bf16[2,255,256]{1,2,0:T(8,128)(2,1)} %get-tuple-element.16), channel_id=1, source_target_pairs={{16,0},{32,16},{48,32},{64,48},{80,64},{96,80},{112,96},{17,1},{33... | collective-permute-start | bytes 783368 | tf_op jit(solution)/shard_map/ppermute | solution.py:21
  130.0 4.6 fusion.70
  138.0 26.8 %all-gather.8.cloned.1.call-done = bf16[4,512,256]{2,1,0:T(8,128)(2,1)} async-done(((bf16[1,512,256]{2,1,0:T(8,128)(2,1)}), bf16[4,512,256]{2,1,0:T(8,128)(2,1)}) %all-gather.8.cloned.1.call-update) | async-done | bytes 1048592 | tf_op jit(solution)/shard_map/all_gather | solution.py:123
  171.2 22.9 %reduce-scatter.7.cloned.1.call-done = bf16[128,1024]{1,0:T(8,128)(2,1)} async-done(((bf16[512,1024]{1,0:T(8,128)(2,1)}), bf16[128,1024]{1,0:T(8,128)(2,1)}) %reduce-scatter.7.cloned.1.call-update) | async-done | bytes 262160 | tf_op jit(solution)/shard_map/reduce_scatter | solution.py:126
  204.8 5.7 %psum.15 = f32[192]{0:T(256)S(1)} all-reduce(f32[192]{0:T(256)S(1)} %get-tuple-element.23), channel_id=1, replica_groups=mesh['req'=8,'row'=4,'col'=4] {'row'}, use_global_device_ids=true, to_apply=%region_9.10 | all-reduce | flops 192 | bytes 1536 | tf_op jit(solution)/shard_map/psum | solution.py:37
  211.7 30.4 %all-gather.10.cloned.1.call-done = bf16[768,1024]{1,0:T(8,128)(2,1)} async-done(((bf16[192,1024]{1,0:T(8,128)(2,1)}), bf16[768,1024]{1,0:T(8,128)(2,1)}) %all-gather.10.cloned.1.call-update) | async-done | bytes 1572880 | tf_op jit(solution)/shard_map/all_gather | solution.py:43
  242.1 5.0 convolution_convert_fusion
  255.2 5.0 convolution_convert_fusion.2
  268.3 5.0 convolution_convert_fusion.1
  281.4 6.0 %pad_maximum_fusion = bf16[768,4,3,256]{0,1,3,2:T(4,128)(2,1)S(1)} fusion(bf16[768,4,1,256]{0,1,3,2:T(4,128)(2,1)} %copy.37, bf16[768,4,1,256]{0,1,3,2:T(4,128)(2,1)} %copy.36, bf16[768,4,1,256]{0,1,3,2:T(4,128)(2,1)} %copy.35), kind=kLoop, calls=%fused_computation.14 | loop fusion | flops 4718592 | bytes 9437184 | tf_op jit(solution)/shard_map/stack | solution.py:116
  290.6 49.3 %reduce-scatter.9.cloned.1.call-done = bf16[768,768]{0,1:T(8,128)(2,1)} async-done(((bf16[3072,768]{0,1:T(8,128)(2,1)}), bf16[768,768]{0,1:T(8,128)(2,1)}) %reduce-scatter.9.cloned.1.call-update) | async-done | bytes 1179664 | tf_op jit(solution)/shard_map/reduce_scatter | solution.py:118
  342.6 5.7 %iota_compare_fusion = pred[768,6144]{1,0:T(8,128)(4,1)} fusion(s32[768]{0:T(1024)S(1)} %iota_add_fusion), kind=kLoop, calls=%fused_computation.12 | loop fusion | flops 4718592 | bytes 4721664 | tf_op jit(solution)/shard_map/ge | solution.py:209
  348.2 79.6 %all-gather.12.cloned.1.call-done = bf16[2,6144,256]{1,2,0:T(8,128)(2,1)} async-done(((bf16[2,768,256]{1,2,0:T(8,128)(2,1)}), bf16[2,6144,256]{1,2,0:T(8,128)(2,1)}) %all-gather.12.cloned.1.call-update) | async-done | bytes 6291472 | tf_op jit(solution)/shard_map/all_gather | solution.py:206
  427.8 5.4 fusion.64
  433.2 14.7 %fusion.72 = f32[2,768,6144]{2,1,0:T(8,128)} fusion(bf16[768,2,128]{0,2,1:T(8,128)(2,1)S(1)} %bitcast.96, bf16[6144,2,128]{0,2,1:T(8,128)(2,1)S(1)} %bitcast.90), kind=kOutput, calls=%fused_computation.120 | convolution fusion | flops 2415919104 | bytes 41287680 | tf_op jit(solution)/shard_map/qhd,khd->hqk/dot_general | solution.py:62
  447.9 36.8 %fusion.71 = (f32[2,768]{1,0:T(2,128)S(1)}, bf16[2,768,6144]{2,1,0:T(8,128)(2,1)}) fusion(f32[2,768,6144]{2,1,0:T(8,128)} %fusion.72, pred[768,6144]{1,0:T(8,128)(4,1)S(1)} %bitcast.94), kind=kOutput, calls=%fused_computation.119 | output fusion | flops 75503616 | bytes 61347840 | tf_op jit(solution)/shard_map/sub | solution.py:67
  484.8 10.4 %fusion.31 = bf16[768,2,128]{0,2,1:T(8,128)(2,1)S(1)} fusion(bf16[6144,2,128]{0,2,1:T(8,128)(2,1)} %bitcast.95, bf16[2,768,6144]{2,1,0:T(8,128)(2,1)} %get-tuple-element.26, f32[768,2]{0,1:T(2,128)S(1)} %bitcast.107), kind=kOutput, calls=%fused_computation.41 | convolution fusion | flops 2416312320 | bytes 22419456 | tf_op jit(solution)/shard_map/hqk,khd->qhd/dot_general | solution.py:69
  496.2 26.8 %all-gather.14.cloned.1.call-done = bf16[4,768,256]{2,1,0:T(8,128)(2,1)} async-done(((bf16[1,768,256]{2,1,0:T(8,128)(2,1)}), bf16[4,768,256]{2,1,0:T(8,128)(2,1)}) %all-gather.14.cloned.1.call-update) | async-done | bytes 1572880 | tf_op jit(solution)/shard_map/all_gather | solution.py:123
  527.3 27.3 %reduce-scatter.11.cloned.1.call-done = bf16[192,1024]{1,0:T(8,128)(2,1)} async-done(((bf16[768,1024]{1,0:T(8,128)(2,1)}), bf16[192,1024]{1,0:T(8,128)(2,1)}) %reduce-scatter.11.cloned.1.call-update) | async-done | bytes 393232 | tf_op jit(solution)/shard_map/reduce_scatter | solution.py:126
  (109 shorter events, 108.6 us)
Async XLA Ops:
  6.5 516.4 %copy-start = (bf16[1024,1024]{1,0:T(8,128)(2,1)S(1)}, bf16[1024,1024]{1,0:T(8,128)(2,1)}, u32[]{:S(2)}) copy-start(bf16[1024,1024]{1,0:T(8,128)(2,1)} %param.27) | copy-start | bytes 6291460
  6.5 36.7 %all-gather.6.cloned.1.call-start = ((), (), s32[]{:S(2)}) async-start(), calls=%async_computation.4 | async-start | bytes 1310720 | tf_op jit(solution)/shard_map/all_gather | solution.py:43
  16.9 95.5 %reduce-scatter.5.cloned.1.call-start = ((), (), s32[]{:S(2)}) async-start(), calls=%async_computation.5 | async-start | bytes 3932160 | tf_op jit(solution)/shard_map/reduce_scatter | solution.py:118
  75.3 0.7 copy-start.3
  75.3 0.7 copy-start.4
  75.3 89.4 %all-gather.8.cloned.1.call-start = ((), (), s32[]{:S(2)}) async-start(), calls=%async_computation.6 | async-start | bytes 1310720 | tf_op jit(solution)/shard_map/all_gather | solution.py:123
  84.6 7.4 %collective-permute-start = (s32[2,255]{1,0:T(2,128)S(1)}, s32[2,255]{1,0:T(2,128)S(1)}, u32[]{:S(2)}, u32[]{:S(2)}) collective-permute-start(s32[2,255]{1,0:T(2,128)S(1)} %get-tuple-element.19), channel_id=1, source_target_pairs={{0,16},{16,32},{32,48},{48,64},{64,80},{80,96},{96,112},{1,17},{17... | collective-permute-start | bytes 6128 | tf_op jit(solution)/shard_map/ppermute | solution.py:19
  85.9 7.3 %collective-permute-start.1 = (s32[2,255]{1,0:T(2,128)S(1)}, s32[2,255]{1,0:T(2,128)S(1)}, u32[]{:S(2)}, u32[]{:S(2)}) collective-permute-start(s32[2,255]{1,0:T(2,128)S(1)} %get-tuple-element.20), channel_id=1, source_target_pairs={{16,0},{32,16},{48,32},{64,48},{80,64},{96,80},{112,96},{17,1},{33... | collective-permute-start | bytes 6128 | tf_op jit(solution)/shard_map/ppermute | solution.py:21
  114.4 12.9 %collective-permute-start.2 = (bf16[2,255,256]{1,2,0:T(8,128)(2,1)}, bf16[2,255,256]{1,2,0:T(8,128)(2,1)}, u32[]{:S(2)}, u32[]{:S(2)}) collective-permute-start(bf16[2,255,256]{1,2,0:T(8,128)(2,1)} %get-tuple-element.15), channel_id=1, source_target_pairs={{0,16},{16,32},{32,48},{48,64},{64,80},{80,96},{96,112},{1,17},{17... | collective-permute-start | bytes 783368 | tf_op jit(solution)/shard_map/ppermute | solution.py:19
  115.7 11.9 %collective-permute-start.3 = (bf16[2,255,256]{1,2,0:T(8,128)(2,1)}, bf16[2,255,256]{1,2,0:T(8,128)(2,1)}, u32[]{:S(2)}, u32[]{:S(2)}) collective-permute-start(bf16[2,255,256]{1,2,0:T(8,128)(2,1)} %get-tuple-element.16), channel_id=1, source_target_pairs={{16,0},{32,16},{48,32},{64,48},{80,64},{96,80},{112,96},{17,1},{33... | collective-permute-start | bytes 783368 | tf_op jit(solution)/shard_map/ppermute | solution.py:21
  137.9 56.2 %reduce-scatter.7.cloned.1.call-start = ((), (), s32[]{:S(2)}) async-start(), calls=%async_computation.7 | async-start | bytes 1310720 | tf_op jit(solution)/shard_map/reduce_scatter | solution.py:126
  164.8 4.3 copy-start.2
  168.9 25.2 %copy-start.1 = (bf16[128,1024]{1,0:T(8,128)(2,1)S(1)}, bf16[128,1024]{1,0:T(8,128)(2,1)}, u32[]{:S(2)}) copy-start(bf16[128,1024]{1,0:T(8,128)(2,1)} %param.15) | copy-start | bytes 786436
  169.0 73.1 %all-gather.10.cloned.1.call-start = ((), (), s32[]{:S(2)}) async-start(), calls=%async_computation.8 | async-start | bytes 1966080 | tf_op jit(solution)/shard_map/all_gather | solution.py:43
  195.2 8.3 %collective-permute-start.4 = (bf16[128,1024]{1,0:T(8,128)(2,1)S(1)}, bf16[128,1024]{1,0:T(8,128)(2,1)S(1)}, u32[]{:S(2)}, u32[]{:S(2)}) collective-permute-start(bf16[128,1024]{1,0:T(8,128)(2,1)S(1)} %fusion.37), channel_id=1, source_target_pairs={{1,0},{2,1},{3,2},{16,3},{17,16},{18,17},{19,18},{32,19},{33,32},{... | collective-permute-start | bytes 786440 | tf_op jit(solution)/shard_map/ppermute | solution.py:31
  211.4 128.6 %reduce-scatter.9.cloned.1.call-start = ((), (), s32[]{:S(2)}) async-start(), calls=%async_computation.9 | async-start | bytes 5898240 | tf_op jit(solution)/shard_map/reduce_scatter | solution.py:118
  290.6 137.2 %all-gather.12.cloned.1.call-start = ((), (), s32[]{:S(2)}) async-start(), calls=%async_computation.10 | async-start | bytes 7077888 | tf_op jit(solution)/shard_map/all_gather | solution.py:206
  342.3 180.7 %all-gather.14.cloned.1.call-start = ((), (), s32[]{:S(2)}) async-start(), calls=%async_computation.11 | async-start | bytes 1966080 | tf_op jit(solution)/shard_map/all_gather | solution.py:123
  427.8 20.1 %slice-start = ((s8[4718592]{0:T(1024)(128)(4,1)}), s8[4194304]{0:T(1024)(128)(4,1)S(1)}, s32[]{:S(2)}) async-start(s8[4718592]{0:T(1024)(128)(4,1)} %bitcast.93), calls=%async_computation.13 | async-start | bytes 8388608
  433.2 14.7 %slice-start.1 = ((s8[4718592]{0:T(1024)(128)(4,1)}), s8[524288]{0:T(1024)(128)(4,1)S(1)}, s32[]{:S(2)}) async-start(s8[4718592]{0:T(1024)(128)(4,1)} %bitcast.93), calls=%async_computation.14 | async-start | bytes 1048576
  496.1 58.5 %reduce-scatter.11.cloned.1.call-start = ((), (), s32[]{:S(2)}) async-start(), calls=%async_computation.12 | async-start | bytes 1966080 | tf_op jit(solution)/shard_map/reduce_scatter | solution.py:126
Sparse Core Ops, SparseCore 0:
  17.0 26.2 all-gather.5
  75.5 36.8 reduce-scatter.4
  138.0 26.7 all-gather.7
  169.1 25.0 reduce-scatter.6
  211.5 30.4 all-gather.9
  290.7 49.2 reduce-scatter.8
  342.6 85.1 all-gather.11
  496.3 26.6 all-gather.13
  527.4 27.1 reduce-scatter.10

commit v2 on v1

--- a/solution.py
+++ b/solution.py
@@ -104,18 +104,15 @@
 
 
 def head_project(values, weights):
-    count = values.shape[0]
     row_count = lax.axis_size("row")
     width = weights[0].shape[1]
-    parts = [
-        jnp.dot(values, w, preferred_element_type=jnp.float32)
-        .astype(jnp.bfloat16)
-        .reshape(count, row_count, width // row_count)
-        for w in weights
-    ]
-    stacked = jnp.stack(parts, axis=2).transpose(1, 0, 2, 3)
-    stacked = stacked.reshape(row_count * count, len(weights) * (width // row_count))
-    return lax.psum_scatter(stacked, "row", scatter_dimension=0, tiled=True)
+    depth = weights[0].shape[0]
+    shaped = jnp.stack(
+        [w.reshape(depth, row_count, width // row_count) for w in weights], axis=2
+    ).reshape(depth, row_count, len(weights) * (width // row_count))
+    summed = jnp.einsum("tf,frc->rtc", values, shaped, preferred_element_type=jnp.float32)
+    summed = summed.astype(jnp.bfloat16).reshape(row_count * values.shape[0], -1)
+    return lax.psum_scatter(summed, "row", scatter_dimension=0, tiled=True)
 
 
 def out_project_heads(attended, weight):

time: 571 us -> 513 us (0.90)
  waiting for transfers between devices: 316 us -> 280 us
  matrix products: 69.7 us -> 59.4 us
  local copies, waits for them, and re-layouts: 59.1 us -> 51.4 us
    another operation x13 -> x1, local copies, waits for them, and re-layouts: 37 us -> 0.11 us  [the longest x12 36.9 us: head_project(): stacked = jnp.stack(parts, axis=2).transpose(1, 0, 2, 3)]
    all_gather x2, waiting for transfers between devices: 56.8 us -> 20 us  [gather_cols(): return lax.all_gather(values, 'col', axis=0, tiled=True)]
    unnamed x16 -> x20, local copies, waits for them, and re-layouts: 6.46 us -> 24.3 us
    reshape x1 -> x3, local copies, waits for them, and re-layouts: 0.01 us -> 11.3 us  [the longest x2 11.3 us: head_project(): summed.astype(jnp.bfloat16).reshape(row_count * values.shape[0], -1)]
    dot_general x6 -> x2, matrix products: 27.6 us -> 17.3 us  [head_project(): jnp.einsum('tf,frc->rtc', values, shaped, preferred_element_type=jnp.floa...]
  transfers between devices with their start and end apart: 14 -> 14, of which waited for: 13 -> 13; matrix products, arithmetic and copies ran while one was open for 2% -> 10% of each run, Pallas kernels for 0% -> 0%
where the time goes in v2:
time: 513 us; the launch traced here: 511 us
  waiting for transfers between devices  280 us (55%)
  other arithmetic  67.9 us (13%)
  matrix products  59.4 us (12%)
  local copies, waits for them, and re-layouts  51.4 us (10%)
  blocking collectives  20.8 us (4%)
  starting transfers between devices  18.3 us (4%)
  between operations  13.5 us (3%)
    all_gather x1, waiting for transfers between devices, per_device(): piece = lax.all_gather(dec_pairs, 'req', axis=1, tiled=True)  79.8 us
    reduce_scatter x2, waiting for transfers between devices, head_project(): return lax.psum_scatter(summed, 'row', scatter_dimension=0, tiled=True)  68.4 us
    all_gather x2, waiting for transfers between devices, out_project_heads(): whole = lax.all_gather(attended, 'row', axis=0, tiled=False)  53.6 us
    reduce_scatter x2, waiting for transfers between devices, out_project_heads(): lax.psum_scatter(summed.astype(jnp.bfloat16), 'col', scatter_dimension=0,...  50.2 us
    sub x1, other arithmetic, attend_block(): weights = jnp.where(allowed[None], jnp.exp(scores - peak), 0.0)  36.8 us
    unnamed x20, local copies, waits for them, and re-layouts  24.3 us
    all_gather x2, waiting for transfers between devices, gather_cols(): return lax.all_gather(values, 'col', axis=0, tiled=True)  20 us
    dot_general x2, matrix products, head_project(): jnp.einsum('tf,frc->rtc', values, shaped, preferred_element_type=jnp.floa...  17.3 us
  transfers between devices with their start and end apart: 14, of which 13 were waited for; matrix products, arithmetic and copies ran while one was open for 10% of the time, Pallas kernels for 0%

profile of v2, /device:TPU:28, one launch (start us, length us, event | category | flops | bytes accessed | tf_op | source)
XLA Modules:
  0.0 511.1 jit_solution(722304668159904372)
XLA Ops:
  7.8 6.6 %psum.14 = f32[128]{0:T(128)S(1)} all-reduce(f32[128]{0:T(128)S(1)} %fusion.36), channel_id=1, replica_groups=mesh['req'=8,'row'=4,'col'=4] {'row'}, use_global_device_ids=true, to_apply=%region_3.4 | all-reduce | flops 128 | bytes 1024 | tf_op jit(solution)/shard_map/psum | solution.py:37
  28.8 6.6 %pad_maximum_fusion = bf16[1024,4,3,256]{0,3,2,1:T(8,128)(2,1)} fusion(bf16[1024,4,1,256]{0,3,2,1:T(8,128)(2,1)} %bitcast.89, bf16[1024,4,1,256]{0,3,2,1:T(8,128)(2,1)} %bitcast.88, bf16[1024,4,1,256]{0,3,2,1:T(8,128)(2,1)} %bitcast.87), kind=kLoop, calls=%fused_computation.14 | loop fusion | flops 6291456 | bytes 12582912 | tf_op jit(solution)/shard_map/stack | solution.py:110
  35.4 7.9 %all-gather.6.cloned.1.call-done = bf16[512,1024]{1,0:T(8,128)(2,1)} async-done(((bf16[128,1024]{1,0:T(8,128)(2,1)}), bf16[512,1024]{1,0:T(8,128)(2,1)}) %all-gather.6.cloned.1.call-update) | async-done | bytes 1048592 | tf_op jit(solution)/shard_map/all_gather | solution.py:43
  43.3 8.2 %convolution_convert_fusion.1 = bf16[4,768,512]{1,2,0:T(8,128)(2,1)} fusion(bf16[1024,4,768]{0,2,1:T(8,128)(2,1)} %bitcast.93, bf16[512,1024]{1,0:T(8,128)(2,1)} %all-gather.6.cloned.1.call-done), kind=kOutput, calls=%fused_computation.21 | convolution fusion | flops 3222798336 | bytes 10485760 | tf_op jit(solution)/shard_map/tf,frc->rtc/dot_general | solution.py:113
  56.8 8.6 %all_gather.20 = s32[2,512]{1,0:T(2,128)S(1)} all-gather(s32[2,128]{1,0:T(2,128)S(1)} %pad_add_fusion.1), channel_id=1, replica_groups=mesh['req'=8,'row'=4,'col'=4] {'col'}, dimensions={1}, use_global_device_ids=true | all-gather | bytes 5120 | tf_op jit(solution)/shard_map/all_gather | solution.py:149
  66.7 6.1 %collective-permute-start.1 = (s32[2,255]{1,0:T(2,128)S(1)}, s32[2,255]{1,0:T(2,128)S(1)}, u32[]{:S(2)}, u32[]{:S(2)}) collective-permute-start(s32[2,255]{1,0:T(2,128)S(1)} %get-tuple-element.20), channel_id=1, source_target_pairs={{16,0},{32,16},{48,32},{64,48},{80,64},{96,80},{112,96},{17,1},{33... | collective-permute-start | bytes 6128 | tf_op jit(solution)/shard_map/ppermute | solution.py:21
  74.2 19.0 %reduce-scatter.5.cloned.1.call-done = bf16[512,768]{0,1:T(8,128)(2,1)} async-done(((bf16[2048,768]{0,1:T(8,128)(2,1)}), bf16[512,768]{0,1:T(8,128)(2,1)}) %reduce-scatter.5.cloned.1.call-update) | async-done | bytes 786448 | tf_op jit(solution)/shard_map/reduce_scatter | solution.py:115
  96.5 6.8 %collective-permute-start.3 = (bf16[2,255,256]{1,2,0:T(8,128)(2,1)}, bf16[2,255,256]{1,2,0:T(8,128)(2,1)}, u32[]{:S(2)}, u32[]{:S(2)}) collective-permute-start(bf16[2,255,256]{1,2,0:T(8,128)(2,1)} %get-tuple-element.16), channel_id=1, source_target_pairs={{16,0},{32,16},{48,32},{64,48},{80,64},{96,80},{112,96},{17,1},{33... | collective-permute-start | bytes 783368 | tf_op jit(solution)/shard_map/ppermute | solution.py:21
  118.8 26.8 %all-gather.8.cloned.1.call-done = bf16[4,512,256]{2,1,0:T(8,128)(2,1)} async-done(((bf16[1,512,256]{2,1,0:T(8,128)(2,1)}), bf16[4,512,256]{2,1,0:T(8,128)(2,1)}) %all-gather.8.cloned.1.call-update) | async-done | bytes 1048592 | tf_op jit(solution)/shard_map/all_gather | solution.py:120
  152.1 22.9 %reduce-scatter.7.cloned.1.call-done = bf16[128,1024]{1,0:T(8,128)(2,1)} async-done(((bf16[512,1024]{1,0:T(8,128)(2,1)}), bf16[128,1024]{1,0:T(8,128)(2,1)}) %reduce-scatter.7.cloned.1.call-update) | async-done | bytes 262160 | tf_op jit(solution)/shard_map/reduce_scatter | solution.py:123
  185.7 5.7 %psum.15 = f32[192]{0:T(256)S(1)} all-reduce(f32[192]{0:T(256)S(1)} %get-tuple-element.23), channel_id=1, replica_groups=mesh['req'=8,'row'=4,'col'=4] {'row'}, use_global_device_ids=true, to_apply=%region_9.10 | all-reduce | flops 192 | bytes 1536 | tf_op jit(solution)/shard_map/psum | solution.py:37
  204.2 6.6 %pad_maximum_fusion.1 = bf16[1024,4,3,256]{0,3,2,1:T(8,128)(2,1)} fusion(bf16[1024,4,1,256]{0,3,2,1:T(8,128)(2,1)} %bitcast.92, bf16[1024,4,1,256]{0,3,2,1:T(8,128)(2,1)} %bitcast.91, bf16[1024,4,1,256]{0,3,2,1:T(8,128)(2,1)} %bitcast.90), kind=kLoop, calls=%fused_computation.15 | loop fusion | flops 6291456 | bytes 12582912 | tf_op jit(solution)/shard_map/stack | solution.py:110
  210.8 12.1 %all-gather.10.cloned.1.call-done = bf16[768,1024]{1,0:T(8,128)(2,1)} async-done(((bf16[192,1024]{1,0:T(8,128)(2,1)}), bf16[768,1024]{1,0:T(8,128)(2,1)}) %all-gather.10.cloned.1.call-update) | async-done | bytes 1572880 | tf_op jit(solution)/shard_map/all_gather | solution.py:43
  222.9 9.1 %convolution_convert_fusion = bf16[4,768,768]{1,2,0:T(8,128)(2,1)} fusion(bf16[1024,4,768]{0,2,1:T(8,128)(2,1)} %bitcast.94, bf16[768,1024]{1,0:T(8,128)(2,1)} %all-gather.10.cloned.1.call-done), kind=kOutput, calls=%fused_computation.20 | convolution fusion | flops 4834197504 | bytes 12582912 | tf_op jit(solution)/shard_map/tf,frc->rtc/dot_general | solution.py:113
  232.0 6.6 %copy.53 = bf16[3072,768]{0,1:T(8,128)(2,1)} copy(bf16[3072,768]{1,0:T(8,128)(2,1)} %bitcast.95) | data formatting | bytes 9437184 | tf_op jit(solution)/shard_map/reshape | solution.py:114
  238.7 49.3 %reduce-scatter.9.cloned.1.call-done = bf16[768,768]{0,1:T(8,128)(2,1)} async-done(((bf16[3072,768]{0,1:T(8,128)(2,1)}), bf16[768,768]{0,1:T(8,128)(2,1)}) %reduce-scatter.9.cloned.1.call-update) | async-done | bytes 1179664 | tf_op jit(solution)/shard_map/reduce_scatter | solution.py:115
  290.4 5.7 %iota_compare_fusion = pred[768,6144]{1,0:T(8,128)(4,1)} fusion(s32[768]{0:T(1024)S(1)} %iota_add_fusion), kind=kLoop, calls=%fused_computation.12 | loop fusion | flops 4718592 | bytes 4721664 | tf_op jit(solution)/shard_map/ge | solution.py:206
  296.1 79.8 %all-gather.12.cloned.1.call-done = bf16[2,6144,256]{1,2,0:T(8,128)(2,1)} async-done(((bf16[2,768,256]{1,2,0:T(8,128)(2,1)}), bf16[2,6144,256]{1,2,0:T(8,128)(2,1)}) %all-gather.12.cloned.1.call-update) | async-done | bytes 6291472 | tf_op jit(solution)/shard_map/all_gather | solution.py:203
  375.9 5.4 %fusion.66 = (bf16[1,6144,256]{1,2,0:T(8,128)(2,1)S(1)}, bf16[1,6144,256]{1,2,0:T(8,128)(2,1)}) fusion(bf16[2,6144,256]{1,2,0:T(8,128)(2,1)} %all-gather.12.cloned.1.call-done), kind=kLoop, calls=%fused_computation.110 | loop fusion | bytes 12582912 | tf_op jit(solution)/shard_map/slice | solution.py:207
  381.3 14.7 %fusion.74 = f32[2,768,6144]{2,1,0:T(8,128)} fusion(bf16[768,2,128]{0,2,1:T(8,128)(2,1)S(1)} %bitcast.100, bf16[6144,2,128]{0,2,1:T(8,128)(2,1)S(1)} %bitcast.86), kind=kOutput, calls=%fused_computation.118 | convolution fusion | flops 2415919104 | bytes 41287680 | tf_op jit(solution)/shard_map/qhd,khd->hqk/dot_general | solution.py:62
  396.1 36.8 %fusion.73 = (f32[2,768]{1,0:T(2,128)S(1)}, bf16[2,768,6144]{2,1,0:T(8,128)(2,1)}) fusion(f32[2,768,6144]{2,1,0:T(8,128)} %fusion.74, pred[768,6144]{1,0:T(8,128)(4,1)S(1)} %bitcast.97), kind=kOutput, calls=%fused_computation.117 | output fusion | flops 75503616 | bytes 61347840 | tf_op jit(solution)/shard_map/sub | solution.py:67
  432.9 10.4 %fusion.32 = bf16[768,2,128]{0,2,1:T(8,128)(2,1)S(1)} fusion(bf16[6144,2,128]{0,2,1:T(8,128)(2,1)} %bitcast.99, bf16[2,768,6144]{2,1,0:T(8,128)(2,1)} %get-tuple-element.26, f32[768,2]{0,1:T(2,128)S(1)} %bitcast.111), kind=kOutput, calls=%fused_computation.38 | convolution fusion | flops 2416312320 | bytes 22419456 | tf_op jit(solution)/shard_map/hqk,khd->qhd/dot_general | solution.py:69
  444.3 26.8 %all-gather.14.cloned.1.call-done = bf16[4,768,256]{2,1,0:T(8,128)(2,1)} async-done(((bf16[1,768,256]{2,1,0:T(8,128)(2,1)}), bf16[4,768,256]{2,1,0:T(8,128)(2,1)}) %all-gather.14.cloned.1.call-update) | async-done | bytes 1572880 | tf_op jit(solution)/shard_map/all_gather | solution.py:120
  475.4 27.3 %reduce-scatter.11.cloned.1.call-done = bf16[192,1024]{1,0:T(8,128)(2,1)} async-done(((bf16[768,1024]{1,0:T(8,128)(2,1)}), bf16[192,1024]{1,0:T(8,128)(2,1)}) %reduce-scatter.11.cloned.1.call-update) | async-done | bytes 393232 | tf_op jit(solution)/shard_map/reduce_scatter | solution.py:123
  (99 shorter events, 81.8 us)
Async XLA Ops:
  6.5 464.5 %copy-start = (bf16[1024,1024]{1,0:T(8,128)(2,1)S(1)}, bf16[1024,1024]{1,0:T(8,128)(2,1)}, u32[]{:S(2)}) copy-start(bf16[1024,1024]{1,0:T(8,128)(2,1)} %param.27) | copy-start | bytes 6291460
  6.5 36.7 %all-gather.6.cloned.1.call-start = ((), (), s32[]{:S(2)}) async-start(), calls=%async_computation.4 | async-start | bytes 1310720 | tf_op jit(solution)/shard_map/all_gather | solution.py:43
  16.9 76.3 %reduce-scatter.5.cloned.1.call-start = ((), (), s32[]{:S(2)}) async-start(), calls=%async_computation.5 | async-start | bytes 3932160 | tf_op jit(solution)/shard_map/reduce_scatter | solution.py:115
  56.1 0.7 copy-start.3
  56.1 0.7 copy-start.4
  56.2 89.4 %all-gather.8.cloned.1.call-start = ((), (), s32[]{:S(2)}) async-start(), calls=%async_computation.6 | async-start | bytes 1310720 | tf_op jit(solution)/shard_map/all_gather | solution.py:120
  65.5 7.4 %collective-permute-start = (s32[2,255]{1,0:T(2,128)S(1)}, s32[2,255]{1,0:T(2,128)S(1)}, u32[]{:S(2)}, u32[]{:S(2)}) collective-permute-start(s32[2,255]{1,0:T(2,128)S(1)} %get-tuple-element.19), channel_id=1, source_target_pairs={{0,16},{16,32},{32,48},{48,64},{64,80},{80,96},{96,112},{1,17},{17... | collective-permute-start | bytes 6128 | tf_op jit(solution)/shard_map/ppermute | solution.py:19
  66.7 7.3 %collective-permute-start.1 = (s32[2,255]{1,0:T(2,128)S(1)}, s32[2,255]{1,0:T(2,128)S(1)}, u32[]{:S(2)}, u32[]{:S(2)}) collective-permute-start(s32[2,255]{1,0:T(2,128)S(1)} %get-tuple-element.20), channel_id=1, source_target_pairs={{16,0},{32,16},{48,32},{64,48},{80,64},{96,80},{112,96},{17,1},{33... | collective-permute-start | bytes 6128 | tf_op jit(solution)/shard_map/ppermute | solution.py:21
  95.3 12.9 %collective-permute-start.2 = (bf16[2,255,256]{1,2,0:T(8,128)(2,1)}, bf16[2,255,256]{1,2,0:T(8,128)(2,1)}, u32[]{:S(2)}, u32[]{:S(2)}) collective-permute-start(bf16[2,255,256]{1,2,0:T(8,128)(2,1)} %get-tuple-element.15), channel_id=1, source_target_pairs={{0,16},{16,32},{32,48},{48,64},{64,80},{80,96},{96,112},{1,17},{17... | collective-permute-start | bytes 783368 | tf_op jit(solution)/shard_map/ppermute | solution.py:19
  96.5 11.9 %collective-permute-start.3 = (bf16[2,255,256]{1,2,0:T(8,128)(2,1)}, bf16[2,255,256]{1,2,0:T(8,128)(2,1)}, u32[]{:S(2)}, u32[]{:S(2)}) collective-permute-start(bf16[2,255,256]{1,2,0:T(8,128)(2,1)} %get-tuple-element.16), channel_id=1, source_target_pairs={{16,0},{32,16},{48,32},{64,48},{80,64},{96,80},{112,96},{17,1},{33... | collective-permute-start | bytes 783368 | tf_op jit(solution)/shard_map/ppermute | solution.py:21
  118.7 56.3 %reduce-scatter.7.cloned.1.call-start = ((), (), s32[]{:S(2)}) async-start(), calls=%async_computation.7 | async-start | bytes 1310720 | tf_op jit(solution)/shard_map/reduce_scatter | solution.py:123
  145.6 4.3 copy-start.2
  145.6 29.4 %copy-start.1 = (bf16[128,1024]{1,0:T(8,128)(2,1)S(1)}, bf16[128,1024]{1,0:T(8,128)(2,1)}, u32[]{:S(2)}) copy-start(bf16[128,1024]{1,0:T(8,128)(2,1)} %param.15) | copy-start | bytes 786436
  149.8 73.1 %all-gather.10.cloned.1.call-start = ((), (), s32[]{:S(2)}) async-start(), calls=%async_computation.8 | async-start | bytes 1966080 | tf_op jit(solution)/shard_map/all_gather | solution.py:43
  176.0 8.3 %collective-permute-start.4 = (bf16[128,1024]{1,0:T(8,128)(2,1)S(1)}, bf16[128,1024]{1,0:T(8,128)(2,1)S(1)}, u32[]{:S(2)}, u32[]{:S(2)}) collective-permute-start(bf16[128,1024]{1,0:T(8,128)(2,1)S(1)} %fusion.39), channel_id=1, source_target_pairs={{1,0},{2,1},{3,2},{16,3},{17,16},{18,17},{19,18},{32,19},{33,32},{... | collective-permute-start | bytes 786440 | tf_op jit(solution)/shard_map/ppermute | solution.py:31
  192.3 95.8 %reduce-scatter.9.cloned.1.call-start = ((), (), s32[]{:S(2)}) async-start(), calls=%async_computation.9 | async-start | bytes 5898240 | tf_op jit(solution)/shard_map/reduce_scatter | solution.py:115
  238.7 137.2 %all-gather.12.cloned.1.call-start = ((), (), s32[]{:S(2)}) async-start(), calls=%async_computation.10 | async-start | bytes 7077888 | tf_op jit(solution)/shard_map/all_gather | solution.py:203
  290.4 180.7 %all-gather.14.cloned.1.call-start = ((), (), s32[]{:S(2)}) async-start(), calls=%async_computation.11 | async-start | bytes 1966080 | tf_op jit(solution)/shard_map/all_gather | solution.py:120
  375.9 20.1 %slice-start = ((s8[4718592]{0:T(1024)(128)(4,1)}), s8[4194304]{0:T(1024)(128)(4,1)S(1)}, s32[]{:S(2)}) async-start(s8[4718592]{0:T(1024)(128)(4,1)} %bitcast.96), calls=%async_computation.13 | async-start | bytes 8388608
  381.3 14.7 %slice-start.1 = ((s8[4718592]{0:T(1024)(128)(4,1)}), s8[524288]{0:T(1024)(128)(4,1)S(1)}, s32[]{:S(2)}) async-start(s8[4718592]{0:T(1024)(128)(4,1)} %bitcast.96), calls=%async_computation.14 | async-start | bytes 1048576
  444.3 58.5 %reduce-scatter.11.cloned.1.call-start = ((), (), s32[]{:S(2)}) async-start(), calls=%async_computation.12 | async-start | bytes 1966080 | tf_op jit(solution)/shard_map/reduce_scatter | solution.py:123
Sparse Core Ops, SparseCore 0:
  17.0 26.2 all-gather.5
  56.3 36.8 reduce-scatter.4
  118.9 26.6 all-gather.7
  149.9 25.0 reduce-scatter.6
  192.4 30.4 all-gather.9
  238.8 49.2 reduce-scatter.8
  290.7 85.1 all-gather.11
  444.4 26.6 all-gather.13
  475.6 27.1 reduce-scatter.10

commit v3 on v2

--- a/solution.py
+++ b/solution.py
@@ -2,6 +2,8 @@
 import jax.numpy as jnp
 from jax import lax
 from jax.sharding import PartitionSpec as P
+from jax.experimental import pallas as pl
+from jax.experimental.pallas import tpu as pltpu
 
 D = 4096
 HD = 128
@@ -123,6 +125,80 @@
     return lax.psum_scatter(
         summed.astype(jnp.bfloat16), "col", scatter_dimension=0, tiled=True
     ).astype(jnp.float32)
+
+
+def causal_attend(proj, keyvals, base, key_tile=512):
+    count = proj.shape[0]
+    heads = proj.shape[1] // (3 * HD)
+    total = keyvals.shape[0]
+    steps = total // key_tile
+    scale = HD ** (-0.5)
+
+    def body(base_ref, q_ref, k_ref, v_ref, o_ref, peak_ref, mass_ref, acc_ref):
+        step = pl.program_id(1)
+        first = base_ref[0]
+
+        @pl.when(step == 0)
+        def _():
+            peak_ref[...] = jnp.full(peak_ref.shape, -1e30, jnp.float32)
+            mass_ref[...] = jnp.zeros(mass_ref.shape, jnp.float32)
+            acc_ref[...] = jnp.zeros(acc_ref.shape, jnp.float32)
+
+        def fold(masked):
+            scores = lax.dot_general(
+                q_ref[...], k_ref[...], (((1,), (1,)), ((), ())),
+                preferred_element_type=jnp.float32) * scale
+            if masked:
+                rows = first + lax.broadcasted_iota(jnp.int32, scores.shape, 0)
+                cols = step * key_tile + lax.broadcasted_iota(jnp.int32, scores.shape, 1)
+                allowed = cols <= rows
+                scores = jnp.where(allowed, scores, -1e30)
+            old = peak_ref[...]
+            new = jnp.maximum(old, jnp.max(scores, axis=1, keepdims=True))
+            weights = jnp.exp(scores - new)
+            if masked:
+                weights = jnp.where(allowed, weights, 0.0)
+            shrink = jnp.exp(old - new)
+            mass_ref[...] = shrink * mass_ref[...] + jnp.sum(weights, axis=1, keepdims=True)
+            acc_ref[...] = shrink * acc_ref[...] + jnp.dot(
+                weights.astype(jnp.bfloat16), v_ref[...], preferred_element_type=jnp.float32)
+            peak_ref[...] = new
+
+        start = step * key_tile
+        end = start + key_tile - 1
+
+        @pl.when(end <= first)
+        def _():
+            fold(False)
+
+        @pl.when((end > first) & (start <= first + count - 1))
+        def _():
+            fold(True)
+
+        @pl.when(step == steps - 1)
+        def _():
+            o_ref[...] = (acc_ref[...] / mass_ref[...]).astype(o_ref.dtype)
+
+    grid_spec = pltpu.PrefetchScalarGridSpec(
+        num_scalar_prefetch=1,
+        grid=(heads, steps),
+        in_specs=[
+            pl.BlockSpec((count, HD), lambda h, j, b: (0, h)),
+            pl.BlockSpec((key_tile, HD), lambda h, j, b: (j, h)),
+            pl.BlockSpec((key_tile, HD), lambda h, j, b: (j, heads + h)),
+        ],
+        out_specs=pl.BlockSpec((count, HD), lambda h, j, b: (0, h)),
+        scratch_shapes=[
+            pltpu.VMEM((count, 1), jnp.float32),
+            pltpu.VMEM((count, 1), jnp.float32),
+            pltpu.VMEM((count, HD), jnp.float32),
+        ],
+    )
+    return pl.pallas_call(
+        body,
+        grid_spec=grid_spec,
+        out_shape=jax.ShapeDtypeStruct((count, heads * HD), jnp.bfloat16),
+    )(base, proj, keyvals, keyvals)
 
 
 def per_device(
@@ -199,12 +275,9 @@
     dec_cols = gather_cols(norm_local(mixed, dec_gain))
     dec_proj = head_project(dec_cols, (dec_wq, dec_wk, dec_wv))
     dec_rows = dec_cols.shape[0]
-    dec_pairs = jnp.stack([dec_proj[:, local : 2 * local], dec_proj[:, 2 * local :]])
-    piece = lax.all_gather(dec_pairs, "req", axis=1, tiled=True)
-    token_slots = lax.axis_index("req") * dec_rows + jnp.arange(dec_rows, dtype=jnp.int32)
-    all_slots = jnp.arange(piece.shape[1], dtype=jnp.int32)
-    causal = token_slots[:, None] >= all_slots[None, :]
-    dec_att = attend_block(dec_proj[:, :local], piece[0], piece[1], causal)
+    piece = lax.all_gather(dec_proj[:, local:], "req", axis=0, tiled=True)
+    base = (lax.axis_index("req") * dec_rows).astype(jnp.int32).reshape(1)
+    dec_att = causal_attend(dec_proj, piece, base)
     return (mixed.astype(jnp.float32) + out_project_heads(dec_att, dec_wo)).astype(jnp.bfloat16)
 
 

time: 513 us -> 487 us (0.949)
  Pallas kernels: 0 us -> 49.9 us
  other arithmetic: 67.9 us -> 24.3 us
  matrix products: 59.4 us -> 34.3 us
  local copies, waits for them, and re-layouts: 51.4 us -> 39.3 us
  waiting for transfers between devices: 280 us -> 292 us
  starting transfers between devices: 18.3 us -> 11.4 us
    pallas_call x0 -> x1, Pallas kernels: none -> 49.9 us  [causal_attend(): pl.pallas_call(body, grid_spec=grid_spec, out_shape=jax.ShapeDtypeStruct(...]
    sub x1 -> x0, other arithmetic: 36.8 us -> none  [attend_block(): weights = jnp.where(allowed[None], jnp.exp(scores - peak), 0.0)]
    dot_general x1 -> x0, matrix products: 14.7 us -> none  [attend_block(): jnp.einsum('qhd,khd->hqk', query_heads, split_heads(keys), preferred_elem...]
    ppermute x2, waiting for transfers between devices: 1.8 us -> 14.7 us  [with_halo(): lax.ppermute(tail, axis, [(i, (i + 1) % count) for i in range(ends)])]
    dot_general x2 -> x1, matrix products: 12.8 us -> 2.43 us  [attend_block(): jnp.einsum('hqk,khd->qhd', weights.astype(jnp.bfloat16), split_heads(valu...]
    ppermute x2, starting transfers between devices: 12.8 us -> 5.94 us  [with_halo(): lax.ppermute(head, axis, [((i + 1) % count, i) for i in range(ends)])]
    reshape x2 -> x1, local copies, waits for them, and re-layouts: 11.3 us -> 4.76 us  [head_project(): summed.astype(jnp.bfloat16).reshape(row_count * values.shape[0], -1)]
    all_gather x1, waiting for transfers between devices: 79.8 us -> 86.1 us  [per_device(): piece = lax.all_gather(dec_proj[:, local:], 'req', axis=0, tiled=True)]
  transfers between devices with their start and end apart: 14 -> 14, of which waited for: 13 -> 13; matrix products, arithmetic and copies ran while one was open for 10% -> 9% of each run, Pallas kernels for 0% -> 0%
where the time goes in v3:
time: 487 us; the launch traced here: 485 us
  waiting for transfers between devices  292 us (60%)
  Pallas kernels  49.9 us (10%)
  local copies, waits for them, and re-layouts  39.3 us (8%)
  matrix products  34.3 us (7%)
  other arithmetic  24.3 us (5%)
  blocking collectives  20.8 us (4%)
  between operations  13.4 us (3%)
  starting transfers between devices  11.4 us (2%)
    all_gather x1, waiting for transfers between devices, per_device(): piece = lax.all_gather(dec_proj[:, local:], 'req', axis=0, tiled=True)  86.1 us
    reduce_scatter x2, waiting for transfers between devices, head_project(): return lax.psum_scatter(summed, 'row', scatter_dimension=0, tiled=True)  67.6 us
    reduce_scatter x2, waiting for transfers between devices, out_project_heads(): lax.psum_scatter(summed.astype(jnp.bfloat16), 'col', scatter_dimension=0,...  50.2 us
    pallas_call x1, Pallas kernels, causal_attend(): pl.pallas_call(body, grid_spec=grid_spec, out_shape=jax.ShapeDtypeStruct(...  49.9 us
    all_gather x2, waiting for transfers between devices, out_project_heads(): whole = lax.all_gather(attended, 'row', axis=0, tiled=False)  47.6 us
    unnamed x16, local copies, waits for them, and re-layouts  24.3 us
    all_gather x2, waiting for transfers between devices, gather_cols(): return lax.all_gather(values, 'col', axis=0, tiled=True)  20.4 us
    dot_general x2, matrix products, head_project(): jnp.einsum('tf,frc->rtc', values, shaped, preferred_element_type=jnp.floa...  17.3 us
  transfers between devices with their start and end apart: 14, of which 13 were waited for; matrix products, arithmetic and copies ran while one was open for 9% of the time, Pallas kernels for 0%

profile of v3, /device:TPU:28, one launch (start us, length us, event | category | flops | bytes accessed | tf_op | source)
XLA Modules:
  0.0 485.5 jit_solution(15492636714619245055)
XLA Ops:
  8.5 6.6 %psum.14 = f32[128]{0:T(128)S(1)} all-reduce(f32[128]{0:T(128)S(1)} %fusion.20), channel_id=1, replica_groups=mesh['req'=8,'row'=4,'col'=4] {'row'}, use_global_device_ids=true, to_apply=%region_3.4 | all-reduce | flops 128 | bytes 1024 | tf_op jit(solution)/shard_map/psum | solution.py:39
  28.8 6.5 %pad_maximum_fusion = bf16[1024,4,3,256]{0,3,2,1:T(8,128)(2,1)} fusion(bf16[1024,4,1,256]{0,3,2,1:T(8,128)(2,1)} %bitcast.69, bf16[1024,4,1,256]{0,3,2,1:T(8,128)(2,1)} %bitcast.70, bf16[1024,4,1,256]{0,3,2,1:T(8,128)(2,1)} %bitcast.71), kind=kLoop, calls=%fused_computation.4 | loop fusion | flops 6291456 | bytes 12582912 | tf_op jit(solution)/shard_map/stack | solution.py:112
  35.3 8.0 %all-gather.7.cloned.1.call-done = bf16[512,1024]{1,0:T(8,128)(2,1)} async-done(((bf16[128,1024]{1,0:T(8,128)(2,1)}), bf16[512,1024]{1,0:T(8,128)(2,1)}) %all-gather.7.cloned.1.call-update) | async-done | bytes 1048592 | tf_op jit(solution)/shard_map/all_gather | solution.py:45
  43.3 8.2 %convolution_convert_fusion.1 = bf16[4,768,512]{1,2,0:T(8,128)(2,1)} fusion(bf16[1024,4,768]{0,2,1:T(8,128)(2,1)} %bitcast.75, bf16[512,1024]{1,0:T(8,128)(2,1)} %all-gather.7.cloned.1.call-done), kind=kOutput, calls=%fused_computation.11 | convolution fusion | flops 3222798336 | bytes 10485760 | tf_op jit(solution)/shard_map/tf,frc->rtc/dot_general | solution.py:115
  51.5 4.8 copy.39
  56.9 8.6 %all_gather.22 = s32[2,512]{1,0:T(2,128)S(1)} all-gather(s32[2,128]{1,0:T(2,128)S(1)} %pad_add_fusion.1), channel_id=1, replica_groups=mesh['req'=8,'row'=4,'col'=4] {'col'}, dimensions={1}, use_global_device_ids=true | all-gather | bytes 5120 | tf_op jit(solution)/shard_map/all_gather | solution.py:225
  69.4 5.6 %collective-permute-done = s32[2,255]{1,0:T(2,128)S(1)} collective-permute-done((s32[2,255]{1,0:T(2,128)S(1)}, s32[2,255]{1,0:T(2,128)S(1)}, u32[]{:S(2)}, u32[]{:S(2)}) %collective-permute-start) | collective-permute-done | bytes 2072 | tf_op jit(solution)/shard_map/ppermute | solution.py:21
  75.1 18.2 %reduce-scatter.5.cloned.1.call-done = bf16[512,768]{0,1:T(8,128)(2,1)} async-done(((bf16[2048,768]{0,1:T(8,128)(2,1)}), bf16[512,768]{0,1:T(8,128)(2,1)}) %reduce-scatter.5.cloned.1.call-update) | async-done | bytes 786448 | tf_op jit(solution)/shard_map/reduce_scatter | solution.py:117
  104.3 9.0 %collective-permute-done.2 = bf16[2,255,256]{1,2,0:T(8,128)(2,1)} collective-permute-done((bf16[2,255,256]{1,2,0:T(8,128)(2,1)}, bf16[2,255,256]{1,2,0:T(8,128)(2,1)}, u32[]{:S(2)}, u32[]{:S(2)}) %collective-permute-start.2) | collective-permute-done | bytes 261152 | tf_op jit(solution)/shard_map/ppermute | solution.py:21
  115.7 4.6 fusion.52
  123.6 21.5 %all-gather.9.cloned.1.call-done = bf16[4,512,256]{2,1,0:T(8,128)(2,1)} async-done(((bf16[1,512,256]{2,1,0:T(8,128)(2,1)}), bf16[4,512,256]{2,1,0:T(8,128)(2,1)}) %all-gather.9.cloned.1.call-update) | async-done | bytes 1048592 | tf_op jit(solution)/shard_map/all_gather | solution.py:122
  145.1 4.2 bitcast_convert_fusion.1
  151.6 22.9 %reduce-scatter.7.cloned.1.call-done = bf16[128,1024]{1,0:T(8,128)(2,1)} async-done(((bf16[512,1024]{1,0:T(8,128)(2,1)}), bf16[128,1024]{1,0:T(8,128)(2,1)}) %reduce-scatter.7.cloned.1.call-update) | async-done | bytes 262160 | tf_op jit(solution)/shard_map/reduce_scatter | solution.py:125
  179.5 4.3 collective-permute-done.4
  185.2 5.7 %psum.15 = f32[192]{0:T(256)S(1)} all-reduce(f32[192]{0:T(256)S(1)} %get-tuple-element.18), channel_id=1, replica_groups=mesh['req'=8,'row'=4,'col'=4] {'row'}, use_global_device_ids=true, to_apply=%region_9.10 | all-reduce | flops 192 | bytes 1536 | tf_op jit(solution)/shard_map/psum | solution.py:39
  203.6 6.5 %pad_maximum_fusion.1 = bf16[1024,4,3,256]{0,3,2,1:T(8,128)(2,1)} fusion(bf16[1024,4,1,256]{0,3,2,1:T(8,128)(2,1)} %bitcast.72, bf16[1024,4,1,256]{0,3,2,1:T(8,128)(2,1)} %bitcast.73, bf16[1024,4,1,256]{0,3,2,1:T(8,128)(2,1)} %bitcast.74), kind=kLoop, calls=%fused_computation.5 | loop fusion | flops 6291456 | bytes 12582912 | tf_op jit(solution)/shard_map/stack | solution.py:112
  210.2 12.4 %all-gather.11.cloned.1.call-done = bf16[768,1024]{1,0:T(8,128)(2,1)} async-done(((bf16[192,1024]{1,0:T(8,128)(2,1)}), bf16[768,1024]{1,0:T(8,128)(2,1)}) %all-gather.11.cloned.1.call-update) | async-done | bytes 1572880 | tf_op jit(solution)/shard_map/all_gather | solution.py:45
  222.5 9.1 %convolution_convert_fusion = bf16[4,768,768]{1,2,0:T(8,128)(2,1)} fusion(bf16[1024,4,768]{0,2,1:T(8,128)(2,1)} %bitcast.76, bf16[768,1024]{1,0:T(8,128)(2,1)} %all-gather.11.cloned.1.call-done), kind=kOutput, calls=%fused_computation.10 | convolution fusion | flops 4834197504 | bytes 12582912 | tf_op jit(solution)/shard_map/tf,frc->rtc/dot_general | solution.py:115
  231.7 49.3 %reduce-scatter.9.cloned.1.call-done.q_ref = bf16[768,768]{1,0:T(8,128)(2,1)} async-done(((bf16[3072,768]{1,0:T(8,128)(2,1)}), bf16[768,768]{1,0:T(8,128)(2,1)}) %reduce-scatter.9.cloned.1.call-update) | async-done | bytes 1179664 | tf_op jit(solution)/shard_map/reduce_scatter | solution.py:117
  283.2 86.1 %all-gather.13.cloned.1.call-done.k_ref.v_ref = bf16[6144,512]{1,0:T(8,128)(2,1)} async-done(((bf16[768,512]{1,0:T(8,128)(2,1)}), bf16[6144,512]{1,0:T(8,128)(2,1)}) %all-gather.13.cloned.1.call-update) | async-done | bytes 6291472 | tf_op jit(solution)/shard_map/all_gather | solution.py:278
  369.4 49.9 %shard_map.136 = bf16[768,256]{1,0:T(8,128)(2,1)} custom-call(s32[1]{0:T(128)} %bitcast.25.base_ref, bf16[768,768]{1,0:T(8,128)(2,1)} %reduce-scatter.9.cloned.1.call-done.q_ref, bf16[6144,512]{1,0:T(8,128)(2,1)} %all-gather.13.cloned.1.call-done.k_ref.v_ref, bf16[6144,512]{1,0:T(8,128)(2,1)} %all-gather.13.cloned.1.call-done.k_ref.v_ref), custom_call_target="tpu_custom_call" | custom-call | tf_op jit(solution)/shard_map/pallas_call | solution.py:197
  419.3 26.1 %all-gather.15.cloned.1.call-done = bf16[3072,256]{1,0:T(8,128)(2,1)} async-done(((bf16[768,256]{1,0:T(8,128)(2,1)}), bf16[3072,256]{1,0:T(8,128)(2,1)}) %all-gather.15.cloned.1.call-update) | async-done | bytes 1572880 | tf_op jit(solution)/shard_map/all_gather | solution.py:122
  445.5 4.4 bitcast_convert_fusion
  449.8 27.3 %reduce-scatter.11.cloned.1.call-done = bf16[192,1024]{1,0:T(8,128)(2,1)} async-done(((bf16[768,1024]{1,0:T(8,128)(2,1)}), bf16[192,1024]{1,0:T(8,128)(2,1)}) %reduce-scatter.11.cloned.1.call-update) | async-done | bytes 393232 | tf_op jit(solution)/shard_map/reduce_scatter | solution.py:125
  (86 shorter events, 62.3 us)
Async XLA Ops:
  6.5 438.9 %copy-start = (bf16[1024,1024]{1,0:T(8,128)(2,1)S(1)}, bf16[1024,1024]{1,0:T(8,128)(2,1)}, u32[]{:S(2)}) copy-start(bf16[1024,1024]{1,0:T(8,128)(2,1)} %param.27) | copy-start | bytes 6291460
  6.5 36.7 %all-gather.7.cloned.1.call-start = ((), (), s32[]{:S(2)}) async-start(), calls=%async_computation.4 | async-start | bytes 1310720 | tf_op jit(solution)/shard_map/all_gather | solution.py:45
  16.9 76.4 %reduce-scatter.5.cloned.1.call-start = ((), (), s32[]{:S(2)}) async-start(), calls=%async_computation.5 | async-start | bytes 3932160 | tf_op jit(solution)/shard_map/reduce_scatter | solution.py:117
  56.2 0.7 copy-start.3
  56.2 0.7 copy-start.4
  56.3 88.8 %all-gather.9.cloned.1.call-start = ((), (), s32[]{:S(2)}) async-start(), calls=%async_computation.6 | async-start | bytes 1310720 | tf_op jit(solution)/shard_map/all_gather | solution.py:122
  65.6 3.8 collective-permute-start.1
  68.0 7.0 %collective-permute-start = (s32[2,255]{1,0:T(2,128)S(1)}, s32[2,255]{1,0:T(2,128)S(1)}, u32[]{:S(2)}, u32[]{:S(2)}) collective-permute-start(s32[2,255]{1,0:T(2,128)S(1)} %get-tuple-element.14), channel_id=1, source_target_pairs={{0,16},{16,32},{32,48},{48,64},{64,80},{80,96},{96,112},{1,17},{17... | collective-permute-start | bytes 6128 | tf_op jit(solution)/shard_map/ppermute | solution.py:21
  95.4 8.9 %collective-permute-start.3 = (bf16[2,255,256]{1,2,0:T(8,128)(2,1)}, bf16[2,255,256]{1,2,0:T(8,128)(2,1)}, u32[]{:S(2)}, u32[]{:S(2)}) collective-permute-start(bf16[2,255,256]{1,2,0:T(8,128)(2,1)} %get-tuple-element.11), channel_id=1, source_target_pairs={{16,0},{32,16},{48,32},{64,48},{80,64},{96,80},{112,96},{17,1},{33... | collective-permute-start | bytes 783368 | tf_op jit(solution)/shard_map/ppermute | solution.py:23
  98.8 14.5 %collective-permute-start.2 = (bf16[2,255,256]{1,2,0:T(8,128)(2,1)}, bf16[2,255,256]{1,2,0:T(8,128)(2,1)}, u32[]{:S(2)}, u32[]{:S(2)}) collective-permute-start(bf16[2,255,256]{1,2,0:T(8,128)(2,1)} %get-tuple-element.10), channel_id=1, source_target_pairs={{0,16},{16,32},{32,48},{48,64},{64,80},{80,96},{96,112},{1,17},{17... | collective-permute-start | bytes 783368 | tf_op jit(solution)/shard_map/ppermute | solution.py:21
  123.6 50.9 %reduce-scatter.7.cloned.1.call-start = ((), (), s32[]{:S(2)}) async-start(), calls=%async_computation.7 | async-start | bytes 1310720 | tf_op jit(solution)/shard_map/reduce_scatter | solution.py:125
  145.1 4.3 copy-start.2
  149.3 25.2 %copy-start.1 = (bf16[128,1024]{1,0:T(8,128)(2,1)S(1)}, bf16[128,1024]{1,0:T(8,128)(2,1)}, u32[]{:S(2)}) copy-start(bf16[128,1024]{1,0:T(8,128)(2,1)} %param.15) | copy-start | bytes 786436
  149.3 73.2 %all-gather.11.cloned.1.call-start = ((), (), s32[]{:S(2)}) async-start(), calls=%async_computation.8 | async-start | bytes 1966080 | tf_op jit(solution)/shard_map/all_gather | solution.py:45
  175.5 8.3 %collective-permute-start.4 = (bf16[128,1024]{1,0:T(8,128)(2,1)S(1)}, bf16[128,1024]{1,0:T(8,128)(2,1)S(1)}, u32[]{:S(2)}, u32[]{:S(2)}) collective-permute-start(bf16[128,1024]{1,0:T(8,128)(2,1)S(1)} %fusion.23), channel_id=1, source_target_pairs={{1,0},{2,1},{3,2},{16,3},{17,16},{18,17},{19,18},{32,19},{33,32},{... | collective-permute-start | bytes 786440 | tf_op jit(solution)/shard_map/ppermute | solution.py:33
  191.7 89.3 %reduce-scatter.9.cloned.1.call-start = ((), (), s32[]{:S(2)}) async-start(), calls=%async_computation.9 | async-start | bytes 5898240 | tf_op jit(solution)/shard_map/reduce_scatter | solution.py:117
  231.7 137.7 %all-gather.13.cloned.1.call-start = ((), (), s32[]{:S(2)}) async-start(), calls=%async_computation.10 | async-start | bytes 7077888 | tf_op jit(solution)/shard_map/all_gather | solution.py:278
  283.2 162.3 %all-gather.15.cloned.1.call-start = ((), (), s32[]{:S(2)}) async-start(), calls=%async_computation.12 | async-start | bytes 1966080 | tf_op jit(solution)/shard_map/all_gather | solution.py:122
  419.3 57.9 %reduce-scatter.11.cloned.1.call-start = ((), (), s32[]{:S(2)}) async-start(), calls=%async_computation.11 | async-start | bytes 1966080 | tf_op jit(solution)/shard_map/reduce_scatter | solution.py:125
Sparse Core Ops, SparseCore 0:
  17.0 26.2 all-gather.6
  56.4 36.8 reduce-scatter.4
  123.7 21.3 all-gather.8
  149.4 25.0 reduce-scatter.6
  191.9 30.6 all-gather.10
  231.8 49.2 reduce-scatter.8
  283.6 85.6 all-gather.12
  419.4 26.0 all-gather.14
  450.0 27.1 reduce-scatter.10

commit v4 on v3

--- a/solution.py
+++ b/solution.py
@@ -107,13 +107,26 @@
 
 def head_project(values, weights):
     row_count = lax.axis_size("row")
-    width = weights[0].shape[1]
-    depth = weights[0].shape[0]
-    shaped = jnp.stack(
-        [w.reshape(depth, row_count, width // row_count) for w in weights], axis=2
-    ).reshape(depth, row_count, len(weights) * (width // row_count))
-    summed = jnp.einsum("tf,frc->rtc", values, shaped, preferred_element_type=jnp.float32)
-    summed = summed.astype(jnp.bfloat16).reshape(row_count * values.shape[0], -1)
+    count, depth = values.shape
+    part = weights[0].shape[1] // row_count
+    groups = len(weights)
+
+    def body(x_ref, *refs):
+        o_ref = refs[-1]
+        for g in range(groups):
+            o_ref[0, :, g * part : (g + 1) * part] = jnp.dot(
+                x_ref[...], refs[g][...], preferred_element_type=jnp.float32
+            ).astype(o_ref.dtype)
+
+    summed = pl.pallas_call(
+        body,
+        grid=(row_count,),
+        in_specs=[pl.BlockSpec((count, depth), lambda r: (0, 0))]
+        + [pl.BlockSpec((depth, part), lambda r: (0, r)) for _ in weights],
+        out_specs=pl.BlockSpec((1, count, groups * part), lambda r: (r, 0, 0)),
+        out_shape=jax.ShapeDtypeStruct((row_count, count, groups * part), jnp.bfloat16),
+    )(values, *weights)
+    summed = summed.reshape(row_count * count, groups * part)
     return lax.psum_scatter(summed, "row", scatter_dimension=0, tiled=True)
 
 

time: 487 us -> 487 us (level)
  waiting for transfers between devices: 292 us -> 322 us
  local copies, waits for them, and re-layouts: 39.3 us -> 15.5 us
  matrix products: 34.3 us -> 17 us
  Pallas kernels: 49.9 us -> 66.9 us
  other arithmetic: 24.3 us -> 11.3 us
  starting transfers between devices: 11.4 us -> 18.3 us
    all_gather x2, waiting for transfers between devices: 20.4 us -> 57 us  [gather_cols(): return lax.all_gather(values, 'col', axis=0, tiled=True)]
    unnamed x16 -> x10, local copies, waits for them, and re-layouts: 24.3 us -> 0.61 us
    dot_general x2 -> x0, matrix products: 17.3 us -> none  [head_project(): jnp.einsum('tf,frc->rtc', values, shaped, preferred_element_type=jnp.floa...]
    pallas_call x0 -> x2, Pallas kernels: none -> 17 us  [head_project(): pl.pallas_call(body, grid=(row_count,), in_specs=[pl.BlockSpec((count, de...]
    another operation x4 -> x2, other arithmetic: 13.4 us -> 0.31 us  [the longest x2 13 us: head_project(): jnp.stack([w.reshape(depth, row_count, width // row_count) for w in weigh...]
    ppermute x2, waiting for transfers between devices: 14.7 us -> 1.8 us  [with_halo(): lax.ppermute(tail, axis, [(i, (i + 1) % count) for i in range(ends)])]
    ppermute x2, starting transfers between devices: 5.94 us -> 12.8 us  [with_halo(): lax.ppermute(head, axis, [((i + 1) % count, i) for i in range(ends)])]
    all_gather x2, waiting for transfers between devices: 47.6 us -> 52.9 us  [out_project_heads(): whole = lax.all_gather(attended, 'row', axis=0, tiled=False)]
  transfers between devices with their start and end apart: 14 -> 14, of which waited for: 13 -> 13; matrix products, arithmetic and copies ran while one was open for 9% -> 1% of each run, Pallas kernels for 0% -> 0%
where the time goes in v4:
time: 487 us; the launch traced here: 486 us
  waiting for transfers between devices  322 us (66%)
  Pallas kernels  66.9 us (14%)
  blocking collectives  20.8 us (4%)
  starting transfers between devices  18.3 us (4%)
  matrix products  17 us (3%)
  local copies, waits for them, and re-layouts  15.5 us (3%)
  between operations  13.4 us (3%)
  other arithmetic  11.3 us (2%)
    all_gather x1, waiting for transfers between devices, per_device(): piece = lax.all_gather(dec_proj[:, local:], 'req', axis=0, tiled=True)  86 us
    reduce_scatter x2, waiting for transfers between devices, head_project(): return lax.psum_scatter(summed, 'row', scatter_dimension=0, tiled=True)  68.4 us
    all_gather x2, waiting for transfers between devices, gather_cols(): return lax.all_gather(values, 'col', axis=0, tiled=True)  57 us
    all_gather x2, waiting for transfers between devices, out_project_heads(): whole = lax.all_gather(attended, 'row', axis=0, tiled=False)  52.9 us
    reduce_scatter x2, waiting for transfers between devices, out_project_heads(): lax.psum_scatter(summed.astype(jnp.bfloat16), 'col', scatter_dimension=0,...  50.2 us
    pallas_call x1, Pallas kernels, causal_attend(): pl.pallas_call(body, grid_spec=grid_spec, out_shape=jax.ShapeDtypeStruct(...  49.9 us
    pallas_call x2, Pallas kernels, head_project(): pl.pallas_call(body, grid=(row_count,), in_specs=[pl.BlockSpec((count, de...  17 us
    ppermute x2, starting transfers between devices, with_halo(): lax.ppermute(head, axis, [((i + 1) % count, i) for i in range(ends)])  12.8 us
  transfers between devices with their start and end apart: 14, of which 13 were waited for; matrix products, arithmetic and copies ran while one was open for 1% of the time, Pallas kernels for 0%

profile of v4, /device:TPU:28, one launch (start us, length us, event | category | flops | bytes accessed | tf_op | source)
XLA Modules:
  0.0 485.6 jit_solution(8564168939127471551)
XLA Ops:
  7.8 6.6 %psum.14 = f32[128]{0:T(128)S(1)} all-reduce(f32[128]{0:T(128)S(1)} %fusion.18), channel_id=1, replica_groups=mesh['req'=8,'row'=4,'col'=4] {'row'}, use_global_device_ids=true, to_apply=%region_3.4 | all-reduce | flops 128 | bytes 1024 | tf_op jit(solution)/shard_map/psum | solution.py:39
  16.9 26.4 %all-gather.7.cloned.1.call-done.x_ref = bf16[512,1024]{1,0:T(8,128)(2,1)} async-done(((bf16[128,1024]{1,0:T(8,128)(2,1)}), bf16[512,1024]{1,0:T(8,128)(2,1)}) %all-gather.7.cloned.1.call-update) | async-done | bytes 1048592 | tf_op jit(solution)/shard_map/all_gather | solution.py:45
  43.3 7.7 %shard_map.136 = bf16[4,512,768]{2,1,0:T(8,128)(2,1)} custom-call(bf16[512,1024]{1,0:T(8,128)(2,1)} %all-gather.7.cloned.1.call-done.x_ref, bf16[1024,1024]{1,0:T(8,128)(2,1)} %refs_0_.2, bf16[1024,1024]{1,0:T(8,128)(2,1)} %refs_1_.2, bf16[1024,1024]{1,0:T(8,128)(2,1)} %refs_2_.2), custom_call_target="tpu_custom_call" | custom-call | tf_op jit(solution)/shard_map/pallas_call | solution.py:121
  51.0 4.7 copy.21
  56.4 8.6 %all_gather.22 = s32[2,512]{1,0:T(2,128)S(1)} all-gather(s32[2,128]{1,0:T(2,128)S(1)} %pad_add_fusion.1), channel_id=1, replica_groups=mesh['req'=8,'row'=4,'col'=4] {'col'}, dimensions={1}, use_global_device_ids=true | all-gather | bytes 5120 | tf_op jit(solution)/shard_map/all_gather | solution.py:238
  66.3 6.1 %collective-permute-start.1 = (s32[2,255]{1,0:T(2,128)S(1)}, s32[2,255]{1,0:T(2,128)S(1)}, u32[]{:S(2)}, u32[]{:S(2)}) collective-permute-start(s32[2,255]{1,0:T(2,128)S(1)} %get-tuple-element.15), channel_id=1, source_target_pairs={{16,0},{32,16},{48,32},{64,48},{80,64},{96,80},{112,96},{17,1},{33... | collective-permute-start | bytes 6128 | tf_op jit(solution)/shard_map/ppermute | solution.py:23
  73.8 19.0 %reduce-scatter.5.cloned.1.call-done = bf16[512,768]{0,1:T(8,128)(2,1)} async-done(((bf16[2048,768]{0,1:T(8,128)(2,1)}), bf16[512,768]{0,1:T(8,128)(2,1)}) %reduce-scatter.5.cloned.1.call-update) | async-done | bytes 786448 | tf_op jit(solution)/shard_map/reduce_scatter | solution.py:130
  96.1 6.8 %collective-permute-start.3 = (bf16[2,255,256]{1,2,0:T(8,128)(2,1)}, bf16[2,255,256]{1,2,0:T(8,128)(2,1)}, u32[]{:S(2)}, u32[]{:S(2)}) collective-permute-start(bf16[2,255,256]{1,2,0:T(8,128)(2,1)} %get-tuple-element.11), channel_id=1, source_target_pairs={{16,0},{32,16},{48,32},{64,48},{80,64},{96,80},{112,96},{17,1},{33... | collective-permute-start | bytes 783368 | tf_op jit(solution)/shard_map/ppermute | solution.py:23
  110.4 4.6 fusion.50
  115.0 2.4 fusion.15
  118.4 26.8 %all-gather.9.cloned.1.call-done = bf16[4,512,256]{2,1,0:T(8,128)(2,1)} async-done(((bf16[1,512,256]{2,1,0:T(8,128)(2,1)}), bf16[4,512,256]{2,1,0:T(8,128)(2,1)}) %all-gather.9.cloned.1.call-update) | async-done | bytes 1048592 | tf_op jit(solution)/shard_map/all_gather | solution.py:135
  145.2 4.2 bitcast_convert_fusion.1
  151.7 22.9 %reduce-scatter.7.cloned.1.call-done = bf16[128,1024]{1,0:T(8,128)(2,1)} async-done(((bf16[512,1024]{1,0:T(8,128)(2,1)}), bf16[128,1024]{1,0:T(8,128)(2,1)}) %reduce-scatter.7.cloned.1.call-update) | async-done | bytes 262160 | tf_op jit(solution)/shard_map/reduce_scatter | solution.py:138
  175.6 2.4 collective-permute-start.4
  179.4 4.5 collective-permute-done.4
  185.2 5.7 %psum.15 = f32[192]{0:T(256)S(1)} all-reduce(f32[192]{0:T(256)S(1)} %get-tuple-element.18), channel_id=1, replica_groups=mesh['req'=8,'row'=4,'col'=4] {'row'}, use_global_device_ids=true, to_apply=%region_9.10 | all-reduce | flops 192 | bytes 1536 | tf_op jit(solution)/shard_map/psum | solution.py:39
  191.9 30.6 %all-gather.11.cloned.1.call-done.x_ref = bf16[768,1024]{1,0:T(8,128)(2,1)} async-done(((bf16[192,1024]{1,0:T(8,128)(2,1)}), bf16[768,1024]{1,0:T(8,128)(2,1)}) %all-gather.11.cloned.1.call-update) | async-done | bytes 1572880 | tf_op jit(solution)/shard_map/all_gather | solution.py:45
  222.5 9.3 %shard_map.137 = bf16[4,768,768]{2,1,0:T(8,128)(2,1)} custom-call(bf16[768,1024]{1,0:T(8,128)(2,1)} %all-gather.11.cloned.1.call-done.x_ref, bf16[1024,1024]{1,0:T(8,128)(2,1)} %refs_0_.3, bf16[1024,1024]{1,0:T(8,128)(2,1)} %refs_1_.3, bf16[1024,1024]{1,0:T(8,128)(2,1)} %refs_2_.3), custom_call_target="tpu_custom_call" | custom-call | tf_op jit(solution)/shard_map/pallas_call | solution.py:121
  231.9 49.3 %reduce-scatter.9.cloned.1.call-done.q_ref = bf16[768,768]{1,0:T(8,128)(2,1)} async-done(((bf16[3072,768]{1,0:T(8,128)(2,1)}), bf16[768,768]{1,0:T(8,128)(2,1)}) %reduce-scatter.9.cloned.1.call-update) | async-done | bytes 1179664 | tf_op jit(solution)/shard_map/reduce_scatter | solution.py:130
  283.5 86.0 %all-gather.13.cloned.1.call-done.k_ref.v_ref = bf16[6144,512]{1,0:T(8,128)(2,1)} async-done(((bf16[768,512]{1,0:T(8,128)(2,1)}), bf16[6144,512]{1,0:T(8,128)(2,1)}) %all-gather.13.cloned.1.call-update) | async-done | bytes 6291472 | tf_op jit(solution)/shard_map/all_gather | solution.py:291
  369.5 49.9 %shard_map.138 = bf16[768,256]{1,0:T(8,128)(2,1)} custom-call(s32[1]{0:T(128)} %bitcast.19.base_ref, bf16[768,768]{1,0:T(8,128)(2,1)} %reduce-scatter.9.cloned.1.call-done.q_ref, bf16[6144,512]{1,0:T(8,128)(2,1)} %all-gather.13.cloned.1.call-done.k_ref.v_ref, bf16[6144,512]{1,0:T(8,128)(2,1)} %all-gather.13.cloned.1.call-done.k_ref.v_ref), custom_call_target="tpu_custom_call" | custom-call | tf_op jit(solution)/shard_map/pallas_call | solution.py:210
  419.5 26.1 %all-gather.15.cloned.1.call-done = bf16[3072,256]{1,0:T(8,128)(2,1)} async-done(((bf16[768,256]{1,0:T(8,128)(2,1)}), bf16[3072,256]{1,0:T(8,128)(2,1)}) %all-gather.15.cloned.1.call-update) | async-done | bytes 1572880 | tf_op jit(solution)/shard_map/all_gather | solution.py:135
  445.6 4.4 bitcast_convert_fusion
  450.0 27.3 %reduce-scatter.11.cloned.1.call-done = bf16[192,1024]{1,0:T(8,128)(2,1)} async-done(((bf16[768,1024]{1,0:T(8,128)(2,1)}), bf16[192,1024]{1,0:T(8,128)(2,1)}) %reduce-scatter.11.cloned.1.call-update) | async-done | bytes 393232 | tf_op jit(solution)/shard_map/reduce_scatter | solution.py:138
  (78 shorter events, 30.1 us)
Async XLA Ops:
  6.5 439.1 %copy-start = (bf16[1024,1024]{1,0:T(8,128)(2,1)S(1)}, bf16[1024,1024]{1,0:T(8,128)(2,1)}, u32[]{:S(2)}) copy-start(bf16[1024,1024]{1,0:T(8,128)(2,1)} %param.27) | copy-start | bytes 6291460
  6.5 36.7 %all-gather.7.cloned.1.call-start = ((), (), s32[]{:S(2)}) async-start(), calls=%async_computation.4 | async-start | bytes 1310720 | tf_op jit(solution)/shard_map/all_gather | solution.py:45
  16.9 75.9 %reduce-scatter.5.cloned.1.call-start = ((), (), s32[]{:S(2)}) async-start(), calls=%async_computation.5 | async-start | bytes 3932160 | tf_op jit(solution)/shard_map/reduce_scatter | solution.py:130
  55.7 0.7 copy-start.3
  55.7 0.7 copy-start.4
  55.7 89.4 %all-gather.9.cloned.1.call-start = ((), (), s32[]{:S(2)}) async-start(), calls=%async_computation.6 | async-start | bytes 1310720 | tf_op jit(solution)/shard_map/all_gather | solution.py:135
  65.0 7.4 %collective-permute-start = (s32[2,255]{1,0:T(2,128)S(1)}, s32[2,255]{1,0:T(2,128)S(1)}, u32[]{:S(2)}, u32[]{:S(2)}) collective-permute-start(s32[2,255]{1,0:T(2,128)S(1)} %get-tuple-element.14), channel_id=1, source_target_pairs={{0,16},{16,32},{32,48},{48,64},{64,80},{80,96},{96,112},{1,17},{17... | collective-permute-start | bytes 6128 | tf_op jit(solution)/shard_map/ppermute | solution.py:21
  66.3 7.3 %collective-permute-start.1 = (s32[2,255]{1,0:T(2,128)S(1)}, s32[2,255]{1,0:T(2,128)S(1)}, u32[]{:S(2)}, u32[]{:S(2)}) collective-permute-start(s32[2,255]{1,0:T(2,128)S(1)} %get-tuple-element.15), channel_id=1, source_target_pairs={{16,0},{32,16},{48,32},{64,48},{80,64},{96,80},{112,96},{17,1},{33... | collective-permute-start | bytes 6128 | tf_op jit(solution)/shard_map/ppermute | solution.py:23
  94.8 12.9 %collective-permute-start.2 = (bf16[2,255,256]{1,2,0:T(8,128)(2,1)}, bf16[2,255,256]{1,2,0:T(8,128)(2,1)}, u32[]{:S(2)}, u32[]{:S(2)}) collective-permute-start(bf16[2,255,256]{1,2,0:T(8,128)(2,1)} %get-tuple-element.10), channel_id=1, source_target_pairs={{0,16},{16,32},{32,48},{48,64},{64,80},{80,96},{96,112},{1,17},{17... | collective-permute-start | bytes 783368 | tf_op jit(solution)/shard_map/ppermute | solution.py:21
  96.1 11.9 %collective-permute-start.3 = (bf16[2,255,256]{1,2,0:T(8,128)(2,1)}, bf16[2,255,256]{1,2,0:T(8,128)(2,1)}, u32[]{:S(2)}, u32[]{:S(2)}) collective-permute-start(bf16[2,255,256]{1,2,0:T(8,128)(2,1)} %get-tuple-element.11), channel_id=1, source_target_pairs={{16,0},{32,16},{48,32},{64,48},{80,64},{96,80},{112,96},{17,1},{33... | collective-permute-start | bytes 783368 | tf_op jit(solution)/shard_map/ppermute | solution.py:23
  118.3 56.2 %reduce-scatter.7.cloned.1.call-start = ((), (), s32[]{:S(2)}) async-start(), calls=%async_computation.7 | async-start | bytes 1310720 | tf_op jit(solution)/shard_map/reduce_scatter | solution.py:138
  145.2 4.3 copy-start.2
  149.4 25.2 %copy-start.1 = (bf16[128,1024]{1,0:T(8,128)(2,1)S(1)}, bf16[128,1024]{1,0:T(8,128)(2,1)}, u32[]{:S(2)}) copy-start(bf16[128,1024]{1,0:T(8,128)(2,1)} %param.15) | copy-start | bytes 786436
  149.4 73.1 %all-gather.11.cloned.1.call-start = ((), (), s32[]{:S(2)}) async-start(), calls=%async_computation.8 | async-start | bytes 1966080 | tf_op jit(solution)/shard_map/all_gather | solution.py:45
  175.6 8.3 %collective-permute-start.4 = (bf16[128,1024]{1,0:T(8,128)(2,1)S(1)}, bf16[128,1024]{1,0:T(8,128)(2,1)S(1)}, u32[]{:S(2)}, u32[]{:S(2)}) collective-permute-start(bf16[128,1024]{1,0:T(8,128)(2,1)S(1)} %fusion.21), channel_id=1, source_target_pairs={{1,0},{2,1},{3,2},{16,3},{17,16},{18,17},{19,18},{32,19},{33,32},{... | collective-permute-start | bytes 786440 | tf_op jit(solution)/shard_map/ppermute | solution.py:33
  191.8 89.4 %reduce-scatter.9.cloned.1.call-start = ((), (), s32[]{:S(2)}) async-start(), calls=%async_computation.9 | async-start | bytes 5898240 | tf_op jit(solution)/shard_map/reduce_scatter | solution.py:130
  231.8 137.7 %all-gather.13.cloned.1.call-start = ((), (), s32[]{:S(2)}) async-start(), calls=%async_computation.10 | async-start | bytes 7077888 | tf_op jit(solution)/shard_map/all_gather | solution.py:291
  283.3 162.3 %all-gather.15.cloned.1.call-start = ((), (), s32[]{:S(2)}) async-start(), calls=%async_computation.12 | async-start | bytes 1966080 | tf_op jit(solution)/shard_map/all_gather | solution.py:135
  419.4 57.9 %reduce-scatter.11.cloned.1.call-start = ((), (), s32[]{:S(2)}) async-start(), calls=%async_computation.11 | async-start | bytes 1966080 | tf_op jit(solution)/shard_map/reduce_scatter | solution.py:138
Sparse Core Ops, SparseCore 0:
  17.0 26.2 all-gather.6
  55.9 36.8 reduce-scatter.4
  118.4 26.6 all-gather.8
  149.5 25.0 reduce-scatter.6
  191.9 30.4 all-gather.10
  232.0 49.2 reduce-scatter.8
  283.8 85.6 all-gather.12
  419.5 26.0 all-gather.14
  450.1 27.1 reduce-scatter.10

commit v5 on v4

--- a/solution.py
+++ b/solution.py
@@ -41,8 +41,35 @@
     return (floats * factor[:, None] * gain.astype(jnp.float32)[None, :]).astype(jnp.bfloat16)
 
 
+def gather_permute(values, axis):
+    count = lax.axis_size(axis)
+    index = lax.axis_index(axis)
+    rows = values.shape[0]
+    got = [values] + [
+        lax.ppermute(values, axis, [(j, (j + s) % count) for j in range(count)])
+        for s in range(1, count)
+    ]
+    ahead = jnp.concatenate([got[0]] + got[:0:-1], axis=0)
+    twice = jnp.concatenate([ahead, ahead], axis=0)
+    start = ((count - index) % count) * rows
+    return lax.dynamic_slice_in_dim(twice, start, count * rows, axis=0)
+
+
+def scatter_permute(values, axis):
+    count = lax.axis_size(axis)
+    index = lax.axis_index(axis)
+    rows = values.shape[0] // count
+    total = lax.dynamic_slice_in_dim(values, index * rows, rows, axis=0).astype(jnp.float32)
+    for s in range(1, count):
+        chunk = lax.dynamic_slice_in_dim(values, ((index + s) % count) * rows, rows, axis=0)
+        total = total + lax.ppermute(
+            chunk, axis, [(j, (j + s) % count) for j in range(count)]
+        ).astype(jnp.float32)
+    return total
+
+
 def gather_cols(values):
-    return lax.all_gather(values, "col", axis=0, tiled=True)
+    return gather_permute(values, "col")
 
 
 def out_project(attended, weight):
@@ -135,9 +162,7 @@
     whole = lax.all_gather(attended, "row", axis=0, tiled=False)
     shaped = weight.reshape(row_count, weight.shape[0] // row_count, weight.shape[1])
     summed = jnp.einsum("rtf,rfo->to", whole, shaped, preferred_element_type=jnp.float32)
-    return lax.psum_scatter(
-        summed.astype(jnp.bfloat16), "col", scatter_dimension=0, tiled=True
-    ).astype(jnp.float32)
+    return scatter_permute(summed.astype(jnp.bfloat16), "col")
 
 
 def causal_attend(proj, keyvals, base, key_tile=512):

time: 487 us -> 483 us (level)
  waiting for transfers between devices: 322 us -> 274 us
  local copies, waits for them, and re-layouts: 15.5 us -> 39.1 us
  starting transfers between devices: 18.3 us -> 38 us
    all_gather x2 -> x0, waiting for transfers between devices: 57 us -> none  [gather_cols(): return lax.all_gather(values, 'col', axis=0, tiled=True)]
    ppermute x0 -> x12, waiting for transfers between devices: none -> 54.1 us  [the longest x6 27.4 us: scatter_permute(): lax.ppermute(chunk, axis, [(j, (j + s) % count) for j in range(count)])]
    reduce_scatter x2 -> x0, waiting for transfers between devices: 50.2 us -> none  [out_project_heads(): lax.psum_scatter(summed.astype(jnp.bfloat16), 'col', scatter_dimension=0,...]
    ppermute x0 -> x12, starting transfers between devices: none -> 18.5 us  [the longest x6 10.3 us: scatter_permute(): lax.ppermute(chunk, axis, [(j, (j + s) % count) for j in range(count)])]
    unnamed x10 -> x24, local copies, waits for them, and re-layouts: 0.61 us -> 14.7 us
    dynamic_slice x0 -> x4, local copies, waits for them, and re-layouts: none -> 6.85 us  [the longest x2 4.98 us: gather_permute(): return lax.dynamic_slice_in_dim(twice, start, count * rows, axis=0)]
    reduce_scatter x2, waiting for transfers between devices: 68.4 us -> 73.8 us  [head_project(): return lax.psum_scatter(summed, 'row', scatter_dimension=0, tiled=True)]
  transfers between devices with their start and end apart: 14 -> 22, of which waited for: 13 -> 20; matrix products, arithmetic and copies ran while one was open for 1% -> 2% of each run, Pallas kernels for 0% -> 0%
where the time goes in v5:
time: 483 us; the launch traced here: 480 us
  waiting for transfers between devices  274 us (57%)
  Pallas kernels  66.9 us (14%)
  local copies, waits for them, and re-layouts  39.1 us (8%)
  starting transfers between devices  38 us (8%)
  blocking collectives  20.9 us (4%)
  matrix products  14.9 us (3%)
  between operations  13.5 us (3%)
  other arithmetic  13 us (3%)
    all_gather x1, waiting for transfers between devices, per_device(): piece = lax.all_gather(dec_proj[:, local:], 'req', axis=0, tiled=True)  85.8 us
    reduce_scatter x2, waiting for transfers between devices, head_project(): return lax.psum_scatter(summed, 'row', scatter_dimension=0, tiled=True)  73.8 us
    all_gather x2, waiting for transfers between devices, out_project_heads(): whole = lax.all_gather(attended, 'row', axis=0, tiled=False)  52.1 us
    pallas_call x1, Pallas kernels, causal_attend(): pl.pallas_call(body, grid_spec=grid_spec, out_shape=jax.ShapeDtypeStruct(...  49.9 us
    ppermute x6, waiting for transfers between devices, scatter_permute(): lax.ppermute(chunk, axis, [(j, (j + s) % count) for j in range(count)])  27.4 us
    ppermute x6, waiting for transfers between devices, gather_permute(): lax.ppermute(values, axis, [(j, (j + s) % count) for j in range(count)])  26.7 us
    pallas_call x2, Pallas kernels, head_project(): pl.pallas_call(body, grid=(row_count,), in_specs=[pl.BlockSpec((count, de...  17.1 us
    unnamed x24, local copies, waits for them, and re-layouts  14.7 us
  transfers between devices with their start and end apart: 22, of which 20 were waited for; matrix products, arithmetic and copies ran while one was open for 2% of the time, Pallas kernels for 0%

profile of v5, /device:TPU:28, one launch (start us, length us, event | category | flops | bytes accessed | tf_op | source)
XLA Modules:
  0.0 480.1 jit_solution(13213720919022021026)
XLA Ops:
  7.8 6.6 %psum.14 = f32[128]{0:T(128)S(1)} all-reduce(f32[128]{0:T(128)S(1)} %fusion.18), channel_id=1, replica_groups=mesh['req'=8,'row'=4,'col'=4] {'row'}, use_global_device_ids=true, to_apply=%region_3.4 | all-reduce | flops 128 | bytes 1024 | tf_op jit(solution)/shard_map/psum | solution.py:39
  16.9 4.0 collective-permute-start.2
  22.2 9.0 %collective-permute-done.2 = bf16[128,1024]{1,0:T(8,128)(2,1)S(1)} collective-permute-done((bf16[128,1024]{1,0:T(8,128)(2,1)S(1)}, bf16[128,1024]{1,0:T(8,128)(2,1)S(1)}, u32[]{:S(2)}, u32[]{:S(2)}) %collective-permute-start.2) | collective-permute-done | bytes 262176 | tf_op jit(solution)/shard_map/ppermute | solution.py:49
  40.5 7.7 %shard_map.136 = bf16[4,512,768]{2,1,0:T(8,128)(2,1)} custom-call(bf16[512,1024]{1,0:T(8,128)(2,1)} %constant_dynamic-slice_fusion.7.x_ref, bf16[1024,1024]{1,0:T(8,128)(2,1)} %refs_0_.2, bf16[1024,1024]{1,0:T(8,128)(2,1)} %refs_1_.2, bf16[1024,1024]{1,0:T(8,128)(2,1)} %refs_2_.2), custom_call_target="tpu_custom_call" | custom-call | tf_op jit(solution)/shard_map/pallas_call | solution.py:148
  48.2 4.8 copy.21
  53.7 8.7 %all_gather.16 = s32[2,512]{1,0:T(2,128)S(1)} all-gather(s32[2,128]{1,0:T(2,128)S(1)} %pad_add_fusion.1), channel_id=1, replica_groups=mesh['req'=8,'row'=4,'col'=4] {'col'}, dimensions={1}, use_global_device_ids=true | all-gather | bytes 5120 | tf_op jit(solution)/shard_map/all_gather | solution.py:263
  63.7 6.1 %collective-permute-start.1 = (s32[2,255]{1,0:T(2,128)S(1)}, s32[2,255]{1,0:T(2,128)S(1)}, u32[]{:S(2)}, u32[]{:S(2)}) collective-permute-start(s32[2,255]{1,0:T(2,128)S(1)} %get-tuple-element.25), channel_id=1, source_target_pairs={{16,0},{32,16},{48,32},{64,48},{80,64},{96,80},{112,96},{17,1},{33... | collective-permute-start | bytes 6128 | tf_op jit(solution)/shard_map/ppermute | solution.py:23
  71.1 18.3 %reduce-scatter.3.cloned.1.call-done = bf16[512,768]{0,1:T(8,128)(2,1)} async-done(((bf16[2048,768]{0,1:T(8,128)(2,1)}), bf16[512,768]{0,1:T(8,128)(2,1)}) %reduce-scatter.3.cloned.1.call-update) | async-done | bytes 786448 | tf_op jit(solution)/shard_map/reduce_scatter | solution.py:157
  92.7 6.8 %collective-permute-start.6 = (bf16[2,255,256]{1,2,0:T(8,128)(2,1)}, bf16[2,255,256]{1,2,0:T(8,128)(2,1)}, u32[]{:S(2)}, u32[]{:S(2)}) collective-permute-start(bf16[2,255,256]{1,2,0:T(8,128)(2,1)} %get-tuple-element.21), channel_id=1, source_target_pairs={{16,0},{32,16},{48,32},{64,48},{80,64},{96,80},{112,96},{17,1},{33... | collective-permute-start | bytes 783368 | tf_op jit(solution)/shard_map/ppermute | solution.py:23
  107.1 4.6 fusion.51
  115.8 26.0 %all-gather.5.cloned.1.call-done = bf16[4,512,256]{2,1,0:T(8,128)(2,1)} async-done(((bf16[1,512,256]{2,1,0:T(8,128)(2,1)}), bf16[4,512,256]{2,1,0:T(8,128)(2,1)}) %all-gather.5.cloned.1.call-update) | async-done | bytes 1048592 | tf_op jit(solution)/shard_map/all_gather | solution.py:162
  156.9 5.7 %collective-permute-done.8 = bf16[128,1024]{1,0:T(8,128)(2,1)} collective-permute-done((bf16[128,1024]{1,0:T(8,128)(2,1)}, bf16[128,1024]{1,0:T(8,128)(2,1)}, u32[]{:S(2)}, u32[]{:S(2)}) %collective-permute-start.8) | collective-permute-done | bytes 262176 | tf_op jit(solution)/shard_map/ppermute | solution.py:65
  164.7 4.0 collective-permute-start.10
  170.1 4.4 collective-permute-done.10
  175.9 5.7 %psum.15 = f32[192]{0:T(256)S(1)} all-reduce(f32[192]{0:T(256)S(1)} %get-tuple-element.28), channel_id=1, replica_groups=mesh['req'=8,'row'=4,'col'=4] {'row'}, use_global_device_ids=true, to_apply=%region_8.9 | all-reduce | flops 192 | bytes 1536 | tf_op jit(solution)/shard_map/psum | solution.py:39
  185.5 9.3 %collective-permute-done.11 = bf16[192,1024]{1,0:T(8,128)(2,1)S(1)} collective-permute-done((bf16[192,1024]{1,0:T(8,128)(2,1)}, bf16[192,1024]{1,0:T(8,128)(2,1)S(1)}, u32[]{:S(2)}, u32[]{:S(2)}) %collective-permute-start.11) | collective-permute-done | bytes 393248 | tf_op jit(solution)/shard_map/ppermute | solution.py:49
  198.3 5.5 %collective-permute-done.13 = bf16[192,1024]{1,0:T(8,128)(2,1)} collective-permute-done((bf16[192,1024]{1,0:T(8,128)(2,1)}, bf16[192,1024]{1,0:T(8,128)(2,1)}, u32[]{:S(2)}, u32[]{:S(2)}) %collective-permute-start.13) | collective-permute-done | bytes 393248 | tf_op jit(solution)/shard_map/ppermute | solution.py:49
  214.4 9.4 %shard_map.137 = bf16[4,768,768]{2,1,0:T(8,128)(2,1)} custom-call(bf16[768,1024]{1,0:T(8,128)(2,1)} %constant_dynamic-slice_fusion.3.x_ref, bf16[1024,1024]{1,0:T(8,128)(2,1)} %refs_0_.3, bf16[1024,1024]{1,0:T(8,128)(2,1)} %refs_1_.3, bf16[1024,1024]{1,0:T(8,128)(2,1)} %refs_2_.3), custom_call_target="tpu_custom_call" | custom-call | tf_op jit(solution)/shard_map/pallas_call | solution.py:148
  223.8 55.5 %reduce-scatter.5.cloned.1.call-done.q_ref = bf16[768,768]{1,0:T(8,128)(2,1)} async-done(((bf16[3072,768]{1,0:T(8,128)(2,1)}), bf16[768,768]{1,0:T(8,128)(2,1)}) %reduce-scatter.5.cloned.1.call-update) | async-done | bytes 1179664 | tf_op jit(solution)/shard_map/reduce_scatter | solution.py:157
  281.5 85.8 %all-gather.7.cloned.1.call-done.k_ref.v_ref = bf16[6144,512]{1,0:T(8,128)(2,1)} async-done(((bf16[768,512]{1,0:T(8,128)(2,1)}), bf16[6144,512]{1,0:T(8,128)(2,1)}) %all-gather.7.cloned.1.call-update) | async-done | bytes 6291472 | tf_op jit(solution)/shard_map/all_gather | solution.py:316
  367.3 49.9 %shard_map.138 = bf16[768,256]{1,0:T(8,128)(2,1)} custom-call(s32[1]{0:T(128)} %bitcast.19.base_ref, bf16[768,768]{1,0:T(8,128)(2,1)} %reduce-scatter.5.cloned.1.call-done.q_ref, bf16[6144,512]{1,0:T(8,128)(2,1)} %all-gather.7.cloned.1.call-done.k_ref.v_ref, bf16[6144,512]{1,0:T(8,128)(2,1)} %all-gather.7.cloned.1.call-done.k_ref.v_ref), custom_call_target="tpu_custom_call" | custom-call | tf_op jit(solution)/shard_map/pallas_call | solution.py:235
  417.2 26.2 %all-gather.9.cloned.1.call-done = bf16[3072,256]{1,0:T(8,128)(2,1)} async-done(((bf16[768,256]{1,0:T(8,128)(2,1)}), bf16[3072,256]{1,0:T(8,128)(2,1)}) %all-gather.9.cloned.1.call-update) | async-done | bytes 1572880 | tf_op jit(solution)/shard_map/all_gather | solution.py:162
  453.9 7.7 %collective-permute-done.14 = bf16[192,1024]{1,0:T(8,128)(2,1)} collective-permute-done((bf16[192,1024]{1,0:T(8,128)(2,1)}, bf16[192,1024]{1,0:T(8,128)(2,1)}, u32[]{:S(2)}, u32[]{:S(2)}) %collective-permute-start.14) | collective-permute-done | bytes 393248 | tf_op jit(solution)/shard_map/ppermute | solution.py:65
  462.6 8.6 %collective-permute-done.15 = bf16[192,1024]{1,0:T(8,128)(2,1)} collective-permute-done((bf16[192,1024]{1,0:T(8,128)(2,1)S(1)}, bf16[192,1024]{1,0:T(8,128)(2,1)}, u32[]{:S(2)}, u32[]{:S(2)}) %collective-permute-start.15) | collective-permute-done | bytes 393248 | tf_op jit(solution)/shard_map/ppermute | solution.py:65
  (110 shorter events, 86.5 us)
Async XLA Ops:
  6.5 436.8 %copy-start = (bf16[1024,1024]{1,0:T(8,128)(2,1)S(1)}, bf16[1024,1024]{1,0:T(8,128)(2,1)}, u32[]{:S(2)}) copy-start(bf16[1024,1024]{1,0:T(8,128)(2,1)} %param.27) | copy-start | bytes 6291460
  6.5 82.9 %reduce-scatter.3.cloned.1.call-start = ((), (), s32[]{:S(2)}) async-start(), calls=%async_computation.2 | async-start | bytes 3932160 | tf_op jit(solution)/shard_map/reduce_scatter | solution.py:157
  16.9 14.3 %collective-permute-start.2 = (bf16[128,1024]{1,0:T(8,128)(2,1)S(1)}, bf16[128,1024]{1,0:T(8,128)(2,1)S(1)}, u32[]{:S(2)}, u32[]{:S(2)}) collective-permute-start(bf16[128,1024]{1,0:T(8,128)(2,1)S(1)} %get-tuple-element.8), channel_id=1, source_target_pairs={{0,3},{1,0},{2,1},{3,2},{4,7},{5,4},{6,5},{7,6},{8,11},{9,8},{10,9... | collective-permute-start | bytes 786440 | tf_op jit(solution)/shard_map/ppermute | solution.py:49
  20.9 11.0 %collective-permute-start.3 = (bf16[128,1024]{1,0:T(8,128)(2,1)S(1)}, bf16[128,1024]{1,0:T(8,128)(2,1)S(1)}, u32[]{:S(2)}, u32[]{:S(2)}) collective-permute-start(bf16[128,1024]{1,0:T(8,128)(2,1)S(1)} %get-tuple-element.8), channel_id=1, source_target_pairs={{0,2},{1,3},{2,0},{3,1},{4,6},{5,7},{6,4},{7,5},{8,10},{9,11},{10,... | collective-permute-start | bytes 786440 | tf_op jit(solution)/shard_map/ppermute | solution.py:49
  20.9 13.7 %collective-permute-start.4 = (bf16[128,1024]{1,0:T(8,128)(2,1)S(1)}, bf16[128,1024]{1,0:T(8,128)(2,1)S(1)}, u32[]{:S(2)}, u32[]{:S(2)}) collective-permute-start(bf16[128,1024]{1,0:T(8,128)(2,1)S(1)} %get-tuple-element.8), channel_id=1, source_target_pairs={{0,1},{1,2},{2,3},{3,0},{4,5},{5,6},{6,7},{7,4},{8,9},{9,10},{10,1... | collective-permute-start | bytes 786440 | tf_op jit(solution)/shard_map/ppermute | solution.py:49
  53.0 88.8 %all-gather.5.cloned.1.call-start = ((), (), s32[]{:S(2)}) async-start(), calls=%async_computation.3 | async-start | bytes 1310720 | tf_op jit(solution)/shard_map/all_gather | solution.py:162
  62.4 7.4 %collective-permute-start = (s32[2,255]{1,0:T(2,128)S(1)}, s32[2,255]{1,0:T(2,128)S(1)}, u32[]{:S(2)}, u32[]{:S(2)}) collective-permute-start(s32[2,255]{1,0:T(2,128)S(1)} %get-tuple-element.24), channel_id=1, source_target_pairs={{0,16},{16,32},{32,48},{48,64},{64,80},{80,96},{96,112},{1,17},{17... | collective-permute-start | bytes 6128 | tf_op jit(solution)/shard_map/ppermute | solution.py:21
  63.7 7.3 %collective-permute-start.1 = (s32[2,255]{1,0:T(2,128)S(1)}, s32[2,255]{1,0:T(2,128)S(1)}, u32[]{:S(2)}, u32[]{:S(2)}) collective-permute-start(s32[2,255]{1,0:T(2,128)S(1)} %get-tuple-element.25), channel_id=1, source_target_pairs={{16,0},{32,16},{48,32},{64,48},{80,64},{96,80},{112,96},{17,1},{33... | collective-permute-start | bytes 6128 | tf_op jit(solution)/shard_map/ppermute | solution.py:23
  91.5 12.9 %collective-permute-start.5 = (bf16[2,255,256]{1,2,0:T(8,128)(2,1)}, bf16[2,255,256]{1,2,0:T(8,128)(2,1)}, u32[]{:S(2)}, u32[]{:S(2)}) collective-permute-start(bf16[2,255,256]{1,2,0:T(8,128)(2,1)} %get-tuple-element.20), channel_id=1, source_target_pairs={{0,16},{16,32},{32,48},{48,64},{64,80},{80,96},{96,112},{1,17},{17... | collective-permute-start | bytes 783368 | tf_op jit(solution)/shard_map/ppermute | solution.py:21
  92.7 11.9 %collective-permute-start.6 = (bf16[2,255,256]{1,2,0:T(8,128)(2,1)}, bf16[2,255,256]{1,2,0:T(8,128)(2,1)}, u32[]{:S(2)}, u32[]{:S(2)}) collective-permute-start(bf16[2,255,256]{1,2,0:T(8,128)(2,1)} %get-tuple-element.21), channel_id=1, source_target_pairs={{16,0},{32,16},{48,32},{64,48},{80,64},{96,80},{112,96},{17,1},{33... | collective-permute-start | bytes 783368 | tf_op jit(solution)/shard_map/ppermute | solution.py:23
  115.0 164.3 %reduce-scatter.5.cloned.1.call-start = ((), (), s32[]{:S(2)}) async-start(), calls=%async_computation.4 | async-start | bytes 5898240 | tf_op jit(solution)/shard_map/reduce_scatter | solution.py:157
  145.0 17.7 %copy-start.1 = (bf16[128,1024]{1,0:T(8,128)(2,1)S(1)}, bf16[128,1024]{1,0:T(8,128)(2,1)}, u32[]{:S(2)}) copy-start(bf16[128,1024]{1,0:T(8,128)(2,1)} %param.15) | copy-start | bytes 786436
  145.9 10.0 %collective-permute-start.7 = (bf16[128,1024]{1,0:T(8,128)(2,1)}, bf16[128,1024]{1,0:T(8,128)(2,1)}, u32[]{:S(2)}, u32[]{:S(2)}) collective-permute-start(bf16[128,1024]{1,0:T(8,128)(2,1)} %get-tuple-element.12), channel_id=1, source_target_pairs={{0,1},{1,2},{2,3},{3,0},{4,5},{5,6},{6,7},{7,4},{8,9},{9,10},{10,1... | collective-permute-start | bytes 786440 | tf_op jit(solution)/shard_map/ppermute | solution.py:65
  147.4 9.5 %collective-permute-start.9 = (bf16[128,1024]{1,0:T(8,128)(2,1)}, bf16[128,1024]{1,0:T(8,128)(2,1)}, u32[]{:S(2)}, u32[]{:S(2)}) collective-permute-start(bf16[128,1024]{1,0:T(8,128)(2,1)} %get-tuple-element.13), channel_id=1, source_target_pairs={{0,3},{1,0},{2,1},{3,2},{4,7},{5,4},{6,5},{7,6},{8,11},{9,8},{10,9... | collective-permute-start | bytes 786440 | tf_op jit(solution)/shard_map/ppermute | solution.py:65
  149.1 13.5 %collective-permute-start.8 = (bf16[128,1024]{1,0:T(8,128)(2,1)}, bf16[128,1024]{1,0:T(8,128)(2,1)}, u32[]{:S(2)}, u32[]{:S(2)}) collective-permute-start(bf16[128,1024]{1,0:T(8,128)(2,1)} %get-tuple-element.14), channel_id=1, source_target_pairs={{0,2},{1,3},{2,0},{3,1},{4,6},{5,7},{6,4},{7,5},{8,10},{9,11},{10,... | collective-permute-start | bytes 786440 | tf_op jit(solution)/shard_map/ppermute | solution.py:65
  164.7 9.7 %collective-permute-start.10 = (bf16[128,1024]{1,0:T(8,128)(2,1)}, bf16[128,1024]{1,0:T(8,128)(2,1)S(1)}, u32[]{:S(2)}, u32[]{:S(2)}) collective-permute-start(bf16[128,1024]{1,0:T(8,128)(2,1)} %fusion.21), channel_id=1, source_target_pairs={{1,0},{2,1},{3,2},{16,3},{17,16},{18,17},{19,18},{32,19},{33,32},{... | collective-permute-start | bytes 786440 | tf_op jit(solution)/shard_map/ppermute | solution.py:33
  182.6 12.2 %collective-permute-start.11 = (bf16[192,1024]{1,0:T(8,128)(2,1)}, bf16[192,1024]{1,0:T(8,128)(2,1)S(1)}, u32[]{:S(2)}, u32[]{:S(2)}) collective-permute-start(bf16[192,1024]{1,0:T(8,128)(2,1)} %get-tuple-element.6), channel_id=1, source_target_pairs={{0,3},{1,0},{2,1},{3,2},{4,7},{5,4},{6,5},{7,6},{8,11},{9,8},{10,9... | collective-permute-start | bytes 1179656 | tf_op jit(solution)/shard_map/ppermute | solution.py:49
  182.6 13.9 %collective-permute-start.12 = (bf16[192,1024]{1,0:T(8,128)(2,1)}, bf16[192,1024]{1,0:T(8,128)(2,1)}, u32[]{:S(2)}, u32[]{:S(2)}) collective-permute-start(bf16[192,1024]{1,0:T(8,128)(2,1)} %get-tuple-element.6), channel_id=1, source_target_pairs={{0,2},{1,3},{2,0},{3,1},{4,6},{5,7},{6,4},{7,5},{8,10},{9,11},{10,... | collective-permute-start | bytes 1179656 | tf_op jit(solution)/shard_map/ppermute | solution.py:49
  185.5 18.2 %collective-permute-start.13 = (bf16[192,1024]{1,0:T(8,128)(2,1)}, bf16[192,1024]{1,0:T(8,128)(2,1)}, u32[]{:S(2)}, u32[]{:S(2)}) collective-permute-start(bf16[192,1024]{1,0:T(8,128)(2,1)} %get-tuple-element.6), channel_id=1, source_target_pairs={{0,1},{1,2},{2,3},{3,0},{4,5},{5,6},{6,7},{7,4},{8,9},{9,10},{10,1... | collective-permute-start | bytes 1179656 | tf_op jit(solution)/shard_map/ppermute | solution.py:49
  223.8 143.6 %all-gather.7.cloned.1.call-start = ((), (), s32[]{:S(2)}) async-start(), calls=%async_computation.5 | async-start | bytes 7077888 | tf_op jit(solution)/shard_map/all_gather | solution.py:316
  281.4 162.0 %all-gather.9.cloned.1.call-start = ((), (), s32[]{:S(2)}) async-start(), calls=%async_computation.6 | async-start | bytes 1966080 | tf_op jit(solution)/shard_map/all_gather | solution.py:162
  448.7 12.9 %collective-permute-start.14 = (bf16[192,1024]{1,0:T(8,128)(2,1)}, bf16[192,1024]{1,0:T(8,128)(2,1)}, u32[]{:S(2)}, u32[]{:S(2)}) collective-permute-start(bf16[192,1024]{1,0:T(8,128)(2,1)} %get-tuple-element.9), channel_id=1, source_target_pairs={{0,1},{1,2},{2,3},{3,0},{4,5},{5,6},{6,7},{7,4},{8,9},{9,10},{10,1... | collective-permute-start | bytes 1179656 | tf_op jit(solution)/shard_map/ppermute | solution.py:65
  450.3 12.3 %collective-permute-start.16 = (bf16[192,1024]{1,0:T(8,128)(2,1)}, bf16[192,1024]{1,0:T(8,128)(2,1)}, u32[]{:S(2)}, u32[]{:S(2)}) collective-permute-start(bf16[192,1024]{1,0:T(8,128)(2,1)} %get-tuple-element.10), channel_id=1, source_target_pairs={{0,3},{1,0},{2,1},{3,2},{4,7},{5,4},{6,5},{7,6},{8,11},{9,8},{10,9... | collective-permute-start | bytes 1179656 | tf_op jit(solution)/shard_map/ppermute | solution.py:65
  451.9 19.2 %collective-permute-start.15 = (bf16[192,1024]{1,0:T(8,128)(2,1)S(1)}, bf16[192,1024]{1,0:T(8,128)(2,1)}, u32[]{:S(2)}, u32[]{:S(2)}) collective-permute-start(bf16[192,1024]{1,0:T(8,128)(2,1)S(1)} %get-tuple-element.11), channel_id=1, source_target_pairs={{0,2},{1,3},{2,0},{3,1},{4,6},{5,7},{6,4},{7,5},{8,10},{9,11},{10,... | collective-permute-start | bytes 1179656 | tf_op jit(solution)/shard_map/ppermute | solution.py:65
  (4 other events, 5.9 us)
Sparse Core Ops, SparseCore 0:
  53.1 36.2 reduce-scatter.2
  115.1 26.6 all-gather.4
  223.9 55.3 reduce-scatter.4
  281.5 85.7 all-gather.6
  417.3 26.0 all-gather.8

commit v6 on v5

--- a/solution.py
+++ b/solution.py
@@ -132,6 +132,36 @@
     )
 
 
+def flip(values, axis, bit):
+    count = lax.axis_size(axis)
+    return lax.ppermute(values, axis, [(j, j ^ bit) for j in range(count)])
+
+
+def scatter_row(values):
+    count = lax.axis_size("row")
+    index = lax.axis_index("row")
+    rows = values.shape[0] // count
+    chunks = values.reshape(count // 2, 2, rows, values.shape[1])
+    mine = lax.dynamic_index_in_dim(chunks, index % 2, axis=1, keepdims=False)
+    theirs = lax.dynamic_index_in_dim(chunks, 1 - index % 2, axis=1, keepdims=False)
+    paired = (mine.astype(jnp.float32) + flip(theirs, "row", 1).astype(jnp.float32))
+    paired = paired.astype(jnp.bfloat16)
+    keep = lax.dynamic_index_in_dim(paired, index // 2, axis=0, keepdims=False)
+    send = lax.dynamic_index_in_dim(paired, 1 - index // 2, axis=0, keepdims=False)
+    return (keep.astype(jnp.float32) + flip(send, "row", 2).astype(jnp.float32)).astype(
+        jnp.bfloat16
+    )
+
+
+def gather_row(values):
+    count = lax.axis_size("row")
+    index = lax.axis_index("row")
+    got = [values] + [flip(values, "row", b) for b in range(1, count)]
+    stacked = jnp.stack(got)
+    order = jnp.arange(count, dtype=jnp.int32) ^ index
+    return jnp.take(stacked, order, axis=0)
+
+
 def head_project(values, weights):
     row_count = lax.axis_size("row")
     count, depth = values.shape
@@ -154,12 +184,12 @@
         out_shape=jax.ShapeDtypeStruct((row_count, count, groups * part), jnp.bfloat16),
     )(values, *weights)
     summed = summed.reshape(row_count * count, groups * part)
-    return lax.psum_scatter(summed, "row", scatter_dimension=0, tiled=True)
+    return scatter_row(summed)
 
 
 def out_project_heads(attended, weight):
     row_count = lax.axis_size("row")
-    whole = lax.all_gather(attended, "row", axis=0, tiled=False)
+    whole = gather_row(attended)
     shaped = weight.reshape(row_count, weight.shape[0] // row_count, weight.shape[1])
     summed = jnp.einsum("rtf,rfo->to", whole, shaped, preferred_element_type=jnp.float32)
     return scatter_permute(summed.astype(jnp.bfloat16), "col")

time: 483 us -> 463 us (0.959)
  waiting for transfers between devices: 274 us -> 229 us
  local copies, waits for them, and re-layouts: 39.1 us -> 49.8 us
  other arithmetic: 13 us -> 21.1 us
  starting transfers between devices: 38 us -> 45.4 us
    ppermute x0 -> x10, waiting for transfers between devices: none -> 74.4 us  [flip(): return lax.ppermute(values, axis, [(j, j ^ bit) for j in range(count)])]
    reduce_scatter x2 -> x0, waiting for transfers between devices: 73.8 us -> none  [head_project(): return lax.psum_scatter(summed, 'row', scatter_dimension=0, tiled=True)]
    all_gather x2 -> x0, waiting for transfers between devices: 52.1 us -> none  [out_project_heads(): whole = lax.all_gather(attended, 'row', axis=0, tiled=False)]
    all_gather x1, waiting for transfers between devices: 85.8 us -> 93.2 us  [per_device(): piece = lax.all_gather(dec_proj[:, local:], 'req', axis=0, tiled=True)]
    ppermute x0 -> x10, starting transfers between devices: none -> 7.15 us  [flip(): return lax.ppermute(values, axis, [(j, j ^ bit) for j in range(count)])]
    dynamic_slice x0 -> x2, local copies, waits for them, and re-layouts: none -> 6.4 us  [the longest x1 3.76 us: scatter_row(): mine = lax.dynamic_index_in_dim(chunks, index % 2, axis=1, keepdims=False)]
    unnamed x24 -> x39, local copies, waits for them, and re-layouts: 14.7 us -> 18.6 us
  transfers between devices with their start and end apart: 22 -> 28, of which waited for: 20 -> 19; matrix products, arithmetic and copies ran while one was open for 2% -> 4% of each run, Pallas kernels for 0% -> 0%
where the time goes in v6:
time: 463 us; the launch traced here: 461 us
  waiting for transfers between devices  229 us (49%)
  Pallas kernels  66.9 us (14%)
  local copies, waits for them, and re-layouts  49.8 us (11%)
  starting transfers between devices  45.4 us (10%)
  other arithmetic  21.1 us (5%)
  blocking collectives  20.9 us (5%)
  matrix products  14 us (3%)
  between operations  13.9 us (3%)
    all_gather x1, waiting for transfers between devices, per_device(): piece = lax.all_gather(dec_proj[:, local:], 'req', axis=0, tiled=True)  93.2 us
    ppermute x10, waiting for transfers between devices, flip(): return lax.ppermute(values, axis, [(j, j ^ bit) for j in range(count)])  74.4 us
    pallas_call x1, Pallas kernels, causal_attend(): pl.pallas_call(body, grid_spec=grid_spec, out_shape=jax.ShapeDtypeStruct(...  49.9 us
    ppermute x6, waiting for transfers between devices, scatter_permute(): lax.ppermute(chunk, axis, [(j, (j + s) % count) for j in range(count)])  28 us
    ppermute x6, waiting for transfers between devices, gather_permute(): lax.ppermute(values, axis, [(j, (j + s) % count) for j in range(count)])  27.6 us
    unnamed x39, local copies, waits for them, and re-layouts  18.6 us
    pallas_call x2, Pallas kernels, head_project(): pl.pallas_call(body, grid=(row_count,), in_specs=[pl.BlockSpec((count, de...  17.1 us
    ppermute x2, starting transfers between devices, with_halo(): lax.ppermute(head, axis, [((i + 1) % count, i) for i in range(ends)])  12.8 us
  transfers between devices with their start and end apart: 28, of which 19 were waited for; matrix products, arithmetic and copies ran while one was open for 4% of the time, Pallas kernels for 0%

profile of v6, /device:TPU:28, one launch (start us, length us, event | category | flops | bytes accessed | tf_op | source)
XLA Modules:
  0.0 461.3 jit_solution(7922014647482468614)
XLA Ops:
  7.8 6.6 %psum.14 = f32[128]{0:T(128)S(1)} all-reduce(f32[128]{0:T(128)S(1)} %fusion.27), channel_id=1, replica_groups=mesh['req'=8,'row'=4,'col'=4] {'row'}, use_global_device_ids=true, to_apply=%region_3.4 | all-reduce | flops 128 | bytes 1024 | tf_op jit(solution)/shard_map/psum | solution.py:39
  16.8 4.0 collective-permute-start.2
  22.1 9.0 %collective-permute-done.2 = bf16[128,1024]{1,0:T(8,128)(2,1)S(1)} collective-permute-done((bf16[128,1024]{1,0:T(8,128)(2,1)S(1)}, bf16[128,1024]{1,0:T(8,128)(2,1)S(1)}, u32[]{:S(2)}, u32[]{:S(2)}) %collective-permute-start.2) | collective-permute-done | bytes 262176 | tf_op jit(solution)/shard_map/ppermute | solution.py:49
  40.4 7.7 %shard_map.136 = bf16[4,512,768]{2,1,0:T(8,128)(2,1)} custom-call(bf16[512,1024]{1,0:T(8,128)(2,1)} %constant_dynamic-slice_fusion.9.x_ref, bf16[1024,1024]{1,0:T(8,128)(2,1)} %refs_0_.2, bf16[1024,1024]{1,0:T(8,128)(2,1)} %refs_1_.2, bf16[1024,1024]{1,0:T(8,128)(2,1)} %refs_2_.2), custom_call_target="tpu_custom_call" | custom-call | tf_op jit(solution)/shard_map/pallas_call | solution.py:178
  54.6 8.7 %all_gather.6 = s32[2,512]{1,0:T(2,128)S(1)} all-gather(s32[2,128]{1,0:T(2,128)S(1)} %pad_add_fusion.1), channel_id=1, replica_groups=mesh['req'=8,'row'=4,'col'=4] {'col'}, dimensions={1}, use_global_device_ids=true | all-gather | bytes 5120 | tf_op jit(solution)/shard_map/all_gather | solution.py:293
  64.6 6.1 %collective-permute-start.1 = (s32[2,255]{1,0:T(2,128)S(1)}, s32[2,255]{1,0:T(2,128)S(1)}, u32[]{:S(2)}, u32[]{:S(2)}) collective-permute-start(s32[2,255]{1,0:T(2,128)S(1)} %get-tuple-element.27), channel_id=1, source_target_pairs={{16,0},{32,16},{48,32},{64,48},{80,64},{96,80},{112,96},{17,1},{33... | collective-permute-start | bytes 6128 | tf_op jit(solution)/shard_map/ppermute | solution.py:23
  79.4 16.0 %collective-permute-done.6 = bf16[512,768]{0,1:T(8,128)(2,1)S(1)} collective-permute-done((bf16[512,768]{0,1:T(8,128)(2,1)}, bf16[512,768]{0,1:T(8,128)(2,1)S(1)}, u32[]{:S(2)}, u32[]{:S(2)}) %collective-permute-start.6) | collective-permute-done | bytes 786464 | tf_op jit(solution)/shard_map/ppermute | solution.py:137
  99.0 6.8 %collective-permute-start.8 = (bf16[2,255,256]{1,2,0:T(8,128)(2,1)}, bf16[2,255,256]{1,2,0:T(8,128)(2,1)}, u32[]{:S(2)}, u32[]{:S(2)}) collective-permute-start(bf16[2,255,256]{1,2,0:T(8,128)(2,1)} %get-tuple-element.23), channel_id=1, source_target_pairs={{16,0},{32,16},{48,32},{64,48},{80,64},{96,80},{112,96},{17,1},{33... | collective-permute-start | bytes 783368 | tf_op jit(solution)/shard_map/ppermute | solution.py:23
  121.9 6.0 %collective-permute-done.11 = bf16[512,256]{1,0:T(8,128)(2,1)S(1)} collective-permute-done((bf16[512,256]{1,0:T(8,128)(2,1)S(1)}, bf16[512,256]{1,0:T(8,128)(2,1)S(1)}, u32[]{:S(2)}, u32[]{:S(2)}) %collective-permute-start.11) | collective-permute-done | bytes 262176 | tf_op jit(solution)/shard_map/ppermute | solution.py:137
  143.8 11.5 %collective-permute-done.12 = bf16[128,1024]{1,0:T(8,128)(2,1)} collective-permute-done((bf16[128,1024]{1,0:T(8,128)(2,1)}, bf16[128,1024]{1,0:T(8,128)(2,1)}, u32[]{:S(2)}, u32[]{:S(2)}) %collective-permute-start.12) | collective-permute-done | bytes 262176 | tf_op jit(solution)/shard_map/ppermute | solution.py:65
  157.4 7.2 %collective-permute-start.15 = (bf16[128,1024]{1,0:T(8,128)(2,1)}, bf16[128,1024]{1,0:T(8,128)(2,1)S(1)}, u32[]{:S(2)}, u32[]{:S(2)}) collective-permute-start(bf16[128,1024]{1,0:T(8,128)(2,1)} %fusion.30), channel_id=1, source_target_pairs={{1,0},{2,1},{3,2},{16,3},{17,16},{18,17},{19,18},{32,19},{33,32},{... | collective-permute-start | bytes 786440 | tf_op jit(solution)/shard_map/ppermute | solution.py:33
  166.0 4.2 collective-permute-done.15
  171.6 5.7 %psum.15 = f32[192]{0:T(256)S(1)} all-reduce(f32[192]{0:T(256)S(1)} %get-tuple-element.30), channel_id=1, replica_groups=mesh['req'=8,'row'=4,'col'=4] {'row'}, use_global_device_ids=true, to_apply=%region_7.8 | all-reduce | flops 192 | bytes 1536 | tf_op jit(solution)/shard_map/psum | solution.py:39
  180.4 10.2 %collective-permute-done.16 = bf16[192,1024]{1,0:T(8,128)(2,1)S(1)} collective-permute-done((bf16[192,1024]{1,0:T(8,128)(2,1)}, bf16[192,1024]{1,0:T(8,128)(2,1)S(1)}, u32[]{:S(2)}, u32[]{:S(2)}) %collective-permute-start.16) | collective-permute-done | bytes 393248 | tf_op jit(solution)/shard_map/ppermute | solution.py:49
  194.0 5.6 %collective-permute-done.18 = bf16[192,1024]{1,0:T(8,128)(2,1)} collective-permute-done((bf16[192,1024]{1,0:T(8,128)(2,1)}, bf16[192,1024]{1,0:T(8,128)(2,1)}, u32[]{:S(2)}, u32[]{:S(2)}) %collective-permute-start.18) | collective-permute-done | bytes 393248 | tf_op jit(solution)/shard_map/ppermute | solution.py:49
  210.1 9.3 %shard_map.137 = bf16[4,768,768]{2,1,0:T(8,128)(2,1)} custom-call(bf16[768,1024]{1,0:T(8,128)(2,1)} %constant_dynamic-slice_fusion.3.x_ref, bf16[1024,1024]{1,0:T(8,128)(2,1)} %refs_0_.3, bf16[1024,1024]{1,0:T(8,128)(2,1)} %refs_1_.3, bf16[1024,1024]{1,0:T(8,128)(2,1)} %refs_2_.3), custom_call_target="tpu_custom_call" | custom-call | tf_op jit(solution)/shard_map/pallas_call | solution.py:178
  221.6 4.5 collective-permute-done.19
  228.4 26.4 %collective-permute-done.20 = bf16[768,768]{1,0:T(8,128)(2,1)S(1)} collective-permute-done((bf16[768,768]{1,0:T(8,128)(2,1)S(1)}, bf16[768,768]{1,0:T(8,128)(2,1)S(1)}, u32[]{:S(2)}, u32[]{:S(2)}) %collective-permute-start.20) | collective-permute-done | bytes 1179680 | tf_op jit(solution)/shard_map/ppermute | solution.py:137
  256.3 93.2 %all-gather.2.cloned.1.call-done.k_ref.v_ref = bf16[6144,512]{1,0:T(8,128)(2,1)} async-done(((bf16[768,512]{1,0:T(8,128)(2,1)}), bf16[6144,512]{1,0:T(8,128)(2,1)}) %all-gather.2.cloned.1.call-update) | async-done | bytes 6291472 | tf_op jit(solution)/shard_map/all_gather | solution.py:346
  349.5 49.9 %shard_map.138 = bf16[768,256]{1,0:T(8,128)(2,1)} custom-call(s32[1]{0:T(128)} %bitcast.28.base_ref, bf16[768,768]{1,0:T(8,128)(2,1)} %copy-done.2, bf16[6144,512]{1,0:T(8,128)(2,1)} %all-gather.2.cloned.1.call-done.k_ref.v_ref, bf16[6144,512]{1,0:T(8,128)(2,1)} %all-gather.2.cloned.1.call-done.k_ref.v_ref), custom_call_target="tpu_custom_call" | custom-call | tf_op jit(solution)/shard_map/pallas_call | solution.py:265
  401.6 8.9 %collective-permute-done.23 = bf16[768,256]{1,0:T(8,128)(2,1)S(1)} collective-permute-done((bf16[768,256]{1,0:T(8,128)(2,1)}, bf16[768,256]{1,0:T(8,128)(2,1)S(1)}, u32[]{:S(2)}, u32[]{:S(2)}) %collective-permute-start.23) | collective-permute-done | bytes 393248 | tf_op jit(solution)/shard_map/ppermute | solution.py:137
  410.5 9.0 %collective-permute-done.22 = bf16[768,256]{1,0:T(8,128)(2,1)S(1)} collective-permute-done((bf16[768,256]{1,0:T(8,128)(2,1)}, bf16[768,256]{1,0:T(8,128)(2,1)S(1)}, u32[]{:S(2)}, u32[]{:S(2)}) %collective-permute-start.22) | collective-permute-done | bytes 393248 | tf_op jit(solution)/shard_map/ppermute | solution.py:137
  435.5 7.2 %collective-permute-done.24 = bf16[192,1024]{1,0:T(8,128)(2,1)} collective-permute-done((bf16[192,1024]{1,0:T(8,128)(2,1)}, bf16[192,1024]{1,0:T(8,128)(2,1)}, u32[]{:S(2)}, u32[]{:S(2)}) %collective-permute-start.24) | collective-permute-done | bytes 393248 | tf_op jit(solution)/shard_map/ppermute | solution.py:65
  444.3 7.8 %collective-permute-done.25 = bf16[192,1024]{1,0:T(8,128)(2,1)} collective-permute-done((bf16[192,1024]{1,0:T(8,128)(2,1)S(1)}, bf16[192,1024]{1,0:T(8,128)(2,1)}, u32[]{:S(2)}, u32[]{:S(2)}) %collective-permute-start.25) | collective-permute-done | bytes 393248 | tf_op jit(solution)/shard_map/ppermute | solution.py:65
  (149 shorter events, 116.1 us)
Async XLA Ops:
  6.5 343.0 %all-gather.2.cloned.1.call-start = ((), (), s32[]{:S(2)}) async-start(), calls=%async_computation | async-start | bytes 7077888 | tf_op jit(solution)/shard_map/all_gather | solution.py:346
  16.8 14.3 %collective-permute-start.2 = (bf16[128,1024]{1,0:T(8,128)(2,1)S(1)}, bf16[128,1024]{1,0:T(8,128)(2,1)S(1)}, u32[]{:S(2)}, u32[]{:S(2)}) collective-permute-start(bf16[128,1024]{1,0:T(8,128)(2,1)S(1)} %get-tuple-element.8), channel_id=1, source_target_pairs={{0,3},{1,0},{2,1},{3,2},{4,7},{5,4},{6,5},{7,6},{8,11},{9,8},{10,9... | collective-permute-start | bytes 786440 | tf_op jit(solution)/shard_map/ppermute | solution.py:49
  20.9 13.7 %collective-permute-start.4 = (bf16[128,1024]{1,0:T(8,128)(2,1)S(1)}, bf16[128,1024]{1,0:T(8,128)(2,1)S(1)}, u32[]{:S(2)}, u32[]{:S(2)}) collective-permute-start(bf16[128,1024]{1,0:T(8,128)(2,1)S(1)} %get-tuple-element.8), channel_id=1, source_target_pairs={{0,1},{1,2},{2,3},{3,0},{4,5},{5,6},{6,7},{7,4},{8,9},{9,10},{10,1... | collective-permute-start | bytes 786440 | tf_op jit(solution)/shard_map/ppermute | solution.py:49
  54.6 18.9 %collective-permute-start.5 = (bf16[2,512,768]{1,2,0:T(8,128)(2,1)}, bf16[2,512,768]{1,2,0:T(8,128)(2,1)}, u32[]{:S(2)}, u32[]{:S(2)}) collective-permute-start(bf16[2,512,768]{1,2,0:T(8,128)(2,1)} %bitcast.81), channel_id=1, source_target_pairs={{0,4},{4,0},{8,12},{12,8},{1,5},{5,1},{9,13},{13,9},{2,6},{6,2},{1... | collective-permute-start | bytes 4718600 | tf_op jit(solution)/shard_map/ppermute | solution.py:137
  63.3 15.9 %collective-permute-start = (s32[2,255]{1,0:T(2,128)S(1)}, s32[2,255]{1,0:T(2,128)S(1)}, u32[]{:S(2)}, u32[]{:S(2)}) collective-permute-start(s32[2,255]{1,0:T(2,128)S(1)} %get-tuple-element.26), channel_id=1, source_target_pairs={{0,16},{16,32},{32,48},{48,64},{64,80},{80,96},{96,112},{1,17},{17... | collective-permute-start | bytes 6128 | tf_op jit(solution)/shard_map/ppermute | solution.py:21
  64.6 14.6 %collective-permute-start.1 = (s32[2,255]{1,0:T(2,128)S(1)}, s32[2,255]{1,0:T(2,128)S(1)}, u32[]{:S(2)}, u32[]{:S(2)}) collective-permute-start(s32[2,255]{1,0:T(2,128)S(1)} %get-tuple-element.27), channel_id=1, source_target_pairs={{16,0},{32,16},{48,32},{64,48},{80,64},{96,80},{112,96},{17,1},{33... | collective-permute-start | bytes 6128 | tf_op jit(solution)/shard_map/ppermute | solution.py:23
  77.9 17.6 %collective-permute-start.6 = (bf16[512,768]{0,1:T(8,128)(2,1)}, bf16[512,768]{0,1:T(8,128)(2,1)S(1)}, u32[]{:S(2)}, u32[]{:S(2)}) collective-permute-start(bf16[512,768]{0,1:T(8,128)(2,1)} %dynamic-slice_bitcast_fusion.2), channel_id=1, source_target_pairs={{0,8},{4,12},{8,0},{12,4},{1,9},{5,13},{9,1},{13,5},{2,10},{6,14},... | collective-permute-start | bytes 2359304 | tf_op jit(solution)/shard_map/ppermute | solution.py:137
  97.7 12.8 %collective-permute-start.7 = (bf16[2,255,256]{1,2,0:T(8,128)(2,1)}, bf16[2,255,256]{1,2,0:T(8,128)(2,1)}, u32[]{:S(2)}, u32[]{:S(2)}) collective-permute-start(bf16[2,255,256]{1,2,0:T(8,128)(2,1)} %get-tuple-element.22), channel_id=1, source_target_pairs={{0,16},{16,32},{32,48},{48,64},{64,80},{80,96},{96,112},{1,17},{17... | collective-permute-start | bytes 783368 | tf_op jit(solution)/shard_map/ppermute | solution.py:21
  99.0 11.6 %collective-permute-start.8 = (bf16[2,255,256]{1,2,0:T(8,128)(2,1)}, bf16[2,255,256]{1,2,0:T(8,128)(2,1)}, u32[]{:S(2)}, u32[]{:S(2)}) collective-permute-start(bf16[2,255,256]{1,2,0:T(8,128)(2,1)} %get-tuple-element.23), channel_id=1, source_target_pairs={{16,0},{32,16},{48,32},{64,48},{80,64},{96,80},{112,96},{17,1},{33... | collective-permute-start | bytes 783368 | tf_op jit(solution)/shard_map/ppermute | solution.py:23
  119.3 12.1 %collective-permute-start.10 = (bf16[512,256]{1,0:T(8,128)(2,1)S(1)}, bf16[512,256]{1,0:T(8,128)(2,1)S(1)}, u32[]{:S(2)}, u32[]{:S(2)}) collective-permute-start(bf16[512,256]{1,0:T(8,128)(2,1)S(1)} %copy.20), channel_id=1, source_target_pairs={{0,8},{4,12},{8,0},{12,4},{1,9},{5,13},{9,1},{13,5},{2,10},{6,14},... | collective-permute-start | bytes 786440 | tf_op jit(solution)/shard_map/ppermute | solution.py:137
  119.8 11.7 %collective-permute-start.9 = (bf16[512,256]{1,0:T(8,128)(2,1)S(1)}, bf16[512,256]{1,0:T(8,128)(2,1)}, u32[]{:S(2)}, u32[]{:S(2)}) collective-permute-start(bf16[512,256]{1,0:T(8,128)(2,1)S(1)} %copy.20), channel_id=1, source_target_pairs={{0,4},{4,0},{8,12},{12,8},{1,5},{5,1},{9,13},{13,9},{2,6},{6,2},{1... | collective-permute-start | bytes 786440 | tf_op jit(solution)/shard_map/ppermute | solution.py:137
  139.1 16.2 %collective-permute-start.12 = (bf16[128,1024]{1,0:T(8,128)(2,1)}, bf16[128,1024]{1,0:T(8,128)(2,1)}, u32[]{:S(2)}, u32[]{:S(2)}) collective-permute-start(bf16[128,1024]{1,0:T(8,128)(2,1)} %get-tuple-element.14), channel_id=1, source_target_pairs={{0,1},{1,2},{2,3},{3,0},{4,5},{5,6},{6,7},{7,4},{8,9},{9,10},{10,1... | collective-permute-start | bytes 786440 | tf_op jit(solution)/shard_map/ppermute | solution.py:65
  139.4 15.9 %collective-permute-start.14 = (bf16[128,1024]{1,0:T(8,128)(2,1)}, bf16[128,1024]{1,0:T(8,128)(2,1)}, u32[]{:S(2)}, u32[]{:S(2)}) collective-permute-start(bf16[128,1024]{1,0:T(8,128)(2,1)} %get-tuple-element.15), channel_id=1, source_target_pairs={{0,3},{1,0},{2,1},{3,2},{4,7},{5,4},{6,5},{7,6},{8,11},{9,8},{10,9... | collective-permute-start | bytes 786440 | tf_op jit(solution)/shard_map/ppermute | solution.py:65
  142.4 13.0 %collective-permute-start.13 = (bf16[128,1024]{1,0:T(8,128)(2,1)}, bf16[128,1024]{1,0:T(8,128)(2,1)}, u32[]{:S(2)}, u32[]{:S(2)}) collective-permute-start(bf16[128,1024]{1,0:T(8,128)(2,1)} %get-tuple-element.16), channel_id=1, source_target_pairs={{0,2},{1,3},{2,0},{3,1},{4,6},{5,7},{6,4},{7,5},{8,10},{9,11},{10,... | collective-permute-start | bytes 786440 | tf_op jit(solution)/shard_map/ppermute | solution.py:65
  157.4 12.7 %collective-permute-start.15 = (bf16[128,1024]{1,0:T(8,128)(2,1)}, bf16[128,1024]{1,0:T(8,128)(2,1)S(1)}, u32[]{:S(2)}, u32[]{:S(2)}) collective-permute-start(bf16[128,1024]{1,0:T(8,128)(2,1)} %fusion.30), channel_id=1, source_target_pairs={{1,0},{2,1},{3,2},{16,3},{17,16},{18,17},{19,18},{32,19},{33,32},{... | collective-permute-start | bytes 786440 | tf_op jit(solution)/shard_map/ppermute | solution.py:33
  178.3 12.2 %collective-permute-start.16 = (bf16[192,1024]{1,0:T(8,128)(2,1)}, bf16[192,1024]{1,0:T(8,128)(2,1)S(1)}, u32[]{:S(2)}, u32[]{:S(2)}) collective-permute-start(bf16[192,1024]{1,0:T(8,128)(2,1)} %get-tuple-element.6), channel_id=1, source_target_pairs={{0,3},{1,0},{2,1},{3,2},{4,7},{5,4},{6,5},{7,6},{8,11},{9,8},{10,9... | collective-permute-start | bytes 1179656 | tf_op jit(solution)/shard_map/ppermute | solution.py:49
  178.3 13.9 %collective-permute-start.17 = (bf16[192,1024]{1,0:T(8,128)(2,1)}, bf16[192,1024]{1,0:T(8,128)(2,1)}, u32[]{:S(2)}, u32[]{:S(2)}) collective-permute-start(bf16[192,1024]{1,0:T(8,128)(2,1)} %get-tuple-element.6), channel_id=1, source_target_pairs={{0,2},{1,3},{2,0},{3,1},{4,6},{5,7},{6,4},{7,5},{8,10},{9,11},{10,... | collective-permute-start | bytes 1179656 | tf_op jit(solution)/shard_map/ppermute | solution.py:49
  179.1 20.4 %collective-permute-start.18 = (bf16[192,1024]{1,0:T(8,128)(2,1)}, bf16[192,1024]{1,0:T(8,128)(2,1)}, u32[]{:S(2)}, u32[]{:S(2)}) collective-permute-start(bf16[192,1024]{1,0:T(8,128)(2,1)} %get-tuple-element.6), channel_id=1, source_target_pairs={{0,1},{1,2},{2,3},{3,0},{4,5},{5,6},{6,7},{7,4},{8,9},{9,10},{10,1... | collective-permute-start | bytes 1179656 | tf_op jit(solution)/shard_map/ppermute | solution.py:49
  226.7 28.1 %collective-permute-start.20 = (bf16[768,768]{1,0:T(8,128)(2,1)S(1)}, bf16[768,768]{1,0:T(8,128)(2,1)S(1)}, u32[]{:S(2)}, u32[]{:S(2)}) collective-permute-start(bf16[768,768]{1,0:T(8,128)(2,1)S(1)} %dynamic-slice_bitcast_fusion.1), channel_id=1, source_target_pairs={{0,8},{4,12},{8,0},{12,4},{1,9},{5,13},{9,1},{13,5},{2,10},{6,14},... | collective-permute-start | bytes 3538952 | tf_op jit(solution)/shard_map/ppermute | solution.py:137
  400.5 18.9 %collective-permute-start.22 = (bf16[768,256]{1,0:T(8,128)(2,1)}, bf16[768,256]{1,0:T(8,128)(2,1)S(1)}, u32[]{:S(2)}, u32[]{:S(2)}) collective-permute-start(bf16[768,256]{1,0:T(8,128)(2,1)} %shard_map.138), channel_id=1, source_target_pairs={{0,8},{4,12},{8,0},{12,4},{1,9},{5,13},{9,1},{13,5},{2,10},{6,14},... | collective-permute-start | bytes 1179656 | tf_op jit(solution)/shard_map/ppermute | solution.py:137
  401.5 18.0 %collective-permute-start.21 = (bf16[768,256]{1,0:T(8,128)(2,1)}, bf16[768,256]{1,0:T(8,128)(2,1)S(1)}, u32[]{:S(2)}, u32[]{:S(2)}) collective-permute-start(bf16[768,256]{1,0:T(8,128)(2,1)} %shard_map.138), channel_id=1, source_target_pairs={{0,4},{4,0},{8,12},{12,8},{1,5},{5,1},{9,13},{13,9},{2,6},{6,2},{1... | collective-permute-start | bytes 1179656 | tf_op jit(solution)/shard_map/ppermute | solution.py:137
  430.4 12.4 %collective-permute-start.24 = (bf16[192,1024]{1,0:T(8,128)(2,1)}, bf16[192,1024]{1,0:T(8,128)(2,1)}, u32[]{:S(2)}, u32[]{:S(2)}) collective-permute-start(bf16[192,1024]{1,0:T(8,128)(2,1)} %get-tuple-element.11), channel_id=1, source_target_pairs={{0,1},{1,2},{2,3},{3,0},{4,5},{5,6},{6,7},{7,4},{8,9},{9,10},{10,1... | collective-permute-start | bytes 1179656 | tf_op jit(solution)/shard_map/ppermute | solution.py:65
  431.9 12.4 %collective-permute-start.26 = (bf16[192,1024]{1,0:T(8,128)(2,1)}, bf16[192,1024]{1,0:T(8,128)(2,1)}, u32[]{:S(2)}, u32[]{:S(2)}) collective-permute-start(bf16[192,1024]{1,0:T(8,128)(2,1)} %get-tuple-element.12), channel_id=1, source_target_pairs={{0,3},{1,0},{2,1},{3,2},{4,7},{5,4},{6,5},{7,6},{8,11},{9,8},{10,9... | collective-permute-start | bytes 1179656 | tf_op jit(solution)/shard_map/ppermute | solution.py:65
  433.6 18.5 %collective-permute-start.25 = (bf16[192,1024]{1,0:T(8,128)(2,1)S(1)}, bf16[192,1024]{1,0:T(8,128)(2,1)}, u32[]{:S(2)}, u32[]{:S(2)}) collective-permute-start(bf16[192,1024]{1,0:T(8,128)(2,1)S(1)} %get-tuple-element.13), channel_id=1, source_target_pairs={{0,2},{1,3},{2,0},{3,1},{4,6},{5,7},{6,4},{7,5},{8,10},{9,11},{10,... | collective-permute-start | bytes 1179656 | tf_op jit(solution)/shard_map/ppermute | solution.py:65
  (17 other events, 643.7 us)
Sparse Core Ops, SparseCore 0:
  256.5 93.0 all-gather.1

commit v7 on v6

--- a/solution.py
+++ b/solution.py
@@ -195,16 +195,15 @@
     return scatter_permute(summed.astype(jnp.bfloat16), "col")
 
 
-def causal_attend(proj, keyvals, base, key_tile=512):
+def causal_attend(proj, blocks, place):
     count = proj.shape[0]
     heads = proj.shape[1] // (3 * HD)
-    total = keyvals.shape[0]
-    steps = total // key_tile
+    steps = blocks.shape[0]
     scale = HD ** (-0.5)
 
-    def body(base_ref, q_ref, k_ref, v_ref, o_ref, peak_ref, mass_ref, acc_ref):
+    def body(place_ref, q_ref, k_ref, v_ref, o_ref, peak_ref, mass_ref, acc_ref):
         step = pl.program_id(1)
-        first = base_ref[0]
+        own = place_ref[0]
 
         @pl.when(step == 0)
         def _():
@@ -217,8 +216,8 @@
                 q_ref[...], k_ref[...], (((1,), (1,)), ((), ())),
                 preferred_element_type=jnp.float32) * scale
             if masked:
-                rows = first + lax.broadcasted_iota(jnp.int32, scores.shape, 0)
-                cols = step * key_tile + lax.broadcasted_iota(jnp.int32, scores.shape, 1)
+                rows = lax.broadcasted_iota(jnp.int32, scores.shape, 0)
+                cols = lax.broadcasted_iota(jnp.int32, scores.shape, 1)
                 allowed = cols <= rows
                 scores = jnp.where(allowed, scores, -1e30)
             old = peak_ref[...]
@@ -232,14 +231,11 @@
                 weights.astype(jnp.bfloat16), v_ref[...], preferred_element_type=jnp.float32)
             peak_ref[...] = new
 
-        start = step * key_tile
-        end = start + key_tile - 1
-
-        @pl.when(end <= first)
+        @pl.when(step < own)
         def _():
             fold(False)
 
-        @pl.when((end > first) & (start <= first + count - 1))
+        @pl.when(step == own)
         def _():
             fold(True)
 
@@ -251,11 +247,13 @@
         num_scalar_prefetch=1,
         grid=(heads, steps),
         in_specs=[
-            pl.BlockSpec((count, HD), lambda h, j, b: (0, h)),
-            pl.BlockSpec((key_tile, HD), lambda h, j, b: (j, h)),
-            pl.BlockSpec((key_tile, HD), lambda h, j, b: (j, heads + h)),
+            pl.BlockSpec((count, HD), lambda h, j, p: (0, h)),
+            pl.BlockSpec((None, count, HD), lambda h, j, p: (p[0] - jnp.minimum(j, p[0]), 0, h)),
+            pl.BlockSpec(
+                (None, count, HD), lambda h, j, p: (p[0] - jnp.minimum(j, p[0]), 0, heads + h)
+            ),
         ],
-        out_specs=pl.BlockSpec((count, HD), lambda h, j, b: (0, h)),
+        out_specs=pl.BlockSpec((count, HD), lambda h, j, p: (0, h)),
         scratch_shapes=[
             pltpu.VMEM((count, 1), jnp.float32),
             pltpu.VMEM((count, 1), jnp.float32),
@@ -266,7 +264,7 @@
         body,
         grid_spec=grid_spec,
         out_shape=jax.ShapeDtypeStruct((count, heads * HD), jnp.bfloat16),
-    )(base, proj, keyvals, keyvals)
+    )(place, proj, blocks, blocks)
 
 
 def per_device(
@@ -343,9 +341,14 @@
     dec_cols = gather_cols(norm_local(mixed, dec_gain))
     dec_proj = head_project(dec_cols, (dec_wq, dec_wk, dec_wv))
     dec_rows = dec_cols.shape[0]
-    piece = lax.all_gather(dec_proj[:, local:], "req", axis=0, tiled=True)
-    base = (lax.axis_index("req") * dec_rows).astype(jnp.int32).reshape(1)
-    dec_att = causal_attend(dec_proj, piece, base)
+    keyvals = dec_proj[:, local:]
+    req_count = lax.axis_size("req")
+    earlier = [keyvals] + [
+        lax.ppermute(keyvals, "req", [(j, j + s) for j in range(req_count - s)])
+        for s in range(1, req_count)
+    ]
+    place = lax.axis_index("req").astype(jnp.int32).reshape(1)
+    dec_att = causal_attend(dec_proj, jnp.stack(earlier), place)
     return (mixed.astype(jnp.float32) + out_project_heads(dec_att, dec_wo)).astype(jnp.bfloat16)
 
 

time: 463 us -> 436 us (0.942)
  waiting for transfers between devices: 229 us -> 210 us
  between operations: 13.9 us -> 0.57 us
  starting transfers between devices: 45.4 us -> 52.6 us
  Pallas kernels: 66.9 us -> 60 us
  local copies, waits for them, and re-layouts: 49.8 us -> 55.6 us
    all_gather x1 -> x0, waiting for transfers between devices: 93.2 us -> none  [per_device(): piece = lax.all_gather(dec_proj[:, local:], 'req', axis=0, tiled=True)]
    ppermute x0 -> x7, waiting for transfers between devices: none -> 70 us  [per_device(): lax.ppermute(keyvals, 'req', [(j, j + s) for j in range(req_count - s)])]
    ppermute x0 -> x7, starting transfers between devices: none -> 9.24 us  [per_device(): lax.ppermute(keyvals, 'req', [(j, j + s) for j in range(req_count - s)])]
    pallas_call x1, Pallas kernels: 49.9 us -> 42.9 us  [causal_attend(): pl.pallas_call(body, grid_spec=grid_spec, out_shape=jax.ShapeDtypeStruct(...]
    unnamed x39 -> x42, local copies, waits for them, and re-layouts: 18.6 us -> 24.6 us
  transfers between devices with their start and end apart: 28 -> 34, of which waited for: 19 -> 24; matrix products, arithmetic and copies ran while one was open for 4% -> 5% of each run, Pallas kernels for 0% -> 0%
where the time goes in v7:
time: 436 us; the launch traced here: 435 us
  waiting for transfers between devices  210 us (48%)
  Pallas kernels  60 us (14%)
  local copies, waits for them, and re-layouts  55.6 us (13%)
  starting transfers between devices  52.6 us (12%)
  other arithmetic  21.4 us (5%)
  blocking collectives  21 us (5%)
  matrix products  14.1 us (3%)
    ppermute x10, waiting for transfers between devices, flip(): return lax.ppermute(values, axis, [(j, j ^ bit) for j in range(count)])  76.8 us
    ppermute x7, waiting for transfers between devices, per_device(): lax.ppermute(keyvals, 'req', [(j, j + s) for j in range(req_count - s)])  70 us
    pallas_call x1, Pallas kernels, causal_attend(): pl.pallas_call(body, grid_spec=grid_spec, out_shape=jax.ShapeDtypeStruct(...  42.9 us
    ppermute x6, waiting for transfers between devices, scatter_permute(): lax.ppermute(chunk, axis, [(j, (j + s) % count) for j in range(count)])  29.2 us
    ppermute x6, waiting for transfers between devices, gather_permute(): lax.ppermute(values, axis, [(j, (j + s) % count) for j in range(count)])  27.5 us
    unnamed x42, local copies, waits for them, and re-layouts  24.6 us
    pallas_call x2, Pallas kernels, head_project(): pl.pallas_call(body, grid=(row_count,), in_specs=[pl.BlockSpec((count, de...  17.1 us
    ppermute x2, starting transfers between devices, with_halo(): lax.ppermute(head, axis, [((i + 1) % count, i) for i in range(ends)])  12.8 us
  transfers between devices with their start and end apart: 34, of which 24 were waited for; matrix products, arithmetic and copies ran while one was open for 5% of the time, Pallas kernels for 0%

profile of v7, /device:TPU:28, one launch (start us, length us, event | category | flops | bytes accessed | tf_op | source)
XLA Modules:
  0.0 434.9 jit_solution(12716163341846036537)
XLA Ops:
  1.9 6.6 %psum.14 = f32[128]{0:T(128)S(1)} all-reduce(f32[128]{0:T(128)S(1)} %fusion.27), channel_id=1, replica_groups=mesh['req'=8,'row'=4,'col'=4] {'row'}, use_global_device_ids=true, to_apply=%region_3.4 | all-reduce | flops 128 | bytes 1024 | tf_op jit(solution)/shard_map/psum | solution.py:39
  15.6 9.0 %collective-permute-done.2 = bf16[128,1024]{1,0:T(8,128)(2,1)S(1)} collective-permute-done((bf16[128,1024]{1,0:T(8,128)(2,1)S(1)}, bf16[128,1024]{1,0:T(8,128)(2,1)S(1)}, u32[]{:S(2)}, u32[]{:S(2)}) %collective-permute-start.2) | collective-permute-done | bytes 262176 | tf_op jit(solution)/shard_map/ppermute | solution.py:49
  34.0 7.7 %shard_map.136 = bf16[4,512,768]{2,1,0:T(8,128)(2,1)} custom-call(bf16[512,1024]{1,0:T(8,128)(2,1)} %constant_dynamic-slice_fusion.9.x_ref, bf16[1024,1024]{1,0:T(8,128)(2,1)} %refs_0_.2, bf16[1024,1024]{1,0:T(8,128)(2,1)} %refs_1_.2, bf16[1024,1024]{1,0:T(8,128)(2,1)} %refs_2_.2), custom_call_target="tpu_custom_call" | custom-call | tf_op jit(solution)/shard_map/pallas_call | solution.py:178
  48.1 8.7 %all_gather.3 = s32[2,512]{1,0:T(2,128)S(1)} all-gather(s32[2,128]{1,0:T(2,128)S(1)} %pad_add_fusion.1), channel_id=1, replica_groups=mesh['req'=8,'row'=4,'col'=4] {'col'}, dimensions={1}, use_global_device_ids=true | all-gather | bytes 5120 | tf_op jit(solution)/shard_map/all_gather | solution.py:291
  58.2 6.1 %collective-permute-start.1 = (s32[2,255]{1,0:T(2,128)S(1)}, s32[2,255]{1,0:T(2,128)S(1)}, u32[]{:S(2)}, u32[]{:S(2)}) collective-permute-start(s32[2,255]{1,0:T(2,128)S(1)} %get-tuple-element.27), channel_id=1, source_target_pairs={{16,0},{32,16},{48,32},{64,48},{80,64},{96,80},{112,96},{17,1},{33... | collective-permute-start | bytes 6128 | tf_op jit(solution)/shard_map/ppermute | solution.py:23
  72.9 16.1 %collective-permute-done.6 = bf16[512,768]{0,1:T(8,128)(2,1)S(1)} collective-permute-done((bf16[512,768]{0,1:T(8,128)(2,1)}, bf16[512,768]{0,1:T(8,128)(2,1)S(1)}, u32[]{:S(2)}, u32[]{:S(2)}) %collective-permute-start.6) | collective-permute-done | bytes 786464 | tf_op jit(solution)/shard_map/ppermute | solution.py:137
  92.6 6.8 %collective-permute-start.8 = (bf16[2,255,256]{1,2,0:T(8,128)(2,1)}, bf16[2,255,256]{1,2,0:T(8,128)(2,1)}, u32[]{:S(2)}, u32[]{:S(2)}) collective-permute-start(bf16[2,255,256]{1,2,0:T(8,128)(2,1)} %get-tuple-element.23), channel_id=1, source_target_pairs={{16,0},{32,16},{48,32},{64,48},{80,64},{96,80},{112,96},{17,1},{33... | collective-permute-start | bytes 783368 | tf_op jit(solution)/shard_map/ppermute | solution.py:23
  115.5 6.6 %collective-permute-done.10 = bf16[512,256]{1,0:T(8,128)(2,1)S(1)} collective-permute-done((bf16[512,256]{1,0:T(8,128)(2,1)S(1)}, bf16[512,256]{1,0:T(8,128)(2,1)S(1)}, u32[]{:S(2)}, u32[]{:S(2)}) %collective-permute-start.10) | collective-permute-done | bytes 262176 | tf_op jit(solution)/shard_map/ppermute | solution.py:137
  138.9 10.6 %collective-permute-done.12 = bf16[128,1024]{1,0:T(8,128)(2,1)} collective-permute-done((bf16[128,1024]{1,0:T(8,128)(2,1)}, bf16[128,1024]{1,0:T(8,128)(2,1)}, u32[]{:S(2)}, u32[]{:S(2)}) %collective-permute-start.12) | collective-permute-done | bytes 262176 | tf_op jit(solution)/shard_map/ppermute | solution.py:65
  152.1 6.5 %collective-permute-start.15 = (bf16[128,1024]{1,0:T(8,128)(2,1)}, bf16[128,1024]{1,0:T(8,128)(2,1)S(1)}, u32[]{:S(2)}, u32[]{:S(2)}) collective-permute-start(bf16[128,1024]{1,0:T(8,128)(2,1)} %fusion.30), channel_id=1, source_target_pairs={{1,0},{2,1},{3,2},{16,3},{17,16},{18,17},{19,18},{32,19},{33,32},{... | collective-permute-start | bytes 786440 | tf_op jit(solution)/shard_map/ppermute | solution.py:33
  166.0 5.7 %psum.15 = f32[192]{0:T(256)S(1)} all-reduce(f32[192]{0:T(256)S(1)} %get-tuple-element.30), channel_id=1, replica_groups=mesh['req'=8,'row'=4,'col'=4] {'row'}, use_global_device_ids=true, to_apply=%region_7.8 | all-reduce | flops 192 | bytes 1536 | tf_op jit(solution)/shard_map/psum | solution.py:39
  174.7 10.2 %collective-permute-done.16 = bf16[192,1024]{1,0:T(8,128)(2,1)S(1)} collective-permute-done((bf16[192,1024]{1,0:T(8,128)(2,1)}, bf16[192,1024]{1,0:T(8,128)(2,1)S(1)}, u32[]{:S(2)}, u32[]{:S(2)}) %collective-permute-start.16) | collective-permute-done | bytes 393248 | tf_op jit(solution)/shard_map/ppermute | solution.py:49
  188.4 5.5 %collective-permute-done.18 = bf16[192,1024]{1,0:T(8,128)(2,1)} collective-permute-done((bf16[192,1024]{1,0:T(8,128)(2,1)}, bf16[192,1024]{1,0:T(8,128)(2,1)}, u32[]{:S(2)}, u32[]{:S(2)}) %collective-permute-start.18) | collective-permute-done | bytes 393248 | tf_op jit(solution)/shard_map/ppermute | solution.py:49
  204.4 9.4 %shard_map.137 = bf16[4,768,768]{2,1,0:T(8,128)(2,1)} custom-call(bf16[768,1024]{1,0:T(8,128)(2,1)} %constant_dynamic-slice_fusion.3.x_ref, bf16[1024,1024]{1,0:T(8,128)(2,1)} %refs_0_.3, bf16[1024,1024]{1,0:T(8,128)(2,1)} %refs_1_.3, bf16[1024,1024]{1,0:T(8,128)(2,1)} %refs_2_.3), custom_call_target="tpu_custom_call" | custom-call | tf_op jit(solution)/shard_map/pallas_call | solution.py:178
  222.4 26.8 %collective-permute-done.20 = bf16[768,768]{1,0:T(8,128)(2,1)S(1)} collective-permute-done((bf16[768,768]{1,0:T(8,128)(2,1)S(1)}, bf16[768,768]{1,0:T(8,128)(2,1)S(1)}, u32[]{:S(2)}, u32[]{:S(2)}) %collective-permute-start.20) | collective-permute-done | bytes 1179680 | tf_op jit(solution)/shard_map/ppermute | solution.py:137
  257.0 17.5 %collective-permute-done.21 = bf16[768,512]{1,0:T(8,128)(2,1)S(1)} collective-permute-done((bf16[768,512]{1,0:T(8,128)(2,1)S(1)}, bf16[768,512]{1,0:T(8,128)(2,1)S(1)}, u32[]{:S(2)}, u32[]{:S(2)}) %collective-permute-start.21) | collective-permute-done | bytes 786464 | tf_op jit(solution)/shard_map/ppermute | solution.py:347
  282.4 14.2 %collective-permute-done.23 = bf16[768,512]{1,0:T(8,128)(2,1)S(1)} collective-permute-done((bf16[768,512]{1,0:T(8,128)(2,1)S(1)}, bf16[768,512]{1,0:T(8,128)(2,1)S(1)}, u32[]{:S(2)}, u32[]{:S(2)}) %collective-permute-start.23) | collective-permute-done | bytes 786464 | tf_op jit(solution)/shard_map/ppermute | solution.py:347
  298.4 15.9 %collective-permute-done.25 = bf16[768,512]{1,0:T(8,128)(2,1)S(1)} collective-permute-done((bf16[768,512]{1,0:T(8,128)(2,1)S(1)}, bf16[768,512]{1,0:T(8,128)(2,1)S(1)}, u32[]{:S(2)}, u32[]{:S(2)}) %collective-permute-start.25) | collective-permute-done | bytes 786464 | tf_op jit(solution)/shard_map/ppermute | solution.py:347
  315.3 19.3 %collective-permute-done.26 = bf16[768,512]{1,0:T(8,128)(2,1)S(1)} collective-permute-done((bf16[768,512]{1,0:T(8,128)(2,1)S(1)}, bf16[768,512]{1,0:T(8,128)(2,1)S(1)}, u32[]{:S(2)}, u32[]{:S(2)}) %collective-permute-start.26) | collective-permute-done | bytes 786464 | tf_op jit(solution)/shard_map/ppermute | solution.py:347
  336.4 42.9 %shard_map.138 = bf16[768,256]{1,0:T(8,128)(2,1)} custom-call(s32[1]{0:T(128)} %bitcast.28.place_ref, bf16[768,768]{1,0:T(8,128)(2,1)} %copy-done.2, bf16[8,768,512]{2,1,0:T(8,128)(2,1)} %bitcast_dynamic-update-slice_fusion.k_ref.v_ref, bf16[8,768,512]{2,1,0:T(8,128)(2,1)} %bitcast_dynamic-update-slice_fusion.k_ref.v_ref), custom_call_target="tpu_custom_call" | custom-call | tf_op jit(solution)/shard_map/pallas_call | solution.py:263
  381.3 10.3 %collective-permute-done.29 = bf16[768,256]{1,0:T(8,128)(2,1)} collective-permute-done((bf16[768,256]{1,0:T(8,128)(2,1)}, bf16[768,256]{1,0:T(8,128)(2,1)}, u32[]{:S(2)}, u32[]{:S(2)}) %collective-permute-start.29) | collective-permute-done | bytes 393248 | tf_op jit(solution)/shard_map/ppermute | solution.py:137
  391.6 7.7 %collective-permute-done.30 = bf16[768,256]{1,0:T(8,128)(2,1)} collective-permute-done((bf16[768,256]{1,0:T(8,128)(2,1)}, bf16[768,256]{1,0:T(8,128)(2,1)}, u32[]{:S(2)}, u32[]{:S(2)}) %collective-permute-start.30) | collective-permute-done | bytes 393248 | tf_op jit(solution)/shard_map/ppermute | solution.py:137
  414.6 8.6 %collective-permute-done.31 = bf16[192,1024]{1,0:T(8,128)(2,1)} collective-permute-done((bf16[192,1024]{1,0:T(8,128)(2,1)}, bf16[192,1024]{1,0:T(8,128)(2,1)}, u32[]{:S(2)}, u32[]{:S(2)}) %collective-permute-start.31) | collective-permute-done | bytes 393248 | tf_op jit(solution)/shard_map/ppermute | solution.py:65
  423.1 9.4 %collective-permute-done.32 = bf16[192,1024]{1,0:T(8,128)(2,1)} collective-permute-done((bf16[192,1024]{1,0:T(8,128)(2,1)}, bf16[192,1024]{1,0:T(8,128)(2,1)}, u32[]{:S(2)}, u32[]{:S(2)}) %collective-permute-start.32) | collective-permute-done | bytes 393248 | tf_op jit(solution)/shard_map/ppermute | solution.py:65
  (164 shorter events, 146.6 us)
Async XLA Ops:
  10.3 14.3 %collective-permute-start.2 = (bf16[128,1024]{1,0:T(8,128)(2,1)S(1)}, bf16[128,1024]{1,0:T(8,128)(2,1)S(1)}, u32[]{:S(2)}, u32[]{:S(2)}) collective-permute-start(bf16[128,1024]{1,0:T(8,128)(2,1)S(1)} %get-tuple-element.8), channel_id=1, source_target_pairs={{0,3},{1,0},{2,1},{3,2},{4,7},{5,4},{6,5},{7,6},{8,11},{9,8},{10,9... | collective-permute-start | bytes 786440 | tf_op jit(solution)/shard_map/ppermute | solution.py:49
  14.4 13.7 %collective-permute-start.4 = (bf16[128,1024]{1,0:T(8,128)(2,1)S(1)}, bf16[128,1024]{1,0:T(8,128)(2,1)S(1)}, u32[]{:S(2)}, u32[]{:S(2)}) collective-permute-start(bf16[128,1024]{1,0:T(8,128)(2,1)S(1)} %get-tuple-element.8), channel_id=1, source_target_pairs={{0,1},{1,2},{2,3},{3,0},{4,5},{5,6},{6,7},{7,4},{8,9},{9,10},{10,1... | collective-permute-start | bytes 786440 | tf_op jit(solution)/shard_map/ppermute | solution.py:49
  48.1 18.9 %collective-permute-start.5 = (bf16[2,512,768]{1,2,0:T(8,128)(2,1)}, bf16[2,512,768]{1,2,0:T(8,128)(2,1)}, u32[]{:S(2)}, u32[]{:S(2)}) collective-permute-start(bf16[2,512,768]{1,2,0:T(8,128)(2,1)} %bitcast.97), channel_id=1, source_target_pairs={{0,4},{4,0},{8,12},{12,8},{1,5},{5,1},{9,13},{13,9},{2,6},{6,2},{1... | collective-permute-start | bytes 4718600 | tf_op jit(solution)/shard_map/ppermute | solution.py:137
  56.9 15.9 %collective-permute-start = (s32[2,255]{1,0:T(2,128)S(1)}, s32[2,255]{1,0:T(2,128)S(1)}, u32[]{:S(2)}, u32[]{:S(2)}) collective-permute-start(s32[2,255]{1,0:T(2,128)S(1)} %get-tuple-element.26), channel_id=1, source_target_pairs={{0,16},{16,32},{32,48},{48,64},{64,80},{80,96},{96,112},{1,17},{17... | collective-permute-start | bytes 6128 | tf_op jit(solution)/shard_map/ppermute | solution.py:21
  58.2 14.6 %collective-permute-start.1 = (s32[2,255]{1,0:T(2,128)S(1)}, s32[2,255]{1,0:T(2,128)S(1)}, u32[]{:S(2)}, u32[]{:S(2)}) collective-permute-start(s32[2,255]{1,0:T(2,128)S(1)} %get-tuple-element.27), channel_id=1, source_target_pairs={{16,0},{32,16},{48,32},{64,48},{80,64},{96,80},{112,96},{17,1},{33... | collective-permute-start | bytes 6128 | tf_op jit(solution)/shard_map/ppermute | solution.py:23
  71.4 17.6 %collective-permute-start.6 = (bf16[512,768]{0,1:T(8,128)(2,1)}, bf16[512,768]{0,1:T(8,128)(2,1)S(1)}, u32[]{:S(2)}, u32[]{:S(2)}) collective-permute-start(bf16[512,768]{0,1:T(8,128)(2,1)} %dynamic-slice_bitcast_fusion.2), channel_id=1, source_target_pairs={{0,8},{4,12},{8,0},{12,4},{1,9},{5,13},{9,1},{13,5},{2,10},{6,14},... | collective-permute-start | bytes 2359304 | tf_op jit(solution)/shard_map/ppermute | solution.py:137
  91.3 12.8 %collective-permute-start.7 = (bf16[2,255,256]{1,2,0:T(8,128)(2,1)}, bf16[2,255,256]{1,2,0:T(8,128)(2,1)}, u32[]{:S(2)}, u32[]{:S(2)}) collective-permute-start(bf16[2,255,256]{1,2,0:T(8,128)(2,1)} %get-tuple-element.22), channel_id=1, source_target_pairs={{0,16},{16,32},{32,48},{48,64},{64,80},{80,96},{96,112},{1,17},{17... | collective-permute-start | bytes 783368 | tf_op jit(solution)/shard_map/ppermute | solution.py:21
  113.4 13.5 %collective-permute-start.11 = (bf16[512,256]{1,0:T(8,128)(2,1)S(1)}, bf16[512,256]{1,0:T(8,128)(2,1)}, u32[]{:S(2)}, u32[]{:S(2)}) collective-permute-start(bf16[512,256]{1,0:T(8,128)(2,1)S(1)} %copy.20), channel_id=1, source_target_pairs={{0,12},{4,8},{8,4},{12,0},{1,13},{5,9},{9,5},{13,1},{2,14},{6,10},... | collective-permute-start | bytes 786440 | tf_op jit(solution)/shard_map/ppermute | solution.py:137
  133.8 15.7 %collective-permute-start.12 = (bf16[128,1024]{1,0:T(8,128)(2,1)}, bf16[128,1024]{1,0:T(8,128)(2,1)}, u32[]{:S(2)}, u32[]{:S(2)}) collective-permute-start(bf16[128,1024]{1,0:T(8,128)(2,1)} %get-tuple-element.14), channel_id=1, source_target_pairs={{0,1},{1,2},{2,3},{3,0},{4,5},{5,6},{6,7},{7,4},{8,9},{9,10},{10,1... | collective-permute-start | bytes 786440 | tf_op jit(solution)/shard_map/ppermute | solution.py:65
  134.1 15.4 %collective-permute-start.13 = (bf16[128,1024]{1,0:T(8,128)(2,1)}, bf16[128,1024]{1,0:T(8,128)(2,1)}, u32[]{:S(2)}, u32[]{:S(2)}) collective-permute-start(bf16[128,1024]{1,0:T(8,128)(2,1)} %get-tuple-element.16), channel_id=1, source_target_pairs={{0,2},{1,3},{2,0},{3,1},{4,6},{5,7},{6,4},{7,5},{8,10},{9,11},{10,... | collective-permute-start | bytes 786440 | tf_op jit(solution)/shard_map/ppermute | solution.py:65
  135.7 14.4 %collective-permute-start.14 = (bf16[128,1024]{1,0:T(8,128)(2,1)}, bf16[128,1024]{1,0:T(8,128)(2,1)}, u32[]{:S(2)}, u32[]{:S(2)}) collective-permute-start(bf16[128,1024]{1,0:T(8,128)(2,1)} %get-tuple-element.15), channel_id=1, source_target_pairs={{0,3},{1,0},{2,1},{3,2},{4,7},{5,4},{6,5},{7,6},{8,11},{9,8},{10,9... | collective-permute-start | bytes 786440 | tf_op jit(solution)/shard_map/ppermute | solution.py:65
  172.7 13.9 %collective-permute-start.17 = (bf16[192,1024]{1,0:T(8,128)(2,1)}, bf16[192,1024]{1,0:T(8,128)(2,1)}, u32[]{:S(2)}, u32[]{:S(2)}) collective-permute-start(bf16[192,1024]{1,0:T(8,128)(2,1)} %get-tuple-element.6), channel_id=1, source_target_pairs={{0,2},{1,3},{2,0},{3,1},{4,6},{5,7},{6,4},{7,5},{8,10},{9,11},{10,... | collective-permute-start | bytes 1179656 | tf_op jit(solution)/shard_map/ppermute | solution.py:49
  173.1 20.7 %collective-permute-start.18 = (bf16[192,1024]{1,0:T(8,128)(2,1)}, bf16[192,1024]{1,0:T(8,128)(2,1)}, u32[]{:S(2)}, u32[]{:S(2)}) collective-permute-start(bf16[192,1024]{1,0:T(8,128)(2,1)} %get-tuple-element.6), channel_id=1, source_target_pairs={{0,1},{1,2},{2,3},{3,0},{4,5},{5,6},{6,7},{7,4},{8,9},{9,10},{10,1... | collective-permute-start | bytes 1179656 | tf_op jit(solution)/shard_map/ppermute | solution.py:49
  221.1 28.1 %collective-permute-start.20 = (bf16[768,768]{1,0:T(8,128)(2,1)S(1)}, bf16[768,768]{1,0:T(8,128)(2,1)S(1)}, u32[]{:S(2)}, u32[]{:S(2)}) collective-permute-start(bf16[768,768]{1,0:T(8,128)(2,1)S(1)} %dynamic-slice_bitcast_fusion.1), channel_id=1, source_target_pairs={{0,8},{4,12},{8,0},{12,4},{1,9},{5,13},{9,1},{13,5},{2,10},{6,14},... | collective-permute-start | bytes 3538952 | tf_op jit(solution)/shard_map/ppermute | solution.py:137
  249.6 24.9 %collective-permute-start.21 = (bf16[768,512]{1,0:T(8,128)(2,1)S(1)}, bf16[768,512]{1,0:T(8,128)(2,1)S(1)}, u32[]{:S(2)}, u32[]{:S(2)}) collective-permute-start(bf16[768,512]{1,0:T(8,128)(2,1)S(1)} %slice.97), channel_id=1, source_target_pairs={{0,16},{16,32},{32,48},{48,64},{64,80},{80,96},{96,112},{1,17},{17... | collective-permute-start | bytes 2359304 | tf_op jit(solution)/shard_map/ppermute | solution.py:347
  250.9 29.1 %collective-permute-start.22 = (bf16[768,512]{1,0:T(8,128)(2,1)S(1)}, bf16[768,512]{1,0:T(8,128)(2,1)S(1)}, u32[]{:S(2)}, u32[]{:S(2)}) collective-permute-start(bf16[768,512]{1,0:T(8,128)(2,1)S(1)} %slice.97), channel_id=1, source_target_pairs={{0,32},{16,48},{32,64},{48,80},{64,96},{80,112},{1,33},{17,49},{33... | collective-permute-start | bytes 2359304 | tf_op jit(solution)/shard_map/ppermute | solution.py:347
  252.2 44.4 %collective-permute-start.23 = (bf16[768,512]{1,0:T(8,128)(2,1)S(1)}, bf16[768,512]{1,0:T(8,128)(2,1)S(1)}, u32[]{:S(2)}, u32[]{:S(2)}) collective-permute-start(bf16[768,512]{1,0:T(8,128)(2,1)S(1)} %slice.97), channel_id=1, source_target_pairs={{0,48},{16,64},{32,80},{48,96},{64,112},{1,49},{17,65},{33,81},{49... | collective-permute-start | bytes 2359304 | tf_op jit(solution)/shard_map/ppermute | solution.py:347
  253.5 44.1 %collective-permute-start.24 = (bf16[768,512]{1,0:T(8,128)(2,1)S(1)}, bf16[768,512]{1,0:T(8,128)(2,1)S(1)}, u32[]{:S(2)}, u32[]{:S(2)}) collective-permute-start(bf16[768,512]{1,0:T(8,128)(2,1)S(1)} %slice.97), channel_id=1, source_target_pairs={{0,64},{16,80},{32,96},{48,112},{1,65},{17,81},{33,97},{49,113},{2... | collective-permute-start | bytes 2359304 | tf_op jit(solution)/shard_map/ppermute | solution.py:347
  254.8 59.6 %collective-permute-start.25 = (bf16[768,512]{1,0:T(8,128)(2,1)S(1)}, bf16[768,512]{1,0:T(8,128)(2,1)S(1)}, u32[]{:S(2)}, u32[]{:S(2)}) collective-permute-start(bf16[768,512]{1,0:T(8,128)(2,1)S(1)} %slice.97), channel_id=1, source_target_pairs={{0,80},{16,96},{32,112},{1,81},{17,97},{33,113},{2,82},{18,98},{34... | collective-permute-start | bytes 2359304 | tf_op jit(solution)/shard_map/ppermute | solution.py:347
  274.4 60.1 %collective-permute-start.26 = (bf16[768,512]{1,0:T(8,128)(2,1)S(1)}, bf16[768,512]{1,0:T(8,128)(2,1)S(1)}, u32[]{:S(2)}, u32[]{:S(2)}) collective-permute-start(bf16[768,512]{1,0:T(8,128)(2,1)S(1)} %slice.97), channel_id=1, source_target_pairs={{0,96},{16,112},{1,97},{17,113},{2,98},{18,114},{3,99},{19,115},{4... | collective-permute-start | bytes 2359304 | tf_op jit(solution)/shard_map/ppermute | solution.py:347
  279.9 55.6 %collective-permute-start.27 = (bf16[768,512]{1,0:T(8,128)(2,1)S(1)}, bf16[768,512]{1,0:T(8,128)(2,1)S(1)}, u32[]{:S(2)}, u32[]{:S(2)}) collective-permute-start(bf16[768,512]{1,0:T(8,128)(2,1)S(1)} %slice.97), channel_id=1, source_target_pairs={{0,112},{1,113},{2,114},{3,115},{4,116},{5,117},{6,118},{7,119},{8... | collective-permute-start | bytes 2359304 | tf_op jit(solution)/shard_map/ppermute | solution.py:347
  380.5 18.7 %collective-permute-start.30 = (bf16[768,256]{1,0:T(8,128)(2,1)}, bf16[768,256]{1,0:T(8,128)(2,1)}, u32[]{:S(2)}, u32[]{:S(2)}) collective-permute-start(bf16[768,256]{1,0:T(8,128)(2,1)} %shard_map.138), channel_id=1, source_target_pairs={{0,12},{4,8},{8,4},{12,0},{1,13},{5,9},{9,5},{13,1},{2,14},{6,10},... | collective-permute-start | bytes 1179656 | tf_op jit(solution)/shard_map/ppermute | solution.py:137
  410.4 22.1 %collective-permute-start.32 = (bf16[192,1024]{1,0:T(8,128)(2,1)}, bf16[192,1024]{1,0:T(8,128)(2,1)}, u32[]{:S(2)}, u32[]{:S(2)}) collective-permute-start(bf16[192,1024]{1,0:T(8,128)(2,1)} %get-tuple-element.13), channel_id=1, source_target_pairs={{0,2},{1,3},{2,0},{3,1},{4,6},{5,7},{6,4},{7,5},{8,10},{9,11},{10,... | collective-permute-start | bytes 1179656 | tf_op jit(solution)/shard_map/ppermute | solution.py:65
  414.6 17.9 %collective-permute-start.33 = (bf16[192,1024]{1,0:T(8,128)(2,1)S(1)}, bf16[192,1024]{1,0:T(8,128)(2,1)}, u32[]{:S(2)}, u32[]{:S(2)}) collective-permute-start(bf16[192,1024]{1,0:T(8,128)(2,1)S(1)} %get-tuple-element.12), channel_id=1, source_target_pairs={{0,3},{1,0},{2,1},{3,2},{4,7},{5,4},{6,5},{7,6},{8,11},{9,8},{10,9... | collective-permute-start | bytes 1179656 | tf_op jit(solution)/shard_map/ppermute | solution.py:65
  (21 other events, 576.1 us)

commit v8 on v7

--- a/solution.py
+++ b/solution.py
@@ -195,21 +195,34 @@
     return scatter_permute(summed.astype(jnp.bfloat16), "col")
 
 
-def causal_attend(proj, blocks, place):
+def causal_attend(proj, blocks, shifts, place, carry=None, last=True):
     count = proj.shape[0]
     heads = proj.shape[1] // (3 * HD)
     steps = blocks.shape[0]
     scale = HD ** (-0.5)
-
-    def body(place_ref, q_ref, k_ref, v_ref, o_ref, peak_ref, mass_ref, acc_ref):
+    shift_table = jnp.asarray(shifts, jnp.int32)
+
+    def body(place_ref, shift_ref, q_ref, k_ref, v_ref, *refs):
+        if carry is None:
+            outs = refs[:-3]
+        else:
+            peak_in, mass_in, acc_in = refs[:3]
+            outs = refs[3:-3]
+        peak_ref, mass_ref, acc_ref = refs[-3:]
         step = pl.program_id(1)
+        shift = shift_ref[step]
         own = place_ref[0]
 
         @pl.when(step == 0)
         def _():
-            peak_ref[...] = jnp.full(peak_ref.shape, -1e30, jnp.float32)
-            mass_ref[...] = jnp.zeros(mass_ref.shape, jnp.float32)
-            acc_ref[...] = jnp.zeros(acc_ref.shape, jnp.float32)
+            if carry is None:
+                peak_ref[...] = jnp.full(peak_ref.shape, -1e30, jnp.float32)
+                mass_ref[...] = jnp.zeros(mass_ref.shape, jnp.float32)
+                acc_ref[...] = jnp.zeros(acc_ref.shape, jnp.float32)
+            else:
+                peak_ref[...] = peak_in[...]
+                mass_ref[...] = mass_in[...]
+                acc_ref[...] = acc_in[...]
 
         def fold(masked):
             scores = lax.dot_general(
@@ -231,40 +244,63 @@
                 weights.astype(jnp.bfloat16), v_ref[...], preferred_element_type=jnp.float32)
             peak_ref[...] = new
 
-        @pl.when(step < own)
+        @pl.when((shift > 0) & (shift <= own))
         def _():
             fold(False)
 
-        @pl.when(step == own)
+        @pl.when(shift == 0)
         def _():
             fold(True)
 
         @pl.when(step == steps - 1)
         def _():
-            o_ref[...] = (acc_ref[...] / mass_ref[...]).astype(o_ref.dtype)
-
+            if last:
+                outs[0][...] = (acc_ref[...] / mass_ref[...]).astype(outs[0].dtype)
+            else:
+                outs[0][...] = peak_ref[...]
+                outs[1][...] = mass_ref[...]
+                outs[2][...] = acc_ref[...]
+
+    state_specs = [
+        pl.BlockSpec((None, count, 1), lambda h, j, p, s: (h, 0, 0)),
+        pl.BlockSpec((None, count, 1), lambda h, j, p, s: (h, 0, 0)),
+        pl.BlockSpec((None, count, HD), lambda h, j, p, s: (h, 0, 0)),
+    ]
+    state_shapes = [
+        jax.ShapeDtypeStruct((heads, count, 1), jnp.float32),
+        jax.ShapeDtypeStruct((heads, count, 1), jnp.float32),
+        jax.ShapeDtypeStruct((heads, count, HD), jnp.float32),
+    ]
+    in_specs = [
+        pl.BlockSpec((count, HD), lambda h, j, p, s: (0, h)),
+        pl.BlockSpec((None, count, HD), lambda h, j, p, s: (j, 0, h)),
+        pl.BlockSpec((None, count, HD), lambda h, j, p, s: (j, 0, heads + h)),
+    ]
+    if carry is not None:
+        in_specs = in_specs + state_specs
+    if last:
+        out_specs = pl.BlockSpec((count, HD), lambda h, j, p, s: (0, h))
+        out_shape = jax.ShapeDtypeStruct((count, heads * HD), jnp.bfloat16)
+    else:
+        out_specs = state_specs
+        out_shape = state_shapes
     grid_spec = pltpu.PrefetchScalarGridSpec(
-        num_scalar_prefetch=1,
+        num_scalar_prefetch=2,
         grid=(heads, steps),
-        in_specs=[
-            pl.BlockSpec((count, HD), lambda h, j, p: (0, h)),
-            pl.BlockSpec((None, count, HD), lambda h, j, p: (p[0] - jnp.minimum(j, p[0]), 0, h)),
-            pl.BlockSpec(
-                (None, count, HD), lambda h, j, p: (p[0] - jnp.minimum(j, p[0]), 0, heads + h)
-            ),
-        ],
-        out_specs=pl.BlockSpec((count, HD), lambda h, j, p: (0, h)),
+        in_specs=in_specs,
+        out_specs=out_specs,
         scratch_shapes=[
             pltpu.VMEM((count, 1), jnp.float32),
             pltpu.VMEM((count, 1), jnp.float32),
             pltpu.VMEM((count, HD), jnp.float32),
         ],
     )
+    extra = () if carry is None else tuple(carry)
     return pl.pallas_call(
         body,
         grid_spec=grid_spec,
-        out_shape=jax.ShapeDtypeStruct((count, heads * HD), jnp.bfloat16),
-    )(place, proj, blocks, blocks)
+        out_shape=out_shape,
+    )(place, shift_table, proj, blocks, blocks, *extra)
 
 
 def per_device(
@@ -288,7 +324,7 @@
     width = vis_wq.shape[1]
     local = width // row_count
     margin = MAXIMG - 1
-    piece_ids = lax.all_gather(jnp.stack([vis_segment, vis_valid]), "col", axis=1, tiled=True)
+    piece_ids = gather_permute(jnp.stack([vis_segment, vis_valid], axis=1), "col").T
     piece_len = piece_ids.shape[1]
     framed_ids = with_halo(piece_ids, (("req", 1),), margin)
     total_slots = piece_len * lax.axis_size("req")
@@ -348,7 +384,14 @@
         for s in range(1, req_count)
     ]
     place = lax.axis_index("req").astype(jnp.int32).reshape(1)
-    dec_att = causal_attend(dec_proj, jnp.stack(earlier), place)
+    near = [s for s in range(0, req_count, 2)]
+    far = [s for s in range(1, req_count, 2)]
+    state = causal_attend(
+        dec_proj, jnp.stack([earlier[s] for s in near]), near, place, last=False
+    )
+    dec_att = causal_attend(
+        dec_proj, jnp.stack([earlier[s] for s in far]), far, place, carry=state
+    )
     return (mixed.astype(jnp.float32) + out_project_heads(dec_att, dec_wo)).astype(jnp.bfloat16)
 
 

time: 436 us -> 431 us (0.989)
  blocking collectives: 21 us -> 11.5 us
  waiting for transfers between devices: 210 us -> 201 us
  starting transfers between devices: 52.6 us -> 60 us
  other arithmetic: 21.4 us -> 27.6 us
  local copies, waits for them, and re-layouts: 55.6 us -> 50.1 us
    ppermute x10, waiting for transfers between devices: 76.8 us -> 62.4 us  [flip(): return lax.ppermute(values, axis, [(j, j ^ bit) for j in range(count)])]
    ppermute x2, waiting for transfers between devices: 1.7 us -> 11.2 us  [with_halo(): lax.ppermute(tail, axis, [(i, (i + 1) % count) for i in range(ends)])]
    all_gather x1 -> x0, blocking collectives: 8.7 us -> none  [per_device(): lax.all_gather(jnp.stack([vis_segment, vis_valid]), 'col', axis=1, tiled=...]
    another operation x3 -> x6, other arithmetic: 0.32 us -> 6.68 us  [the longest x1 3.2 us: per_device(): jnp.stack([earlier[s] for s in far])]
    ppermute x6 -> x9, starting transfers between devices: 7.33 us -> 13.3 us  [gather_permute(): lax.ppermute(values, axis, [(j, (j + s) % count) for j in range(count)])]
    unnamed x42 -> x40, local copies, waits for them, and re-layouts: 24.6 us -> 18.9 us
    pallas_call x1 -> x2, Pallas kernels: 42.9 us -> 47.1 us  [causal_attend(): pl.pallas_call(body, grid_spec=grid_spec, out_shape=out_shape)]
    ppermute x6 -> x9, waiting for transfers between devices: 27.5 us -> 26.8 us  [gather_permute(): lax.ppermute(values, axis, [(j, (j + s) % count) for j in range(count)])]
  transfers between devices with their start and end apart: 34 -> 37, of which waited for: 24 -> 20; matrix products, arithmetic and copies ran while one was open for 5% -> 7% of each run, Pallas kernels for 0% -> 7%
where the time goes in v8:
time: 431 us; the launch traced here: 430 us
  waiting for transfers between devices  201 us (47%)
  Pallas kernels  64.1 us (15%)
  starting transfers between devices  60 us (14%)
  local copies, waits for them, and re-layouts  50.1 us (12%)
  other arithmetic  27.6 us (6%)
  matrix products  14.1 us (3%)
  blocking collectives  11.5 us (3%)
    ppermute x7, waiting for transfers between devices, per_device(): lax.ppermute(keyvals, 'req', [(j, j + s) for j in range(req_count - s)])  68.4 us
    ppermute x10, waiting for transfers between devices, flip(): return lax.ppermute(values, axis, [(j, j ^ bit) for j in range(count)])  62.4 us
    pallas_call x2, Pallas kernels, causal_attend(): pl.pallas_call(body, grid_spec=grid_spec, out_shape=out_shape)  47.1 us
    ppermute x6, waiting for transfers between devices, scatter_permute(): lax.ppermute(chunk, axis, [(j, (j + s) % count) for j in range(count)])  27.1 us
    ppermute x9, waiting for transfers between devices, gather_permute(): lax.ppermute(values, axis, [(j, (j + s) % count) for j in range(count)])  26.8 us
    unnamed x40, local copies, waits for them, and re-layouts  18.9 us
    pallas_call x2, Pallas kernels, head_project(): pl.pallas_call(body, grid=(row_count,), in_specs=[pl.BlockSpec((count, de...  17.1 us
    ppermute x9, starting transfers between devices, gather_permute(): lax.ppermute(values, axis, [(j, (j + s) % count) for j in range(count)])  13.3 us
  transfers between devices with their start and end apart: 37, of which 20 were waited for; matrix products, arithmetic and copies ran while one was open for 7% of the time, Pallas kernels for 7%

profile of v8, /device:TPU:28, one launch (start us, length us, event | category | flops | bytes accessed | tf_op | source)
XLA Modules:
  0.0 429.5 jit_solution(2877120185124230358)
XLA Ops:
  6.5 5.7 %psum.14 = f32[128]{0:T(128)S(1)} all-reduce(f32[128]{0:T(128)S(1)} %fusion.27), channel_id=1, replica_groups=mesh['req'=8,'row'=4,'col'=4] {'row'}, use_global_device_ids=true, to_apply=%region_3.4 | all-reduce | flops 128 | bytes 1024 | tf_op jit(solution)/shard_map/psum | solution.py:39
  19.8 10.4 %collective-permute-done.5 = bf16[128,1024]{1,0:T(8,128)(2,1)S(1)} collective-permute-done((bf16[128,1024]{1,0:T(8,128)(2,1)S(1)}, bf16[128,1024]{1,0:T(8,128)(2,1)S(1)}, u32[]{:S(2)}, u32[]{:S(2)}) %collective-permute-start.5) | collective-permute-done | bytes 262176 | tf_op jit(solution)/shard_map/ppermute | solution.py:49
  39.3 7.7 %shard_map.154 = bf16[4,512,768]{2,1,0:T(8,128)(2,1)} custom-call(bf16[512,1024]{1,0:T(8,128)(2,1)} %constant_dynamic-slice_fusion.9.x_ref, bf16[1024,1024]{1,0:T(8,128)(2,1)} %refs_0_.2, bf16[1024,1024]{1,0:T(8,128)(2,1)} %refs_1_.2, bf16[1024,1024]{1,0:T(8,128)(2,1)} %refs_2_.2), custom_call_target="tpu_custom_call" | custom-call | tf_op jit(solution)/shard_map/pallas_call | solution.py:178
  64.2 6.1 %collective-permute-start.4 = (s32[2,255]{1,0:T(2,128)S(1)}, s32[2,255]{1,0:T(2,128)S(1)}, u32[]{:S(2)}, u32[]{:S(2)}) collective-permute-start(s32[2,255]{1,0:T(2,128)S(1)} %get-tuple-element.35), channel_id=1, source_target_pairs={{16,0},{32,16},{48,32},{64,48},{80,64},{96,80},{112,96},{17,1},{33... | collective-permute-start | bytes 6128 | tf_op jit(solution)/shard_map/ppermute | solution.py:23
  70.3 11.1 %collective-permute-done.3 = s32[2,255]{1,0:T(2,128)S(1)} collective-permute-done((s32[2,255]{1,0:T(2,128)S(1)}, s32[2,255]{1,0:T(2,128)S(1)}, u32[]{:S(2)}, u32[]{:S(2)}) %collective-permute-start.3) | collective-permute-done | bytes 2072 | tf_op jit(solution)/shard_map/ppermute | solution.py:21
  85.3 6.8 %collective-permute-start.11 = (bf16[2,255,256]{1,2,0:T(8,128)(2,1)}, bf16[2,255,256]{1,2,0:T(8,128)(2,1)}, u32[]{:S(2)}, u32[]{:S(2)}) collective-permute-start(bf16[2,255,256]{1,2,0:T(8,128)(2,1)} %get-tuple-element.31), channel_id=1, source_target_pairs={{16,0},{32,16},{48,32},{64,48},{80,64},{96,80},{112,96},{17,1},{33... | collective-permute-start | bytes 783368 | tf_op jit(solution)/shard_map/ppermute | solution.py:23
  107.5 6.0 %collective-permute-done.14 = bf16[512,256]{1,0:T(8,128)(2,1)S(1)} collective-permute-done((bf16[512,256]{1,0:T(8,128)(2,1)S(1)}, bf16[512,256]{1,0:T(8,128)(2,1)S(1)}, u32[]{:S(2)}, u32[]{:S(2)}) %collective-permute-start.14) | collective-permute-done | bytes 262176 | tf_op jit(solution)/shard_map/ppermute | solution.py:137
  113.5 5.1 %collective-permute-done.13 = bf16[512,256]{1,0:T(8,128)(2,1)S(1)} collective-permute-done((bf16[512,256]{1,0:T(8,128)(2,1)S(1)}, bf16[512,256]{1,0:T(8,128)(2,1)S(1)}, u32[]{:S(2)}, u32[]{:S(2)}) %collective-permute-start.13) | collective-permute-done | bytes 262176 | tf_op jit(solution)/shard_map/ppermute | solution.py:137
  132.2 9.6 %collective-permute-done.15 = bf16[128,1024]{1,0:T(8,128)(2,1)} collective-permute-done((bf16[128,1024]{1,0:T(8,128)(2,1)}, bf16[128,1024]{1,0:T(8,128)(2,1)}, u32[]{:S(2)}, u32[]{:S(2)}) %collective-permute-start.15) | collective-permute-done | bytes 262176 | tf_op jit(solution)/shard_map/ppermute | solution.py:65
  143.8 7.9 %collective-permute-start.18 = (bf16[128,1024]{1,0:T(8,128)(2,1)}, bf16[128,1024]{1,0:T(8,128)(2,1)S(1)}, u32[]{:S(2)}, u32[]{:S(2)}) collective-permute-start(bf16[128,1024]{1,0:T(8,128)(2,1)} %fusion.30), channel_id=1, source_target_pairs={{1,0},{2,1},{3,2},{16,3},{17,16},{18,17},{19,18},{32,19},{33,32},{... | collective-permute-start | bytes 786440 | tf_op jit(solution)/shard_map/ppermute | solution.py:33
  159.0 5.8 %psum.15 = f32[192]{0:T(256)S(1)} all-reduce(f32[192]{0:T(256)S(1)} %get-tuple-element.40), channel_id=1, replica_groups=mesh['req'=8,'row'=4,'col'=4] {'row'}, use_global_device_ids=true, to_apply=%region_7.8 | all-reduce | flops 192 | bytes 1536 | tf_op jit(solution)/shard_map/psum | solution.py:39
  167.9 10.2 %collective-permute-done.19 = bf16[192,1024]{1,0:T(8,128)(2,1)S(1)} collective-permute-done((bf16[192,1024]{1,0:T(8,128)(2,1)}, bf16[192,1024]{1,0:T(8,128)(2,1)S(1)}, u32[]{:S(2)}, u32[]{:S(2)}) %collective-permute-start.19) | collective-permute-done | bytes 393248 | tf_op jit(solution)/shard_map/ppermute | solution.py:49
  181.5 5.3 %collective-permute-done.21 = bf16[192,1024]{1,0:T(8,128)(2,1)} collective-permute-done((bf16[192,1024]{1,0:T(8,128)(2,1)}, bf16[192,1024]{1,0:T(8,128)(2,1)}, u32[]{:S(2)}, u32[]{:S(2)}) %collective-permute-start.21) | collective-permute-done | bytes 393248 | tf_op jit(solution)/shard_map/ppermute | solution.py:49
  197.5 9.4 %shard_map.155 = bf16[4,768,768]{2,1,0:T(8,128)(2,1)} custom-call(bf16[768,1024]{1,0:T(8,128)(2,1)} %constant_dynamic-slice_fusion.3.x_ref, bf16[1024,1024]{1,0:T(8,128)(2,1)} %refs_0_.3, bf16[1024,1024]{1,0:T(8,128)(2,1)} %refs_1_.3, bf16[1024,1024]{1,0:T(8,128)(2,1)} %refs_2_.3), custom_call_target="tpu_custom_call" | custom-call | tf_op jit(solution)/shard_map/pallas_call | solution.py:178
  208.9 4.5 %collective-permute-done.22 = bf16[2,768,768]{2,1,0:T(8,128)(2,1)S(1)} collective-permute-done((bf16[2,768,768]{2,1,0:T(8,128)(2,1)S(1)}, bf16[2,768,768]{2,1,0:T(8,128)(2,1)S(1)}, u32[]{:S(2)}, u32[]{:S(2)}) %collective-permute-start.22) | collective-permute-done | bytes 2359328 | tf_op jit(solution)/shard_map/ppermute | solution.py:137
  214.6 27.6 %collective-permute-done.23 = bf16[768,768]{1,0:T(8,128)(2,1)S(1)} collective-permute-done((bf16[768,768]{1,0:T(8,128)(2,1)S(1)}, bf16[768,768]{1,0:T(8,128)(2,1)S(1)}, u32[]{:S(2)}, u32[]{:S(2)}) %collective-permute-start.23) | collective-permute-done | bytes 1179680 | tf_op jit(solution)/shard_map/ppermute | solution.py:137
  250.1 55.0 %collective-permute-done.29 = bf16[768,512]{1,0:T(8,128)(2,1)S(1)} collective-permute-done((bf16[768,512]{1,0:T(8,128)(2,1)}, bf16[768,512]{1,0:T(8,128)(2,1)S(1)}, u32[]{:S(2)}, u32[]{:S(2)}) %collective-permute-start.29) | collective-permute-done | bytes 786464 | tf_op jit(solution)/shard_map/ppermute | solution.py:383
  308.5 13.4 %collective-permute-done.30 = bf16[768,512]{1,0:T(8,128)(2,1)S(1)} collective-permute-done((bf16[768,512]{1,0:T(8,128)(2,1)}, bf16[768,512]{1,0:T(8,128)(2,1)S(1)}, u32[]{:S(2)}, u32[]{:S(2)}) %collective-permute-start.30) | collective-permute-done | bytes 786464 | tf_op jit(solution)/shard_map/ppermute | solution.py:383
  323.7 22.8 %shard_map.156 = (f32[2,768,1]{2,1,0:T(8,128)}, f32[2,768,1]{2,1,0:T(8,128)}, f32[2,768,128]{2,1,0:T(8,128)}) custom-call(s32[1]{0:T(128)} %bitcast.29.place_ref, s32[4]{0:T(128)} %iota_multiply_fusion.shift_ref, bf16[768,768]{1,0:T(8,128)(2,1)} %copy-done.2, bf16[4,768,512]{2,1,0:T(8,128)(2,1)} %pad_maximum_fusion.1.k_ref.v_ref, ...), custom_call_target="tpu_custom_call" | custom-call | tf_op jit(solution)/shard_map/pallas_call | solution.py:299
  349.7 24.3 %shard_map.157 = bf16[768,256]{1,0:T(8,128)(2,1)} custom-call(s32[1]{0:T(128)} %bitcast.29.place_ref, s32[4]{0:T(128)} %constant.208.clone.shift_ref, bf16[768,768]{1,0:T(8,128)(2,1)} %copy-done.2, bf16[4,768,512]{2,1,0:T(8,128)(2,1)} %pad_maximum_fusion.k_ref.v_ref, bf16[4,768,512]{2,1,0:T(8,128)(2,1)} %pad_maximum_fusion.k_ref.v_ref, ...), custom_call_target="tpu_custom_call" | custom-call | tf_op jit(solution)/shard_map/pallas_call | solution.py:299
  375.9 9.5 %collective-permute-done.33 = bf16[768,256]{1,0:T(8,128)(2,1)S(1)} collective-permute-done((bf16[768,256]{1,0:T(8,128)(2,1)}, bf16[768,256]{1,0:T(8,128)(2,1)S(1)}, u32[]{:S(2)}, u32[]{:S(2)}) %collective-permute-start.33) | collective-permute-done | bytes 393248 | tf_op jit(solution)/shard_map/ppermute | solution.py:137
  385.3 8.8 %collective-permute-done.32 = bf16[768,256]{1,0:T(8,128)(2,1)} collective-permute-done((bf16[768,256]{1,0:T(8,128)(2,1)}, bf16[768,256]{1,0:T(8,128)(2,1)}, u32[]{:S(2)}, u32[]{:S(2)}) %collective-permute-start.32) | collective-permute-done | bytes 393248 | tf_op jit(solution)/shard_map/ppermute | solution.py:137
  409.6 8.4 %collective-permute-done.34 = bf16[192,1024]{1,0:T(8,128)(2,1)} collective-permute-done((bf16[192,1024]{1,0:T(8,128)(2,1)}, bf16[192,1024]{1,0:T(8,128)(2,1)}, u32[]{:S(2)}, u32[]{:S(2)}) %collective-permute-start.34) | collective-permute-done | bytes 393248 | tf_op jit(solution)/shard_map/ppermute | solution.py:65
  417.9 7.5 %collective-permute-done.36 = bf16[192,1024]{1,0:T(8,128)(2,1)} collective-permute-done((bf16[192,1024]{1,0:T(8,128)(2,1)}, bf16[192,1024]{1,0:T(8,128)(2,1)}, u32[]{:S(2)}, u32[]{:S(2)}) %collective-permute-start.36) | collective-permute-done | bytes 393248 | tf_op jit(solution)/shard_map/ppermute | solution.py:65
  (173 shorter events, 140.1 us)
Async XLA Ops:
  0.8 52.8 %collective-permute-start.1 = (s32[128,2]{0,1:T(2,128)S(1)}, s32[128,2]{0,1:T(2,128)S(1)}, u32[]{:S(2)}, u32[]{:S(2)}) collective-permute-start(s32[128,2]{0,1:T(2,128)S(1)} %get-tuple-element.36), channel_id=1, source_target_pairs={{0,2},{1,3},{2,0},{3,1},{4,6},{5,7},{6,4},{7,5},{8,10},{9,11},{10,... | collective-permute-start | bytes 3080 | tf_op jit(solution)/shard_map/ppermute | solution.py:49
  4.7 48.9 %collective-permute-start = (s32[128,2]{0,1:T(2,128)S(1)}, s32[128,2]{0,1:T(2,128)S(1)}, u32[]{:S(2)}, u32[]{:S(2)}) collective-permute-start(s32[128,2]{0,1:T(2,128)S(1)} %get-tuple-element.36), channel_id=1, source_target_pairs={{0,3},{1,0},{2,1},{3,2},{4,7},{5,4},{6,5},{7,6},{8,11},{9,8},{10,9... | collective-permute-start | bytes 3080 | tf_op jit(solution)/shard_map/ppermute | solution.py:49
  14.7 18.6 %collective-permute-start.7 = (bf16[128,1024]{1,0:T(8,128)(2,1)S(1)}, bf16[128,1024]{1,0:T(8,128)(2,1)S(1)}, u32[]{:S(2)}, u32[]{:S(2)}) collective-permute-start(bf16[128,1024]{1,0:T(8,128)(2,1)S(1)} %get-tuple-element.14), channel_id=1, source_target_pairs={{0,1},{1,2},{2,3},{3,0},{4,5},{5,6},{6,7},{7,4},{8,9},{9,10},{10,1... | collective-permute-start | bytes 786440 | tf_op jit(solution)/shard_map/ppermute | solution.py:49
  16.0 16.6 %collective-permute-start.6 = (bf16[128,1024]{1,0:T(8,128)(2,1)S(1)}, bf16[128,1024]{1,0:T(8,128)(2,1)S(1)}, u32[]{:S(2)}, u32[]{:S(2)}) collective-permute-start(bf16[128,1024]{1,0:T(8,128)(2,1)S(1)} %get-tuple-element.14), channel_id=1, source_target_pairs={{0,2},{1,3},{2,0},{3,1},{4,6},{5,7},{6,4},{7,5},{8,10},{9,11},{10,... | collective-permute-start | bytes 786440 | tf_op jit(solution)/shard_map/ppermute | solution.py:49
  30.2 23.4 %collective-permute-start.2 = (s32[128,2]{0,1:T(2,128)S(1)}, s32[128,2]{0,1:T(2,128)S(1)}, u32[]{:S(2)}, u32[]{:S(2)}) collective-permute-start(s32[128,2]{0,1:T(2,128)S(1)} %get-tuple-element.36), channel_id=1, source_target_pairs={{0,1},{1,2},{2,3},{3,0},{4,5},{5,6},{6,7},{7,4},{8,9},{9,10},{10,1... | collective-permute-start | bytes 3080 | tf_op jit(solution)/shard_map/ppermute | solution.py:49
  61.6 20.0 %collective-permute-start.9 = (bf16[512,768]{0,1:T(8,128)(2,1)}, bf16[512,768]{0,1:T(8,128)(2,1)S(1)}, u32[]{:S(2)}, u32[]{:S(2)}) collective-permute-start(bf16[512,768]{0,1:T(8,128)(2,1)} %dynamic-slice_bitcast_fusion.2), channel_id=1, source_target_pairs={{0,8},{4,12},{8,0},{12,4},{1,9},{5,13},{9,1},{13,5},{2,10},{6,14},... | collective-permute-start | bytes 2359304 | tf_op jit(solution)/shard_map/ppermute | solution.py:137
  62.9 18.6 %collective-permute-start.3 = (s32[2,255]{1,0:T(2,128)S(1)}, s32[2,255]{1,0:T(2,128)S(1)}, u32[]{:S(2)}, u32[]{:S(2)}) collective-permute-start(s32[2,255]{1,0:T(2,128)S(1)} %get-tuple-element.34), channel_id=1, source_target_pairs={{0,16},{16,32},{32,48},{48,64},{64,80},{80,96},{96,112},{1,17},{17... | collective-permute-start | bytes 6128 | tf_op jit(solution)/shard_map/ppermute | solution.py:21
  64.2 17.3 %collective-permute-start.4 = (s32[2,255]{1,0:T(2,128)S(1)}, s32[2,255]{1,0:T(2,128)S(1)}, u32[]{:S(2)}, u32[]{:S(2)}) collective-permute-start(s32[2,255]{1,0:T(2,128)S(1)} %get-tuple-element.35), channel_id=1, source_target_pairs={{16,0},{32,16},{48,32},{64,48},{80,64},{96,80},{112,96},{17,1},{33... | collective-permute-start | bytes 6128 | tf_op jit(solution)/shard_map/ppermute | solution.py:23
  126.3 15.5 %collective-permute-start.15 = (bf16[128,1024]{1,0:T(8,128)(2,1)}, bf16[128,1024]{1,0:T(8,128)(2,1)}, u32[]{:S(2)}, u32[]{:S(2)}) collective-permute-start(bf16[128,1024]{1,0:T(8,128)(2,1)} %get-tuple-element.22), channel_id=1, source_target_pairs={{0,1},{1,2},{2,3},{3,0},{4,5},{5,6},{6,7},{7,4},{8,9},{9,10},{10,1... | collective-permute-start | bytes 786440 | tf_op jit(solution)/shard_map/ppermute | solution.py:65
  126.9 14.8 %collective-permute-start.17 = (bf16[128,1024]{1,0:T(8,128)(2,1)}, bf16[128,1024]{1,0:T(8,128)(2,1)}, u32[]{:S(2)}, u32[]{:S(2)}) collective-permute-start(bf16[128,1024]{1,0:T(8,128)(2,1)} %get-tuple-element.23), channel_id=1, source_target_pairs={{0,3},{1,0},{2,1},{3,2},{4,7},{5,4},{6,5},{7,6},{8,11},{9,8},{10,9... | collective-permute-start | bytes 786440 | tf_op jit(solution)/shard_map/ppermute | solution.py:65
  165.9 13.9 %collective-permute-start.20 = (bf16[192,1024]{1,0:T(8,128)(2,1)}, bf16[192,1024]{1,0:T(8,128)(2,1)}, u32[]{:S(2)}, u32[]{:S(2)}) collective-permute-start(bf16[192,1024]{1,0:T(8,128)(2,1)} %get-tuple-element.12), channel_id=1, source_target_pairs={{0,2},{1,3},{2,0},{3,1},{4,6},{5,7},{6,4},{7,5},{8,10},{9,11},{10,... | collective-permute-start | bytes 1179656 | tf_op jit(solution)/shard_map/ppermute | solution.py:49
  165.9 21.0 %collective-permute-start.21 = (bf16[192,1024]{1,0:T(8,128)(2,1)}, bf16[192,1024]{1,0:T(8,128)(2,1)}, u32[]{:S(2)}, u32[]{:S(2)}) collective-permute-start(bf16[192,1024]{1,0:T(8,128)(2,1)} %get-tuple-element.12), channel_id=1, source_target_pairs={{0,1},{1,2},{2,3},{3,0},{4,5},{5,6},{6,7},{7,4},{8,9},{9,10},{10,1... | collective-permute-start | bytes 1179656 | tf_op jit(solution)/shard_map/ppermute | solution.py:49
  214.1 28.1 %collective-permute-start.23 = (bf16[768,768]{1,0:T(8,128)(2,1)S(1)}, bf16[768,768]{1,0:T(8,128)(2,1)S(1)}, u32[]{:S(2)}, u32[]{:S(2)}) collective-permute-start(bf16[768,768]{1,0:T(8,128)(2,1)S(1)} %dynamic-slice_bitcast_fusion.1), channel_id=1, source_target_pairs={{0,8},{4,12},{8,0},{12,4},{1,9},{5,13},{9,1},{13,5},{2,10},{6,14},... | collective-permute-start | bytes 3538952 | tf_op jit(solution)/shard_map/ppermute | solution.py:137
  243.6 61.5 %collective-permute-start.29 = (bf16[768,512]{1,0:T(8,128)(2,1)}, bf16[768,512]{1,0:T(8,128)(2,1)S(1)}, u32[]{:S(2)}, u32[]{:S(2)}) collective-permute-start(bf16[768,512]{1,0:T(8,128)(2,1)} %get-tuple-element.21), channel_id=1, source_target_pairs={{0,64},{16,80},{32,96},{48,112},{1,65},{17,81},{33,97},{49,113},{2... | collective-permute-start | bytes 2359304 | tf_op jit(solution)/shard_map/ppermute | solution.py:383
  244.9 61.5 %collective-permute-start.28 = (bf16[768,512]{1,0:T(8,128)(2,1)}, bf16[768,512]{1,0:T(8,128)(2,1)S(1)}, u32[]{:S(2)}, u32[]{:S(2)}) collective-permute-start(bf16[768,512]{1,0:T(8,128)(2,1)} %get-tuple-element.21), channel_id=1, source_target_pairs={{0,32},{16,48},{32,64},{48,80},{64,96},{80,112},{1,33},{17,49},{33... | collective-permute-start | bytes 2359304 | tf_op jit(solution)/shard_map/ppermute | solution.py:383
  246.2 75.7 %collective-permute-start.30 = (bf16[768,512]{1,0:T(8,128)(2,1)}, bf16[768,512]{1,0:T(8,128)(2,1)S(1)}, u32[]{:S(2)}, u32[]{:S(2)}) collective-permute-start(bf16[768,512]{1,0:T(8,128)(2,1)} %get-tuple-element.21), channel_id=1, source_target_pairs={{0,96},{16,112},{1,97},{17,113},{2,98},{18,114},{3,99},{19,115},{4... | collective-permute-start | bytes 2359304 | tf_op jit(solution)/shard_map/ppermute | solution.py:383
  247.5 99.0 %collective-permute-start.27 = (bf16[768,512]{1,0:T(8,128)(2,1)}, bf16[768,512]{1,0:T(8,128)(2,1)}, u32[]{:S(2)}, u32[]{:S(2)}) collective-permute-start(bf16[768,512]{1,0:T(8,128)(2,1)} %get-tuple-element.21), channel_id=1, source_target_pairs={{0,112},{1,113},{2,114},{3,115},{4,116},{5,117},{6,118},{7,119},{8... | collective-permute-start | bytes 2359304 | tf_op jit(solution)/shard_map/ppermute | solution.py:383
  248.8 97.7 %collective-permute-start.26 = (bf16[768,512]{1,0:T(8,128)(2,1)}, bf16[768,512]{1,0:T(8,128)(2,1)}, u32[]{:S(2)}, u32[]{:S(2)}) collective-permute-start(bf16[768,512]{1,0:T(8,128)(2,1)} %get-tuple-element.21), channel_id=1, source_target_pairs={{0,80},{16,96},{32,112},{1,81},{17,97},{33,113},{2,82},{18,98},{34... | collective-permute-start | bytes 2359304 | tf_op jit(solution)/shard_map/ppermute | solution.py:383
  305.1 41.3 %collective-permute-start.25 = (bf16[768,512]{1,0:T(8,128)(2,1)}, bf16[768,512]{1,0:T(8,128)(2,1)}, u32[]{:S(2)}, u32[]{:S(2)}) collective-permute-start(bf16[768,512]{1,0:T(8,128)(2,1)} %get-tuple-element.21), channel_id=1, source_target_pairs={{0,48},{16,64},{32,80},{48,96},{64,112},{1,49},{17,65},{33,81},{49... | collective-permute-start | bytes 2359304 | tf_op jit(solution)/shard_map/ppermute | solution.py:383
  306.4 40.1 %collective-permute-start.24 = (bf16[768,512]{1,0:T(8,128)(2,1)}, bf16[768,512]{1,0:T(8,128)(2,1)}, u32[]{:S(2)}, u32[]{:S(2)}) collective-permute-start(bf16[768,512]{1,0:T(8,128)(2,1)} %get-tuple-element.21), channel_id=1, source_target_pairs={{0,16},{16,32},{32,48},{48,64},{64,80},{80,96},{96,112},{1,17},{17... | collective-permute-start | bytes 2359304 | tf_op jit(solution)/shard_map/ppermute | solution.py:383
  375.4 18.8 %collective-permute-start.32 = (bf16[768,256]{1,0:T(8,128)(2,1)}, bf16[768,256]{1,0:T(8,128)(2,1)}, u32[]{:S(2)}, u32[]{:S(2)}) collective-permute-start(bf16[768,256]{1,0:T(8,128)(2,1)} %shard_map.157), channel_id=1, source_target_pairs={{0,8},{4,12},{8,0},{12,4},{1,9},{5,13},{9,1},{13,5},{2,10},{6,14},... | collective-permute-start | bytes 1179656 | tf_op jit(solution)/shard_map/ppermute | solution.py:137
  375.8 18.4 %collective-permute-start.31 = (bf16[768,256]{1,0:T(8,128)(2,1)}, bf16[768,256]{1,0:T(8,128)(2,1)}, u32[]{:S(2)}, u32[]{:S(2)}) collective-permute-start(bf16[768,256]{1,0:T(8,128)(2,1)} %shard_map.157), channel_id=1, source_target_pairs={{0,4},{4,0},{8,12},{12,8},{1,5},{5,1},{9,13},{13,9},{2,6},{6,2},{1... | collective-permute-start | bytes 1179656 | tf_op jit(solution)/shard_map/ppermute | solution.py:137
  405.4 20.0 %collective-permute-start.36 = (bf16[192,1024]{1,0:T(8,128)(2,1)}, bf16[192,1024]{1,0:T(8,128)(2,1)}, u32[]{:S(2)}, u32[]{:S(2)}) collective-permute-start(bf16[192,1024]{1,0:T(8,128)(2,1)} %get-tuple-element.18), channel_id=1, source_target_pairs={{0,3},{1,0},{2,1},{3,2},{4,7},{5,4},{6,5},{7,6},{8,11},{9,8},{10,9... | collective-permute-start | bytes 1179656 | tf_op jit(solution)/shard_map/ppermute | solution.py:65
  408.6 18.5 %collective-permute-start.35 = (bf16[192,1024]{1,0:T(8,128)(2,1)S(1)}, bf16[192,1024]{1,0:T(8,128)(2,1)}, u32[]{:S(2)}, u32[]{:S(2)}) collective-permute-start(bf16[192,1024]{1,0:T(8,128)(2,1)S(1)} %get-tuple-element.19), channel_id=1, source_target_pairs={{0,2},{1,3},{2,0},{3,1},{4,6},{5,7},{6,4},{7,5},{8,10},{9,11},{10,... | collective-permute-start | bytes 1179656 | tf_op jit(solution)/shard_map/ppermute | solution.py:65
  (24 other events, 672.5 us)

commit v9 on v8

--- a/solution.py
+++ b/solution.py
@@ -36,7 +36,8 @@
 def norm_local(values, gain):
     floats = values.astype(jnp.float32)
     squares = jnp.sum(floats * floats, axis=-1)
-    totals = lax.psum(squares, "row")
+    totals = squares + flip(squares, "row", 1)
+    totals = totals + flip(totals, "row", 2)
     factor = lax.rsqrt(totals / D + 1e-05)
     return (floats * factor[:, None] * gain.astype(jnp.float32)[None, :]).astype(jnp.bfloat16)
 
@@ -162,28 +163,47 @@
     return jnp.take(stacked, order, axis=0)
 
 
-def head_project(values, weights):
+def received(values, axis):
+    count = lax.axis_size(axis)
+    return [values] + [
+        lax.ppermute(values, axis, [(j, (j + s) % count) for j in range(count)])
+        for s in range(1, count)
+    ]
+
+
+def head_project(pieces, weights, axis):
     row_count = lax.axis_size("row")
-    count, depth = values.shape
+    count = len(pieces)
+    rows, depth = pieces[0].shape
     part = weights[0].shape[1] // row_count
     groups = len(weights)
-
-    def body(x_ref, *refs):
+    index = lax.axis_index(axis).astype(jnp.int32).reshape(1)
+
+    def body(index_ref, *refs):
+        x_refs = refs[:count]
+        w_refs = refs[count : count + groups]
         o_ref = refs[-1]
-        for g in range(groups):
-            o_ref[0, :, g * part : (g + 1) * part] = jnp.dot(
-                x_ref[...], refs[g][...], preferred_element_type=jnp.float32
-            ).astype(o_ref.dtype)
-
+        own = index_ref[0]
+        for s in range(count):
+            start = pl.multiple_of(((own - s + count) % count) * rows, 8)
+            for g in range(groups):
+                o_ref[0, pl.ds(start, rows), g * part : (g + 1) * part] = jnp.dot(
+                    x_refs[s][...], w_refs[g][...], preferred_element_type=jnp.float32
+                ).astype(o_ref.dtype)
+
+    grid_spec = pltpu.PrefetchScalarGridSpec(
+        num_scalar_prefetch=1,
+        grid=(row_count,),
+        in_specs=[pl.BlockSpec((rows, depth), lambda r, i: (0, 0)) for _ in pieces]
+        + [pl.BlockSpec((depth, part), lambda r, i: (0, r)) for _ in weights],
+        out_specs=pl.BlockSpec((1, count * rows, groups * part), lambda r, i: (r, 0, 0)),
+    )
     summed = pl.pallas_call(
         body,
-        grid=(row_count,),
-        in_specs=[pl.BlockSpec((count, depth), lambda r: (0, 0))]
-        + [pl.BlockSpec((depth, part), lambda r: (0, r)) for _ in weights],
-        out_specs=pl.BlockSpec((1, count, groups * part), lambda r: (r, 0, 0)),
-        out_shape=jax.ShapeDtypeStruct((row_count, count, groups * part), jnp.bfloat16),
-    )(values, *weights)
-    summed = summed.reshape(row_count * count, groups * part)
+        grid_spec=grid_spec,
+        out_shape=jax.ShapeDtypeStruct((row_count, count * rows, groups * part), jnp.bfloat16),
+    )(index, *pieces, *weights)
+    summed = summed.reshape(row_count * count * rows, groups * part)
     return scatter_row(summed)
 
 
@@ -341,8 +361,8 @@
     begins = begins | (key_slots == 0)
     image_first = lax.cummax(jnp.where(begins, key_slots, window_start), axis=0)
     target_window = image_first * prompt_total // total_slots + key_slots - image_first
-    vis_cols = gather_cols(norm_local(vis_embed, vis_gain))
-    vis_proj = head_project(vis_cols, (vis_wq, vis_wk, vis_wv))
+    vis_cols = received(norm_local(vis_embed, vis_gain), "col")
+    vis_proj = head_project(vis_cols, (vis_wq, vis_wk, vis_wv), "col")
     vis_pairs = jnp.stack([vis_proj[:, local : 2 * local], vis_proj[:, 2 * local :]])
     framed = with_halo(vis_pairs, (("req", 1),), margin)
     query_local = margin + jnp.arange(piece_len, dtype=jnp.int32)
@@ -374,9 +394,9 @@
     )
     carried = jnp.dot(onehot, near_rows, preferred_element_type=jnp.float32)
     mixed = (text_embed.astype(jnp.float32) + carried).astype(jnp.bfloat16)
-    dec_cols = gather_cols(norm_local(mixed, dec_gain))
-    dec_proj = head_project(dec_cols, (dec_wq, dec_wk, dec_wv))
-    dec_rows = dec_cols.shape[0]
+    dec_cols = received(norm_local(mixed, dec_gain), "col")
+    dec_proj = head_project(dec_cols, (dec_wq, dec_wk, dec_wv), "col")
+    dec_rows = dec_proj.shape[0]
     keyvals = dec_proj[:, local:]
     req_count = lax.axis_size("req")
     earlier = [keyvals] + [

time: 431 us -> 403 us (0.935)
  local copies, waits for them, and re-layouts: 50.1 us -> 30.9 us
  blocking collectives: 11.5 us -> 0 us
  waiting for transfers between devices: 201 us -> 207 us
    ppermute x0 -> x6, waiting for transfers between devices: none -> 27.9 us  [received(): lax.ppermute(values, axis, [(j, (j + s) % count) for j in range(count)])]
    ppermute x9 -> x3, waiting for transfers between devices: 26.8 us -> 0.01 us  [gather_permute(): lax.ppermute(values, axis, [(j, (j + s) % count) for j in range(count)])]
    unnamed x40 -> x42, local copies, waits for them, and re-layouts: 18.9 us -> 7.2 us
    psum x2 -> x0, blocking collectives: 11.5 us -> none  [norm_local(): totals = lax.psum(squares, 'row')]
    ppermute x9 -> x3, starting transfers between devices: 13.3 us -> 5.45 us  [gather_permute(): lax.ppermute(values, axis, [(j, (j + s) % count) for j in range(count)])]
    ppermute x0 -> x6, starting transfers between devices: none -> 5.94 us  [received(): lax.ppermute(values, axis, [(j, (j + s) % count) for j in range(count)])]
    dynamic_slice x2 -> x0, local copies, waits for them, and re-layouts: 4.98 us -> none  [gather_permute(): return lax.dynamic_slice_in_dim(twice, start, count * rows, axis=0)]
    ppermute x10 -> x14, waiting for transfers between devices: 62.4 us -> 66.1 us  [flip(): return lax.ppermute(values, axis, [(j, j ^ bit) for j in range(count)])]
  transfers between devices with their start and end apart: 37 -> 41, of which waited for: 20 -> 26; matrix products, arithmetic and copies ran while one was open for 7% -> 5% of each run, Pallas kernels for 7% -> 8%
where the time goes in v9:
time: 403 us; the launch traced here: 402 us
  waiting for transfers between devices  207 us (51%)
  Pallas kernels  63.8 us (16%)
  starting transfers between devices  59.2 us (15%)
  local copies, waits for them, and re-layouts  30.9 us (8%)
  other arithmetic  26.1 us (6%)
  matrix products  14.1 us (3%)
    ppermute x7, waiting for transfers between devices, per_device(): lax.ppermute(keyvals, 'req', [(j, j + s) for j in range(req_count - s)])  68.9 us
    ppermute x14, waiting for transfers between devices, flip(): return lax.ppermute(values, axis, [(j, j ^ bit) for j in range(count)])  66.1 us
    pallas_call x2, Pallas kernels, causal_attend(): pl.pallas_call(body, grid_spec=grid_spec, out_shape=out_shape)  47.1 us
    ppermute x6, waiting for transfers between devices, received(): lax.ppermute(values, axis, [(j, (j + s) % count) for j in range(count)])  27.9 us
    ppermute x6, waiting for transfers between devices, scatter_permute(): lax.ppermute(chunk, axis, [(j, (j + s) % count) for j in range(count)])  27.8 us
    pallas_call x2, Pallas kernels, head_project(): pl.pallas_call(body, grid_spec=grid_spec, out_shape=jax.ShapeDtypeStruct(...  16.7 us
    ppermute x2, starting transfers between devices, with_halo(): lax.ppermute(head, axis, [((i + 1) % count, i) for i in range(ends)])  12.8 us
    ppermute x2, waiting for transfers between devices, with_halo(): lax.ppermute(tail, axis, [(i, (i + 1) % count) for i in range(ends)])  11.2 us
  transfers between devices with their start and end apart: 41, of which 26 were waited for; matrix products, arithmetic and copies ran while one was open for 5% of the time, Pallas kernels for 8%

profile of v9, /device:TPU:28, one launch (start us, length us, event | category | flops | bytes accessed | tf_op | source)
XLA Modules:
  0.0 402.1 jit_solution(9513139483230343028)
XLA Ops:
  3.6 3.9 collective-permute-start.1
  13.9 5.4 %collective-permute-done.9.refs_3_ = bf16[128,1024]{1,0:T(8,128)(2,1)S(1)} collective-permute-done((bf16[128,1024]{1,0:T(8,128)(2,1)S(1)}, bf16[128,1024]{1,0:T(8,128)(2,1)S(1)}, u32[]{:S(2)}, u32[]{:S(2)}) %collective-permute-start.9) | collective-permute-done | bytes 262176 | tf_op jit(solution)/shard_map/ppermute | solution.py:169
  26.0 7.6 %shard_map.154 = bf16[4,512,768]{2,1,0:T(8,128)(2,1)} custom-call(s32[1]{0:T(128)} %bitcast.7.index_ref, bf16[128,1024]{1,0:T(8,128)(2,1)} %copy-done.7, bf16[128,1024]{1,0:T(8,128)(2,1)} %copy-done.14, bf16[128,1024]{1,0:T(8,128)(2,1)} %copy-done.13, bf16[128,1024]{1,0:T(8,128)(2,1)} %copy-done.12, bf16[1024,1024]{1,0:T(8,128)(2,1)} %refs_4_.2, ...), custom_call_target="tpu_custom_call" | custom-call | tf_op jit(solution)/shard_map/pallas_call | solution.py:201
  50.7 6.1 %collective-permute-start.4 = (s32[2,255]{1,0:T(2,128)S(1)}, s32[2,255]{1,0:T(2,128)S(1)}, u32[]{:S(2)}, u32[]{:S(2)}) collective-permute-start(s32[2,255]{1,0:T(2,128)S(1)} %get-tuple-element.31), channel_id=1, source_target_pairs={{16,0},{32,16},{48,32},{64,48},{80,64},{96,80},{112,96},{17,1},{33... | collective-permute-start | bytes 6128 | tf_op jit(solution)/shard_map/ppermute | solution.py:23
  56.8 11.2 %collective-permute-done.3 = s32[2,255]{1,0:T(2,128)S(1)} collective-permute-done((s32[2,255]{1,0:T(2,128)S(1)}, s32[2,255]{1,0:T(2,128)S(1)}, u32[]{:S(2)}, u32[]{:S(2)}) %collective-permute-start.3) | collective-permute-done | bytes 2072 | tf_op jit(solution)/shard_map/ppermute | solution.py:21
  71.8 6.8 %collective-permute-start.13 = (bf16[2,255,256]{1,2,0:T(8,128)(2,1)}, bf16[2,255,256]{1,2,0:T(8,128)(2,1)}, u32[]{:S(2)}, u32[]{:S(2)}) collective-permute-start(bf16[2,255,256]{1,2,0:T(8,128)(2,1)} %get-tuple-element.27), channel_id=1, source_target_pairs={{16,0},{32,16},{48,32},{64,48},{80,64},{96,80},{112,96},{17,1},{33... | collective-permute-start | bytes 783368 | tf_op jit(solution)/shard_map/ppermute | solution.py:23
  94.0 6.0 %collective-permute-done.16 = bf16[512,256]{1,0:T(8,128)(2,1)S(1)} collective-permute-done((bf16[512,256]{1,0:T(8,128)(2,1)S(1)}, bf16[512,256]{1,0:T(8,128)(2,1)S(1)}, u32[]{:S(2)}, u32[]{:S(2)}) %collective-permute-start.16) | collective-permute-done | bytes 262176 | tf_op jit(solution)/shard_map/ppermute | solution.py:138
  100.0 5.1 %collective-permute-done.15 = bf16[512,256]{1,0:T(8,128)(2,1)S(1)} collective-permute-done((bf16[512,256]{1,0:T(8,128)(2,1)S(1)}, bf16[512,256]{1,0:T(8,128)(2,1)S(1)}, u32[]{:S(2)}, u32[]{:S(2)}) %collective-permute-start.15) | collective-permute-done | bytes 262176 | tf_op jit(solution)/shard_map/ppermute | solution.py:138
  118.1 10.2 %collective-permute-done.17 = bf16[128,1024]{1,0:T(8,128)(2,1)} collective-permute-done((bf16[128,1024]{1,0:T(8,128)(2,1)}, bf16[128,1024]{1,0:T(8,128)(2,1)}, u32[]{:S(2)}, u32[]{:S(2)}) %collective-permute-start.17) | collective-permute-done | bytes 262176 | tf_op jit(solution)/shard_map/ppermute | solution.py:66
  130.4 7.9 %collective-permute-start.20 = (bf16[128,1024]{1,0:T(8,128)(2,1)}, bf16[128,1024]{1,0:T(8,128)(2,1)S(1)}, u32[]{:S(2)}, u32[]{:S(2)}) collective-permute-start(bf16[128,1024]{1,0:T(8,128)(2,1)} %fusion.30), channel_id=1, source_target_pairs={{1,0},{2,1},{3,2},{16,3},{17,16},{18,17},{19,18},{32,19},{33,32},{... | collective-permute-start | bytes 786440 | tf_op jit(solution)/shard_map/ppermute | solution.py:33
  139.6 4.4 %collective-permute-done.20 = bf16[128,1024]{1,0:T(8,128)(2,1)S(1)} collective-permute-done((bf16[128,1024]{1,0:T(8,128)(2,1)}, bf16[128,1024]{1,0:T(8,128)(2,1)S(1)}, u32[]{:S(2)}, u32[]{:S(2)}) %collective-permute-start.20) | collective-permute-done | bytes 262176 | tf_op jit(solution)/shard_map/ppermute | solution.py:33
  152.6 10.0 %collective-permute-done.25.refs_3_ = bf16[192,1024]{1,0:T(8,128)(2,1)S(1)} collective-permute-done((bf16[192,1024]{1,0:T(8,128)(2,1)S(1)}, bf16[192,1024]{1,0:T(8,128)(2,1)S(1)}, u32[]{:S(2)}, u32[]{:S(2)}) %collective-permute-start.25) | collective-permute-done | bytes 393248 | tf_op jit(solution)/shard_map/ppermute | solution.py:169
  165.0 5.7 %collective-permute-done.23.refs_1_ = bf16[192,1024]{1,0:T(8,128)(2,1)} collective-permute-done((bf16[192,1024]{1,0:T(8,128)(2,1)S(1)}, bf16[192,1024]{1,0:T(8,128)(2,1)}, u32[]{:S(2)}, u32[]{:S(2)}) %collective-permute-start.23) | collective-permute-done | bytes 393248 | tf_op jit(solution)/shard_map/ppermute | solution.py:169
  170.7 9.2 %shard_map.155 = bf16[4,768,768]{2,1,0:T(8,128)(2,1)} custom-call(s32[1]{0:T(128)} %bitcast.7.index_ref, bf16[192,1024]{1,0:T(8,128)(2,1)} %copy-done.5, bf16[192,1024]{1,0:T(8,128)(2,1)} %collective-permute-done.23.refs_1_, bf16[192,1024]{1,0:T(8,128)(2,1)} %copy-done.9, bf16[192,1024]{1,0:T(8,128)(2,1)} %copy-done.8, bf16[1024,1024]{1,0:T(8,128)(2,1)} %refs_4_.3, ...), custom_call_target="tpu_custom_call" | custom-call | tf_op jit(solution)/shard_map/pallas_call | solution.py:201
  182.0 4.5 %collective-permute-done.26 = bf16[2,768,768]{2,1,0:T(8,128)(2,1)S(1)} collective-permute-done((bf16[2,768,768]{2,1,0:T(8,128)(2,1)S(1)}, bf16[2,768,768]{2,1,0:T(8,128)(2,1)S(1)}, u32[]{:S(2)}, u32[]{:S(2)}) %collective-permute-start.26) | collective-permute-done | bytes 2359328 | tf_op jit(solution)/shard_map/ppermute | solution.py:138
  188.1 27.1 %collective-permute-done.27 = bf16[768,768]{1,0:T(8,128)(2,1)S(1)} collective-permute-done((bf16[768,768]{1,0:T(8,128)(2,1)S(1)}, bf16[768,768]{1,0:T(8,128)(2,1)S(1)}, u32[]{:S(2)}, u32[]{:S(2)}) %collective-permute-start.27) | collective-permute-done | bytes 1179680 | tf_op jit(solution)/shard_map/ppermute | solution.py:138
  223.2 55.4 %collective-permute-done.33 = bf16[768,512]{1,0:T(8,128)(2,1)S(1)} collective-permute-done((bf16[768,512]{1,0:T(8,128)(2,1)}, bf16[768,512]{1,0:T(8,128)(2,1)S(1)}, u32[]{:S(2)}, u32[]{:S(2)}) %collective-permute-start.33) | collective-permute-done | bytes 786464 | tf_op jit(solution)/shard_map/ppermute | solution.py:403
  282.0 13.4 %collective-permute-done.34 = bf16[768,512]{1,0:T(8,128)(2,1)S(1)} collective-permute-done((bf16[768,512]{1,0:T(8,128)(2,1)}, bf16[768,512]{1,0:T(8,128)(2,1)S(1)}, u32[]{:S(2)}, u32[]{:S(2)}) %collective-permute-start.34) | collective-permute-done | bytes 786464 | tf_op jit(solution)/shard_map/ppermute | solution.py:403
  297.2 22.8 %shard_map.156 = (f32[2,768,1]{2,1,0:T(8,128)}, f32[2,768,1]{2,1,0:T(8,128)}, f32[2,768,128]{2,1,0:T(8,128)}) custom-call(s32[1]{0:T(128)} %bitcast.30.place_ref, s32[4]{0:T(128)} %iota_multiply_fusion.shift_ref, bf16[768,768]{1,0:T(8,128)(2,1)} %copy-done.2, bf16[4,768,512]{2,1,0:T(8,128)(2,1)} %pad_maximum_fusion.1.k_ref.v_ref, ...), custom_call_target="tpu_custom_call" | custom-call | tf_op jit(solution)/shard_map/pallas_call | solution.py:319
  323.3 24.3 %shard_map.157 = bf16[768,256]{1,0:T(8,128)(2,1)} custom-call(s32[1]{0:T(128)} %bitcast.30.place_ref, s32[4]{0:T(128)} %constant.202.clone.shift_ref, bf16[768,768]{1,0:T(8,128)(2,1)} %copy-done.2, bf16[4,768,512]{2,1,0:T(8,128)(2,1)} %pad_maximum_fusion.k_ref.v_ref, bf16[4,768,512]{2,1,0:T(8,128)(2,1)} %pad_maximum_fusion.k_ref.v_ref, ...), custom_call_target="tpu_custom_call" | custom-call | tf_op jit(solution)/shard_map/pallas_call | solution.py:319
  349.4 9.5 %collective-permute-done.37 = bf16[768,256]{1,0:T(8,128)(2,1)S(1)} collective-permute-done((bf16[768,256]{1,0:T(8,128)(2,1)}, bf16[768,256]{1,0:T(8,128)(2,1)S(1)}, u32[]{:S(2)}, u32[]{:S(2)}) %collective-permute-start.37) | collective-permute-done | bytes 393248 | tf_op jit(solution)/shard_map/ppermute | solution.py:138
  358.9 8.8 %collective-permute-done.36 = bf16[768,256]{1,0:T(8,128)(2,1)} collective-permute-done((bf16[768,256]{1,0:T(8,128)(2,1)}, bf16[768,256]{1,0:T(8,128)(2,1)}, u32[]{:S(2)}, u32[]{:S(2)}) %collective-permute-start.36) | collective-permute-done | bytes 393248 | tf_op jit(solution)/shard_map/ppermute | solution.py:138
  382.2 10.3 %collective-permute-done.38 = bf16[192,1024]{1,0:T(8,128)(2,1)} collective-permute-done((bf16[192,1024]{1,0:T(8,128)(2,1)}, bf16[192,1024]{1,0:T(8,128)(2,1)}, u32[]{:S(2)}, u32[]{:S(2)}) %collective-permute-start.38) | collective-permute-done | bytes 393248 | tf_op jit(solution)/shard_map/ppermute | solution.py:66
  392.5 6.5 %collective-permute-done.40 = bf16[192,1024]{1,0:T(8,128)(2,1)} collective-permute-done((bf16[192,1024]{1,0:T(8,128)(2,1)}, bf16[192,1024]{1,0:T(8,128)(2,1)}, u32[]{:S(2)}, u32[]{:S(2)}) %collective-permute-start.40) | collective-permute-done | bytes 393248 | tf_op jit(solution)/shard_map/ppermute | solution.py:66
  (179 shorter events, 119.3 us)
Async XLA Ops:
  3.6 36.5 %collective-permute-start.1 = (s32[128,2]{0,1:T(2,128)S(1)}, s32[128,2]{0,1:T(2,128)S(1)}, u32[]{:S(2)}, u32[]{:S(2)}) collective-permute-start(s32[128,2]{0,1:T(2,128)S(1)} %get-tuple-element.32), channel_id=1, source_target_pairs={{0,2},{1,3},{2,0},{3,1},{4,6},{5,7},{6,4},{7,5},{8,10},{9,11},{10,... | collective-permute-start | bytes 3080 | tf_op jit(solution)/shard_map/ppermute | solution.py:50
  7.5 32.6 %collective-permute-start = (s32[128,2]{0,1:T(2,128)S(1)}, s32[128,2]{0,1:T(2,128)S(1)}, u32[]{:S(2)}, u32[]{:S(2)}) collective-permute-start(s32[128,2]{0,1:T(2,128)S(1)} %get-tuple-element.32), channel_id=1, source_target_pairs={{0,3},{1,0},{2,1},{3,2},{4,7},{5,4},{6,5},{7,6},{8,11},{9,8},{10,9... | collective-permute-start | bytes 3080 | tf_op jit(solution)/shard_map/ppermute | solution.py:50
  19.3 20.9 %collective-permute-start.2 = (s32[128,2]{0,1:T(2,128)S(1)}, s32[128,2]{0,1:T(2,128)S(1)}, u32[]{:S(2)}, u32[]{:S(2)}) collective-permute-start(s32[128,2]{0,1:T(2,128)S(1)} %get-tuple-element.32), channel_id=1, source_target_pairs={{0,1},{1,2},{2,3},{3,0},{4,5},{5,6},{6,7},{7,4},{8,9},{9,10},{10,1... | collective-permute-start | bytes 3080 | tf_op jit(solution)/shard_map/ppermute | solution.py:50
  48.2 20.0 %collective-permute-start.11 = (bf16[512,768]{0,1:T(8,128)(2,1)}, bf16[512,768]{0,1:T(8,128)(2,1)S(1)}, u32[]{:S(2)}, u32[]{:S(2)}) collective-permute-start(bf16[512,768]{0,1:T(8,128)(2,1)} %dynamic-slice_bitcast_fusion.2), channel_id=1, source_target_pairs={{0,8},{4,12},{8,0},{12,4},{1,9},{5,13},{9,1},{13,5},{2,10},{6,14},... | collective-permute-start | bytes 2359304 | tf_op jit(solution)/shard_map/ppermute | solution.py:138
  49.4 18.6 %collective-permute-start.3 = (s32[2,255]{1,0:T(2,128)S(1)}, s32[2,255]{1,0:T(2,128)S(1)}, u32[]{:S(2)}, u32[]{:S(2)}) collective-permute-start(s32[2,255]{1,0:T(2,128)S(1)} %get-tuple-element.30), channel_id=1, source_target_pairs={{0,16},{16,32},{32,48},{48,64},{64,80},{80,96},{96,112},{1,17},{17... | collective-permute-start | bytes 6128 | tf_op jit(solution)/shard_map/ppermute | solution.py:21
  50.7 17.3 %collective-permute-start.4 = (s32[2,255]{1,0:T(2,128)S(1)}, s32[2,255]{1,0:T(2,128)S(1)}, u32[]{:S(2)}, u32[]{:S(2)}) collective-permute-start(s32[2,255]{1,0:T(2,128)S(1)} %get-tuple-element.31), channel_id=1, source_target_pairs={{16,0},{32,16},{48,32},{64,48},{80,64},{96,80},{112,96},{17,1},{33... | collective-permute-start | bytes 6128 | tf_op jit(solution)/shard_map/ppermute | solution.py:23
  91.4 13.7 %collective-permute-start.15 = (bf16[512,256]{1,0:T(8,128)(2,1)S(1)}, bf16[512,256]{1,0:T(8,128)(2,1)S(1)}, u32[]{:S(2)}, u32[]{:S(2)}) collective-permute-start(bf16[512,256]{1,0:T(8,128)(2,1)S(1)} %copy.22), channel_id=1, source_target_pairs={{0,8},{4,12},{8,0},{12,4},{1,9},{5,13},{9,1},{13,5},{2,10},{6,14},... | collective-permute-start | bytes 786440 | tf_op jit(solution)/shard_map/ppermute | solution.py:138
  112.8 15.5 %collective-permute-start.17 = (bf16[128,1024]{1,0:T(8,128)(2,1)}, bf16[128,1024]{1,0:T(8,128)(2,1)}, u32[]{:S(2)}, u32[]{:S(2)}) collective-permute-start(bf16[128,1024]{1,0:T(8,128)(2,1)} %get-tuple-element.18), channel_id=1, source_target_pairs={{0,1},{1,2},{2,3},{3,0},{4,5},{5,6},{6,7},{7,4},{8,9},{9,10},{10,1... | collective-permute-start | bytes 786440 | tf_op jit(solution)/shard_map/ppermute | solution.py:66
  114.3 14.0 %collective-permute-start.19 = (bf16[128,1024]{1,0:T(8,128)(2,1)}, bf16[128,1024]{1,0:T(8,128)(2,1)}, u32[]{:S(2)}, u32[]{:S(2)}) collective-permute-start(bf16[128,1024]{1,0:T(8,128)(2,1)} %get-tuple-element.19), channel_id=1, source_target_pairs={{0,3},{1,0},{2,1},{3,2},{4,7},{5,4},{6,5},{7,6},{8,11},{9,8},{10,9... | collective-permute-start | bytes 786440 | tf_op jit(solution)/shard_map/ppermute | solution.py:66
  130.4 13.7 %collective-permute-start.20 = (bf16[128,1024]{1,0:T(8,128)(2,1)}, bf16[128,1024]{1,0:T(8,128)(2,1)S(1)}, u32[]{:S(2)}, u32[]{:S(2)}) collective-permute-start(bf16[128,1024]{1,0:T(8,128)(2,1)} %fusion.30), channel_id=1, source_target_pairs={{1,0},{2,1},{3,2},{16,3},{17,16},{18,17},{19,18},{32,19},{33,32},{... | collective-permute-start | bytes 786440 | tf_op jit(solution)/shard_map/ppermute | solution.py:33
  150.6 13.7 %collective-permute-start.24 = (bf16[192,1024]{1,0:T(8,128)(2,1)S(1)}, bf16[192,1024]{1,0:T(8,128)(2,1)S(1)}, u32[]{:S(2)}, u32[]{:S(2)}) collective-permute-start(bf16[192,1024]{1,0:T(8,128)(2,1)S(1)} %multiply_convert_fusion.refs_0_), channel_id=1, source_target_pairs={{0,2},{1,3},{2,0},{3,1},{4,6},{5,7},{6,4},{7,5},{8,10},{9,11},{10,... | collective-permute-start | bytes 1179656 | tf_op jit(solution)/shard_map/ppermute | solution.py:169
  150.7 20.1 %collective-permute-start.23 = (bf16[192,1024]{1,0:T(8,128)(2,1)S(1)}, bf16[192,1024]{1,0:T(8,128)(2,1)}, u32[]{:S(2)}, u32[]{:S(2)}) collective-permute-start(bf16[192,1024]{1,0:T(8,128)(2,1)S(1)} %multiply_convert_fusion.refs_0_), channel_id=1, source_target_pairs={{0,1},{1,2},{2,3},{3,0},{4,5},{5,6},{6,7},{7,4},{8,9},{9,10},{10,1... | collective-permute-start | bytes 1179656 | tf_op jit(solution)/shard_map/ppermute | solution.py:169
  187.2 28.1 %collective-permute-start.27 = (bf16[768,768]{1,0:T(8,128)(2,1)S(1)}, bf16[768,768]{1,0:T(8,128)(2,1)S(1)}, u32[]{:S(2)}, u32[]{:S(2)}) collective-permute-start(bf16[768,768]{1,0:T(8,128)(2,1)S(1)} %dynamic-slice_bitcast_fusion.1), channel_id=1, source_target_pairs={{0,8},{4,12},{8,0},{12,4},{1,9},{5,13},{9,1},{13,5},{2,10},{6,14},... | collective-permute-start | bytes 3538952 | tf_op jit(solution)/shard_map/ppermute | solution.py:138
  216.7 61.9 %collective-permute-start.33 = (bf16[768,512]{1,0:T(8,128)(2,1)}, bf16[768,512]{1,0:T(8,128)(2,1)S(1)}, u32[]{:S(2)}, u32[]{:S(2)}) collective-permute-start(bf16[768,512]{1,0:T(8,128)(2,1)} %get-tuple-element.17), channel_id=1, source_target_pairs={{0,64},{16,80},{32,96},{48,112},{1,65},{17,81},{33,97},{49,113},{2... | collective-permute-start | bytes 2359304 | tf_op jit(solution)/shard_map/ppermute | solution.py:403
  218.0 61.9 %collective-permute-start.32 = (bf16[768,512]{1,0:T(8,128)(2,1)}, bf16[768,512]{1,0:T(8,128)(2,1)S(1)}, u32[]{:S(2)}, u32[]{:S(2)}) collective-permute-start(bf16[768,512]{1,0:T(8,128)(2,1)} %get-tuple-element.17), channel_id=1, source_target_pairs={{0,32},{16,48},{32,64},{48,80},{64,96},{80,112},{1,33},{17,49},{33... | collective-permute-start | bytes 2359304 | tf_op jit(solution)/shard_map/ppermute | solution.py:403
  219.3 76.1 %collective-permute-start.34 = (bf16[768,512]{1,0:T(8,128)(2,1)}, bf16[768,512]{1,0:T(8,128)(2,1)S(1)}, u32[]{:S(2)}, u32[]{:S(2)}) collective-permute-start(bf16[768,512]{1,0:T(8,128)(2,1)} %get-tuple-element.17), channel_id=1, source_target_pairs={{0,96},{16,112},{1,97},{17,113},{2,98},{18,114},{3,99},{19,115},{4... | collective-permute-start | bytes 2359304 | tf_op jit(solution)/shard_map/ppermute | solution.py:403
  220.6 99.4 %collective-permute-start.31 = (bf16[768,512]{1,0:T(8,128)(2,1)}, bf16[768,512]{1,0:T(8,128)(2,1)}, u32[]{:S(2)}, u32[]{:S(2)}) collective-permute-start(bf16[768,512]{1,0:T(8,128)(2,1)} %get-tuple-element.17), channel_id=1, source_target_pairs={{0,112},{1,113},{2,114},{3,115},{4,116},{5,117},{6,118},{7,119},{8... | collective-permute-start | bytes 2359304 | tf_op jit(solution)/shard_map/ppermute | solution.py:403
  221.9 98.1 %collective-permute-start.30 = (bf16[768,512]{1,0:T(8,128)(2,1)}, bf16[768,512]{1,0:T(8,128)(2,1)}, u32[]{:S(2)}, u32[]{:S(2)}) collective-permute-start(bf16[768,512]{1,0:T(8,128)(2,1)} %get-tuple-element.17), channel_id=1, source_target_pairs={{0,80},{16,96},{32,112},{1,81},{17,97},{33,113},{2,82},{18,98},{34... | collective-permute-start | bytes 2359304 | tf_op jit(solution)/shard_map/ppermute | solution.py:403
  278.6 41.4 %collective-permute-start.29 = (bf16[768,512]{1,0:T(8,128)(2,1)}, bf16[768,512]{1,0:T(8,128)(2,1)}, u32[]{:S(2)}, u32[]{:S(2)}) collective-permute-start(bf16[768,512]{1,0:T(8,128)(2,1)} %get-tuple-element.17), channel_id=1, source_target_pairs={{0,48},{16,64},{32,80},{48,96},{64,112},{1,49},{17,65},{33,81},{49... | collective-permute-start | bytes 2359304 | tf_op jit(solution)/shard_map/ppermute | solution.py:403
  279.9 40.1 %collective-permute-start.28 = (bf16[768,512]{1,0:T(8,128)(2,1)}, bf16[768,512]{1,0:T(8,128)(2,1)}, u32[]{:S(2)}, u32[]{:S(2)}) collective-permute-start(bf16[768,512]{1,0:T(8,128)(2,1)} %get-tuple-element.17), channel_id=1, source_target_pairs={{0,16},{16,32},{32,48},{48,64},{64,80},{80,96},{96,112},{1,17},{17... | collective-permute-start | bytes 2359304 | tf_op jit(solution)/shard_map/ppermute | solution.py:403
  348.4 19.3 %collective-permute-start.36 = (bf16[768,256]{1,0:T(8,128)(2,1)}, bf16[768,256]{1,0:T(8,128)(2,1)}, u32[]{:S(2)}, u32[]{:S(2)}) collective-permute-start(bf16[768,256]{1,0:T(8,128)(2,1)} %shard_map.157), channel_id=1, source_target_pairs={{0,8},{4,12},{8,0},{12,4},{1,9},{5,13},{9,1},{13,5},{2,10},{6,14},... | collective-permute-start | bytes 1179656 | tf_op jit(solution)/shard_map/ppermute | solution.py:138
  349.3 18.4 %collective-permute-start.35 = (bf16[768,256]{1,0:T(8,128)(2,1)}, bf16[768,256]{1,0:T(8,128)(2,1)}, u32[]{:S(2)}, u32[]{:S(2)}) collective-permute-start(bf16[768,256]{1,0:T(8,128)(2,1)} %shard_map.157), channel_id=1, source_target_pairs={{0,4},{4,0},{8,12},{12,8},{1,5},{5,1},{9,13},{13,9},{2,6},{6,2},{1... | collective-permute-start | bytes 1179656 | tf_op jit(solution)/shard_map/ppermute | solution.py:138
  378.9 20.0 %collective-permute-start.40 = (bf16[192,1024]{1,0:T(8,128)(2,1)}, bf16[192,1024]{1,0:T(8,128)(2,1)}, u32[]{:S(2)}, u32[]{:S(2)}) collective-permute-start(bf16[192,1024]{1,0:T(8,128)(2,1)} %get-tuple-element.14), channel_id=1, source_target_pairs={{0,3},{1,0},{2,1},{3,2},{4,7},{5,4},{6,5},{7,6},{8,11},{9,8},{10,9... | collective-permute-start | bytes 1179656 | tf_op jit(solution)/shard_map/ppermute | solution.py:66
  382.2 17.5 %collective-permute-start.39 = (bf16[192,1024]{1,0:T(8,128)(2,1)S(1)}, bf16[192,1024]{1,0:T(8,128)(2,1)}, u32[]{:S(2)}, u32[]{:S(2)}) collective-permute-start(bf16[192,1024]{1,0:T(8,128)(2,1)S(1)} %get-tuple-element.15), channel_id=1, source_target_pairs={{0,2},{1,3},{2,0},{3,1},{4,6},{5,7},{6,4},{7,5},{8,10},{9,11},{10,... | collective-permute-start | bytes 1179656 | tf_op jit(solution)/shard_map/ppermute | solution.py:66
  (35 other events, 714.8 us)
